TPU v7x, 512 devices: a whole 4x4x16 slice. The times are simulated.
512 devices in a mesh: act: 4 (over z_hi, core), axial: 16 (over x, y), hoop: 8 (over z_lo).
Axes of the slice: x: 4, y: 4, z: 16 (z_hi: 2, z_lo: 8; z = z_hi * 8 + z_lo), core: 2. Of those that a mesh axis runs over, the one named last changes fastest.
Arguments:
- wave_state: float32 [4, 5, 256, 4096], P('act', None, 'axial', 'hoop'), may hold values from -6 to 6
- layup_zone: int32 [256, 4096], P('axial', 'hoop'), may hold values from 0 to 7
- moduli: float32 [8, 6], replicated, may hold values from 0.1 to 0.35
- sensors: int32 [512], P(('axial', 'hoop')), may hold values from 0 to 8191
- history: float32 [4, 512, 253], P('act', ('axial', 'hoop')), may hold values from -6 to 6
- receivers: int32 [4, 128], P('act'), may hold values from 0 to 511, as said below
- delays: int32 [4, 128, 256, 1024], P('act', None, 'axial', 'hoop'), may hold values from 0 to 255
Outputs:
- next_state: float32 [4, 5, 256, 4096], P('act', None, 'axial', 'hoop')
- traces: float32 [4, 512, 3], P('act', ('axial', 'hoop'))
- damage_map: float32 [256, 1024], P('axial', 'hoop')
Inputs may be any that keep to these rules, and one draw needn't show every extreme that they name: `receivers`: each row names 128 different sensors.
All inputs are finite; a program needn't handle non-finite values.
Results may differ from a plain program's by a relative error of at most 0.000029.
Values sent between devices are 32-bit elements; how exact they have to be, the bound alone decides.
No kernel may reach another device: no remote copies, remote signals or barrier semaphores. Data moves between devices by JAX's collectives and lax.ppermute only.
A program may use at most 64 MiB of HBM per device.

v0:
```python
import math

import jax
import jax.numpy as jnp
from jax import lax
from jax.sharding import PartitionSpec as P

STEPS = 3


def padded(cells, sides, width, closed):
    for axis, dim in sides:
        count = lax.axis_size(axis)
        ends = count if closed else count - 1
        head = lax.slice_in_dim(cells, 0, width, axis=dim)
        tail = lax.slice_in_dim(cells, cells.shape[dim] - width, cells.shape[dim], axis=dim)
        cells = jnp.concatenate(
            [
                lax.ppermute(tail, axis, [(i, (i + 1) % count) for i in range(ends)]),
                cells,
                lax.ppermute(head, axis, [((i + 1) % count, i) for i in range(ends)]),
            ],
            axis=dim,
        )
    return cells


def extend(axial_pair, hoop_pair):
    along_axial = padded(axial_pair, (("axial", 1),), 1, False)
    along_hoop = padded(hoop_pair, (("hoop", 2),), 1, True)
    return (along_axial, along_hoop)


def advance(fields, moduli_map):
    speed_axial, speed_hoop, normal_axial, normal_hoop, shear_stress = fields
    mobility_axial = moduli_map[0]
    mobility_hoop = moduli_map[1]
    stiff_axial = moduli_map[2]
    stiff_cross = moduli_map[3]
    stiff_hoop = moduli_map[4]
    stiff_shear = moduli_map[5]
    stress_axial, stress_hoop = extend(
        jnp.stack([normal_axial, shear_stress]), jnp.stack([normal_hoop, shear_stress])
    )
    normal_upper = stress_axial[0, 2:, :]
    shear_lower_axial = stress_axial[1, :-2, :]
    hoop_upper = stress_hoop[0, :, 2:]
    shear_lower_hoop = stress_hoop[1, :, :-2]
    speed_axial = speed_axial + mobility_axial * (
        normal_upper - normal_axial + (shear_stress - shear_lower_hoop)
    )
    speed_hoop = speed_hoop + mobility_hoop * (
        hoop_upper - normal_hoop + (shear_stress - shear_lower_axial)
    )
    pair_now = jnp.stack([speed_axial, speed_hoop])
    speed_along_axial, speed_along_hoop = extend(pair_now, pair_now)
    axial_lower = speed_along_axial[0, :-2, :]
    hoop_next_axial = speed_along_axial[1, 2:, :]
    axial_next_hoop = speed_along_hoop[0, :, 2:]
    hoop_lower = speed_along_hoop[1, :, :-2]
    strain_axial = speed_axial - axial_lower
    strain_hoop = speed_hoop - hoop_lower
    normal_axial = normal_axial + stiff_axial * strain_axial + stiff_cross * strain_hoop
    normal_hoop = normal_hoop + stiff_cross * strain_axial + stiff_hoop * strain_hoop
    strain_shear = axial_next_hoop - speed_axial + (hoop_next_axial - speed_hoop)
    shear_stress = shear_stress + stiff_shear * strain_shear
    return (speed_axial, speed_hoop, normal_axial, normal_hoop, shear_stress)


def pick_block(running, block_item):
    block_rows, block_delays = block_item
    sample_ids = jnp.arange(block_rows.shape[1], dtype=jnp.int32)
    matches = block_delays[:, None, :] == sample_ids[None, :, None]
    picked = jnp.where(matches, block_rows[:, :, None], jnp.float32(0.0))
    return (running + jnp.sum(picked, axis=(0, 1)), None)


def per_device(wave_state, layup_zone, moduli, sensors, history, receivers, delays):
    moduli_map = jnp.zeros((moduli.shape[1],) + layup_zone.shape, jnp.float32)
    for zone_level in range(moduli.shape[0]):
        moduli_map = jnp.where(
            layup_zone[None] == zone_level, moduli[zone_level][:, None, None], moduli_map
        )
    samples = []
    fields = tuple((wave_state[0, component] for component in range(5)))
    for step_index in range(STEPS):
        fields = advance(fields, moduli_map)
        samples.append((fields[2] + fields[3]).reshape(-1)[sensors])
    next_state = jnp.stack(fields)[None]
    recorded = jnp.stack(samples, axis=1)[None]
    local_waves = jnp.concatenate([history, recorded], axis=2)
    waveforms = lax.all_gather(local_waves, ("axial", "hoop"), axis=1, tiled=True)
    pair_count = receivers.shape[1]
    pixel_rows = delays.shape[2]
    pixel_cols = delays.shape[3]
    sample_count = waveforms.shape[2]
    group_size = math.gcd(pair_count, 8)
    block_count = pair_count // group_size
    chosen_rows = waveforms[0][receivers[0]].reshape(block_count, group_size, sample_count)
    flat_delays = delays[0].reshape(block_count, group_size, pixel_rows * pixel_cols)
    start_sum = jnp.zeros((pixel_rows * pixel_cols,), jnp.float32)
    partial_value = lax.scan(pick_block, start_sum, (chosen_rows, flat_delays))[0].reshape(
        pixel_rows, pixel_cols
    )
    group_count = lax.axis_size("act")
    summed = lax.psum(partial_value, "act")
    damage_map = summed * summed / (pair_count * group_count)
    return (next_state, recorded, damage_map)


def solution(mesh):
    return jax.shard_map(
        per_device,
        mesh=mesh,
        in_specs=(
            P("act", None, "axial", "hoop"),
            P("axial", "hoop"),
            P(),
            P(("axial", "hoop")),
            P("act", ("axial", "hoop"), None),
            P("act", None),
            P("act", None, "axial", "hoop"),
        ),
        out_specs=(
            P("act", None, "axial", "hoop"),
            P("act", ("axial", "hoop"), None),
            P("axial", "hoop"),
        ),
        check_vma=False,
    )
```

profile of v0, /device:TPU:1, one launch (start us, length us, event | category | flops | bytes accessed | tf_op | source)
XLA Modules:
  0.0 730.9 jit_solution(5585976204349389870)
XLA Ops:
  0.7 0.9 slice_bitcast_fusion
  1.7 4.4 collective-permute-start.1
  6.0 11.3 %collective-permute-start.2 = (f32[2,16,1]{2,1,0:T(8,128)S(1)}, f32[2,16,1]{2,1,0:T(8,128)S(1)}, u32[]{:S(2)}, u32[]{:S(2)}) collective-permute-start(f32[2,16,1]{2,1,0:T(8,128)S(1)} %get-tuple-element.140), channel_id=1, source_target_pairs={{1,0},{2,1},{3,2},{4,3},{5,4},{6,5},{7,6},{0,7},{9,8},{10,9},{11,1... | collective-permute-start | bytes 392 | tf_op jit(solution)/shard_map/ppermute | solution.py:21
  17.3 1.3 collective-permute-start
  18.6 4.0 collective-permute-start.3
  22.6 0.8 broadcast_compare_fusion.7
  23.4 1.0 slice_bitcast_fusion.21
  24.4 0.7 compare_select_fusion.1
  25.1 0.7 fusion.41
  25.7 0.1 select_select_fusion
  26.0 0.2 reshape_squeeze.3
  26.3 0.7 copy-done.1
  27.0 0.1 bitcast_add_fusion
  27.1 3.2 collective-permute-start.4
  30.3 1.3 collective-permute-start.7
  31.6 1.9 collective-permute-start.5
  33.6 10.0 %collective-permute-start.6 = (f32[2,16,1]{2,1,0:T(8,128)S(1)}, f32[2,16,1]{2,1,0:T(8,128)S(1)}, u32[]{:S(2)}, u32[]{:S(2)}) collective-permute-start(f32[2,16,1]{2,1,0:T(8,128)S(1)} %get-tuple-element.137), channel_id=1, source_target_pairs={{1,0},{2,1},{3,2},{4,3},{5,4},{6,5},{7,6},{0,7},{9,8},{10,9},{11,1... | collective-permute-start | bytes 392 | tf_op jit(solution)/shard_map/ppermute | solution.py:21
  43.7 0.7 collective-permute-done.6
  44.6 10.3 %collective-permute-start.10 = (f32[2,16,1]{2,1,0:T(8,128)S(1)}, f32[2,16,1]{2,1,0:T(8,128)S(1)}, u32[]{:S(2)}, u32[]{:S(2)}) collective-permute-start(f32[2,16,1]{2,1,0:T(8,128)S(1)} %get-tuple-element.132), channel_id=1, source_target_pairs={{1,0},{2,1},{3,2},{4,3},{5,4},{6,5},{7,6},{0,7},{9,8},{10,9},{11,1... | collective-permute-start | bytes 392 | tf_op jit(solution)/shard_map/ppermute | solution.py:21
  54.8 1.9 collective-permute-start.9
  56.9 3.9 collective-permute-start.11
  60.8 1.3 collective-permute-start.8
  62.3 3.7 collective-permute-done.9
  65.9 0.8 collective-permute-done.8
  66.9 10.0 %collective-permute-start.14 = (f32[2,16,1]{2,1,0:T(8,128)S(1)}, f32[2,16,1]{2,1,0:T(8,128)S(1)}, u32[]{:S(2)}, u32[]{:S(2)}) collective-permute-start(f32[2,16,1]{2,1,0:T(8,128)S(1)} %get-tuple-element.129), channel_id=1, source_target_pairs={{1,0},{2,1},{3,2},{4,3},{5,4},{6,5},{7,6},{0,7},{9,8},{10,9},{11,1... | collective-permute-start | bytes 392 | tf_op jit(solution)/shard_map/ppermute | solution.py:21
  76.9 1.3 collective-permute-start.15
  78.2 4.0 collective-permute-start.12
  82.3 1.9 collective-permute-start.13
  84.3 9.1 %collective-permute-done.13 = f32[2,16,1]{2,1,0:T(8,128)S(1)} collective-permute-done((f32[2,16,1]{2,1,0:T(8,128)S(1)}, f32[2,16,1]{2,1,0:T(8,128)S(1)}, u32[]{:S(2)}, u32[]{:S(2)}) %collective-permute-start.13) | collective-permute-done | bytes 160 | tf_op jit(solution)/shard_map/ppermute | solution.py:19
  93.5 1.3 collective-permute-start.16
  95.1 1.9 collective-permute-start.17
  97.1 10.0 %collective-permute-start.18 = (f32[2,16,1]{2,1,0:T(8,128)S(1)}, f32[2,16,1]{2,1,0:T(8,128)S(1)}, u32[]{:S(2)}, u32[]{:S(2)}) collective-permute-start(f32[2,16,1]{2,1,0:T(8,128)S(1)} %get-tuple-element.124), channel_id=1, source_target_pairs={{1,0},{2,1},{3,2},{4,3},{5,4},{6,5},{7,6},{0,7},{9,8},{10,9},{11,1... | collective-permute-start | bytes 392 | tf_op jit(solution)/shard_map/ppermute | solution.py:21
  107.0 5.1 collective-permute-start.19
  112.3 0.6 collective-permute-done.19
  113.2 5.2 collective-permute-start.20
  118.4 1.9 collective-permute-start.21
  120.3 1.3 collective-permute-start.23
  121.6 10.0 %collective-permute-start.22 = (f32[2,16,1]{2,1,0:T(8,128)S(1)}, f32[2,16,1]{2,1,0:T(8,128)S(1)}, u32[]{:S(2)}, u32[]{:S(2)}) collective-permute-start(f32[2,16,1]{2,1,0:T(8,128)S(1)} %get-tuple-element.120), channel_id=1, source_target_pairs={{1,0},{2,1},{3,2},{4,3},{5,4},{6,5},{7,6},{0,7},{9,8},{10,9},{11,1... | collective-permute-start | bytes 392 | tf_op jit(solution)/shard_map/ppermute | solution.py:21
  131.7 0.6 gather_fusion.1
  132.3 0.6 gather_fusion
  133.4 0.6 gather_fusion.2
  134.0 0.1 copy.18
  134.2 472.8 %all_gather.3 = f32[1,512,256]{2,0,1:T(1,128)S(1)} all-gather(f32[1,4,256]{2,0,1:T(1,128)S(1)} %pad_maximum_fusion.66), channel_id=1, replica_groups=mesh['act'=4,'axial'=16,'hoop'=8] {'axial','hoop'}, dimensions={1}, use_global_device_ids=true | all-gather | bytes 528384 | tf_op jit(solution)/shard_map/all_gather | solution.py:92
  607.0 0.8 gather_fusion.3
  607.8 40.4 %while.11 = (s32[]{:T(128)}, f32[2048]{0:T(1024)S(1)}, s32[16,8,2048]{2,1,0:T(8,128)S(1)}, f32[16,8,256]{2,1,0:T(8,128)S(1)}, s32[]{:T(128)}, /*index=5*/s32[]{:T(128)}) while((s32[]{:T(128)}, f32[2048]{0:T(1024)S(1)}, s32[16,8,2048]{2,1,0:T(8,128)S(1)}, f32[16,8,256]{2,1,0:T(8,128)S(1)}, s32[]{:T(128)}, ...), condition=%wide.region_2.3_spmd.clone, body=%wide.region_0.2_spmd.clone.sunk | while | flops 12584963 | bytes 254039 | solution.py:102
  607.8 2.4 select_reduce_fusion.2
  610.4 2.4 select_reduce_fusion.2
  612.9 2.4 select_reduce_fusion.2
  615.4 2.4 select_reduce_fusion.2
  618.0 2.4 select_reduce_fusion.2
  620.5 2.4 select_reduce_fusion.2
  623.0 2.4 select_reduce_fusion.2
  625.5 2.4 select_reduce_fusion.2
  628.1 2.4 select_reduce_fusion.2
  630.6 2.4 select_reduce_fusion.2
  633.1 2.4 select_reduce_fusion.2
  635.6 2.4 select_reduce_fusion.2
  638.2 2.4 select_reduce_fusion.2
  640.7 2.4 select_reduce_fusion.2
  643.2 2.4 select_reduce_fusion.2
  645.7 2.4 select_reduce_fusion.2
  648.2 81.4 %psum.7 = f32[16,128]{1,0:T(8,128)S(1)} all-reduce(f32[16,128]{1,0:T(8,128)S(1)} %bitcast.173), channel_id=1, replica_groups=mesh['act'=4,'axial'=16,'hoop'=8] {'act'}, use_global_device_ids=true, to_apply=%region_3.4 | all-reduce | flops 2048 | bytes 16384 | tf_op jit(solution)/shard_map/psum | solution.py:106
  729.7 0.6 multiply_multiply_fusion
  730.3 0.6 copy.21
  (143 shorter events, 2.8 us)
Async XLA Ops:
  0.6 25.4 %copy-start.3 = (f32[1,4,253]{2,1,0:T(4,128)S(1)}, f32[1,4,253]{2,1,0:T(4,128)}, u32[]{:S(2)}) copy-start(f32[1,4,253]{2,1,0:T(4,128)} %param.13) | copy-start | bytes 12148
  0.6 25.4 %copy-start = (s32[1,128,16,128]{3,2,1,0:T(8,128)S(1)}, s32[1,128,16,128]{3,2,1,0:T(8,128)}, u32[]{:S(2)}) copy-start(s32[1,128,16,128]{3,2,1,0:T(8,128)} %param.15) | copy-start | bytes 3145732
  1.7 24.5 %collective-permute-start.1 = (f32[2,16,1]{2,1,0:T(8,128)S(1)}, f32[2,16,1]{2,1,0:T(8,128)S(1)}, u32[]{:S(2)}, u32[]{:S(2)}) collective-permute-start(f32[2,16,1]{2,1,0:T(8,128)S(1)} %get-tuple-element.141), channel_id=1, source_target_pairs={{0,1},{1,2},{2,3},{3,4},{4,5},{5,6},{6,7},{7,0},{8,9},{9,10},{10,1... | collective-permute-start | bytes 392 | tf_op jit(solution)/shard_map/ppermute | solution.py:19
  6.0 20.2 %collective-permute-start.2 = (f32[2,16,1]{2,1,0:T(8,128)S(1)}, f32[2,16,1]{2,1,0:T(8,128)S(1)}, u32[]{:S(2)}, u32[]{:S(2)}) collective-permute-start(f32[2,16,1]{2,1,0:T(8,128)S(1)} %get-tuple-element.140), channel_id=1, source_target_pairs={{1,0},{2,1},{3,2},{4,3},{5,4},{6,5},{7,6},{0,7},{9,8},{10,9},{11,1... | collective-permute-start | bytes 392 | tf_op jit(solution)/shard_map/ppermute | solution.py:21
  17.3 8.9 %collective-permute-start = (f32[2,1,512]{2,1,0:T(1,128)S(1)}, f32[2,1,512]{2,1,0:T(1,128)S(1)}, u32[]{:S(2)}, u32[]{:S(2)}) collective-permute-start(f32[2,1,512]{2,1,0:T(1,128)S(1)} %get-tuple-element.143), channel_id=1, source_target_pairs={{8,0},{16,8},{24,16},{32,24},{40,32},{48,40},{56,48},{64,56},{72,6... | collective-permute-start | bytes 12296 | tf_op jit(solution)/shard_map/ppermute | solution.py:21
  18.6 7.6 %collective-permute-start.3 = (f32[2,1,512]{2,1,0:T(1,128)S(1)}, f32[2,1,512]{2,1,0:T(1,128)S(1)}, u32[]{:S(2)}, u32[]{:S(2)}) collective-permute-start(f32[2,1,512]{2,1,0:T(1,128)S(1)} %get-tuple-element.142), channel_id=1, source_target_pairs={{0,8},{8,16},{16,24},{24,32},{32,40},{40,48},{48,56},{56,64},{64,7... | collective-permute-start | bytes 12296 | tf_op jit(solution)/shard_map/ppermute | solution.py:19
  26.0 0.9 copy-start.1
  27.1 17.3 %collective-permute-start.4 = (f32[2,1,512]{2,1,0:T(1,128)S(1)}, f32[2,1,512]{2,1,0:T(1,128)S(1)}, u32[]{:S(2)}, u32[]{:S(2)}) collective-permute-start(f32[2,1,512]{2,1,0:T(1,128)S(1)} %get-tuple-element.138), channel_id=1, source_target_pairs={{0,8},{8,16},{16,24},{24,32},{32,40},{40,48},{48,56},{56,64},{64,7... | collective-permute-start | bytes 12296 | tf_op jit(solution)/shard_map/ppermute | solution.py:19
  30.3 14.1 %collective-permute-start.7 = (f32[2,1,512]{2,1,0:T(1,128)S(1)}, f32[2,1,512]{2,1,0:T(1,128)S(1)}, u32[]{:S(2)}, u32[]{:S(2)}) collective-permute-start(f32[2,1,512]{2,1,0:T(1,128)S(1)} %get-tuple-element.139), channel_id=1, source_target_pairs={{8,0},{16,8},{24,16},{32,24},{40,32},{48,40},{56,48},{64,56},{72,6... | collective-permute-start | bytes 12296 | tf_op jit(solution)/shard_map/ppermute | solution.py:21
  31.6 12.1 %collective-permute-start.5 = (f32[2,16,1]{2,1,0:T(8,128)S(1)}, f32[2,16,1]{2,1,0:T(8,128)S(1)}, u32[]{:S(2)}, u32[]{:S(2)}) collective-permute-start(f32[2,16,1]{2,1,0:T(8,128)S(1)} %get-tuple-element.136), channel_id=1, source_target_pairs={{0,1},{1,2},{2,3},{3,4},{4,5},{5,6},{6,7},{7,0},{8,9},{9,10},{10,1... | collective-permute-start | bytes 392 | tf_op jit(solution)/shard_map/ppermute | solution.py:19
  33.6 10.8 %collective-permute-start.6 = (f32[2,16,1]{2,1,0:T(8,128)S(1)}, f32[2,16,1]{2,1,0:T(8,128)S(1)}, u32[]{:S(2)}, u32[]{:S(2)}) collective-permute-start(f32[2,16,1]{2,1,0:T(8,128)S(1)} %get-tuple-element.137), channel_id=1, source_target_pairs={{1,0},{2,1},{3,2},{4,3},{5,4},{6,5},{7,6},{0,7},{9,8},{10,9},{11,1... | collective-permute-start | bytes 392 | tf_op jit(solution)/shard_map/ppermute | solution.py:21
  44.6 17.7 %collective-permute-start.10 = (f32[2,16,1]{2,1,0:T(8,128)S(1)}, f32[2,16,1]{2,1,0:T(8,128)S(1)}, u32[]{:S(2)}, u32[]{:S(2)}) collective-permute-start(f32[2,16,1]{2,1,0:T(8,128)S(1)} %get-tuple-element.132), channel_id=1, source_target_pairs={{1,0},{2,1},{3,2},{4,3},{5,4},{6,5},{7,6},{0,7},{9,8},{10,9},{11,1... | collective-permute-start | bytes 392 | tf_op jit(solution)/shard_map/ppermute | solution.py:21
  54.8 11.1 %collective-permute-start.9 = (f32[2,16,1]{2,1,0:T(8,128)S(1)}, f32[2,16,1]{2,1,0:T(8,128)S(1)}, u32[]{:S(2)}, u32[]{:S(2)}) collective-permute-start(f32[2,16,1]{2,1,0:T(8,128)S(1)} %get-tuple-element.133), channel_id=1, source_target_pairs={{0,1},{1,2},{2,3},{3,4},{4,5},{5,6},{6,7},{7,0},{8,9},{9,10},{10,1... | collective-permute-start | bytes 392 | tf_op jit(solution)/shard_map/ppermute | solution.py:19
  56.9 9.1 %collective-permute-start.11 = (f32[2,1,512]{2,1,0:T(1,128)S(1)}, f32[2,1,512]{2,1,0:T(1,128)S(1)}, u32[]{:S(2)}, u32[]{:S(2)}) collective-permute-start(f32[2,1,512]{2,1,0:T(1,128)S(1)} %get-tuple-element.134), channel_id=1, source_target_pairs={{0,8},{8,16},{16,24},{24,32},{32,40},{40,48},{48,56},{56,64},{64,7... | collective-permute-start | bytes 12296 | tf_op jit(solution)/shard_map/ppermute | solution.py:19
  60.8 5.9 collective-permute-start.8
  66.9 17.4 %collective-permute-start.14 = (f32[2,16,1]{2,1,0:T(8,128)S(1)}, f32[2,16,1]{2,1,0:T(8,128)S(1)}, u32[]{:S(2)}, u32[]{:S(2)}) collective-permute-start(f32[2,16,1]{2,1,0:T(8,128)S(1)} %get-tuple-element.129), channel_id=1, source_target_pairs={{1,0},{2,1},{3,2},{4,3},{5,4},{6,5},{7,6},{0,7},{9,8},{10,9},{11,1... | collective-permute-start | bytes 392 | tf_op jit(solution)/shard_map/ppermute | solution.py:21
  76.9 16.5 %collective-permute-start.15 = (f32[2,1,512]{2,1,0:T(1,128)S(1)}, f32[2,1,512]{2,1,0:T(1,128)S(1)}, u32[]{:S(2)}, u32[]{:S(2)}) collective-permute-start(f32[2,1,512]{2,1,0:T(1,128)S(1)} %get-tuple-element.131), channel_id=1, source_target_pairs={{8,0},{16,8},{24,16},{32,24},{40,32},{48,40},{56,48},{64,56},{72,6... | collective-permute-start | bytes 12296 | tf_op jit(solution)/shard_map/ppermute | solution.py:21
  78.2 15.2 %collective-permute-start.12 = (f32[2,1,512]{2,1,0:T(1,128)S(1)}, f32[2,1,512]{2,1,0:T(1,128)S(1)}, u32[]{:S(2)}, u32[]{:S(2)}) collective-permute-start(f32[2,1,512]{2,1,0:T(1,128)S(1)} %get-tuple-element.130), channel_id=1, source_target_pairs={{0,8},{8,16},{16,24},{24,32},{32,40},{40,48},{48,56},{56,64},{64,7... | collective-permute-start | bytes 12296 | tf_op jit(solution)/shard_map/ppermute | solution.py:19
  82.3 11.1 %collective-permute-start.13 = (f32[2,16,1]{2,1,0:T(8,128)S(1)}, f32[2,16,1]{2,1,0:T(8,128)S(1)}, u32[]{:S(2)}, u32[]{:S(2)}) collective-permute-start(f32[2,16,1]{2,1,0:T(8,128)S(1)} %get-tuple-element.128), channel_id=1, source_target_pairs={{0,1},{1,2},{2,3},{3,4},{4,5},{5,6},{6,7},{7,0},{8,9},{9,10},{10,1... | collective-permute-start | bytes 392 | tf_op jit(solution)/shard_map/ppermute | solution.py:19
  93.5 18.6 %collective-permute-start.16 = (f32[2,1,512]{2,1,0:T(1,128)S(1)}, f32[2,1,512]{2,1,0:T(1,128)S(1)}, u32[]{:S(2)}, u32[]{:S(2)}) collective-permute-start(f32[2,1,512]{2,1,0:T(1,128)S(1)} %get-tuple-element.127), channel_id=1, source_target_pairs={{8,0},{16,8},{24,16},{32,24},{40,32},{48,40},{56,48},{64,56},{72,6... | collective-permute-start | bytes 12296 | tf_op jit(solution)/shard_map/ppermute | solution.py:21
  95.1 17.1 %collective-permute-start.17 = (f32[2,16,1]{2,1,0:T(8,128)S(1)}, f32[2,16,1]{2,1,0:T(8,128)S(1)}, u32[]{:S(2)}, u32[]{:S(2)}) collective-permute-start(f32[2,16,1]{2,1,0:T(8,128)S(1)} %get-tuple-element.125), channel_id=1, source_target_pairs={{0,1},{1,2},{2,3},{3,4},{4,5},{5,6},{6,7},{7,0},{8,9},{9,10},{10,1... | collective-permute-start | bytes 392 | tf_op jit(solution)/shard_map/ppermute | solution.py:19
  97.1 15.2 %collective-permute-start.18 = (f32[2,16,1]{2,1,0:T(8,128)S(1)}, f32[2,16,1]{2,1,0:T(8,128)S(1)}, u32[]{:S(2)}, u32[]{:S(2)}) collective-permute-start(f32[2,16,1]{2,1,0:T(8,128)S(1)} %get-tuple-element.124), channel_id=1, source_target_pairs={{1,0},{2,1},{3,2},{4,3},{5,4},{6,5},{7,6},{0,7},{9,8},{10,9},{11,1... | collective-permute-start | bytes 392 | tf_op jit(solution)/shard_map/ppermute | solution.py:21
  107.0 5.8 collective-permute-start.19
  113.2 19.8 %collective-permute-start.20 = (f32[2,1,512]{2,1,0:T(1,128)S(1)}, f32[2,1,512]{2,1,0:T(1,128)S(1)}, u32[]{:S(2)}, u32[]{:S(2)}) collective-permute-start(f32[2,1,512]{2,1,0:T(1,128)S(1)} %get-tuple-element.123), channel_id=1, source_target_pairs={{0,8},{8,16},{16,24},{24,32},{32,40},{40,48},{48,56},{56,64},{64,7... | collective-permute-start | bytes 12296 | tf_op jit(solution)/shard_map/ppermute | solution.py:19
  118.4 14.6 %collective-permute-start.21 = (f32[2,16,1]{2,1,0:T(8,128)S(1)}, f32[2,16,1]{2,1,0:T(8,128)S(1)}, u32[]{:S(2)}, u32[]{:S(2)}) collective-permute-start(f32[2,16,1]{2,1,0:T(8,128)S(1)} %get-tuple-element.121), channel_id=1, source_target_pairs={{0,1},{1,2},{2,3},{3,4},{4,5},{5,6},{6,7},{7,0},{8,9},{9,10},{10,1... | collective-permute-start | bytes 392 | tf_op jit(solution)/shard_map/ppermute | solution.py:19
  120.3 12.9 %collective-permute-start.23 = (f32[2,1,512]{2,1,0:T(1,128)S(1)}, f32[2,1,512]{2,1,0:T(1,128)S(1)}, u32[]{:S(2)}, u32[]{:S(2)}) collective-permute-start(f32[2,1,512]{2,1,0:T(1,128)S(1)} %get-tuple-element.122), channel_id=1, source_target_pairs={{8,0},{16,8},{24,16},{32,24},{40,32},{48,40},{56,48},{64,56},{72,6... | collective-permute-start | bytes 12296 | tf_op jit(solution)/shard_map/ppermute | solution.py:21
  121.6 11.6 %collective-permute-start.22 = (f32[2,16,1]{2,1,0:T(8,128)S(1)}, f32[2,16,1]{2,1,0:T(8,128)S(1)}, u32[]{:S(2)}, u32[]{:S(2)}) collective-permute-start(f32[2,16,1]{2,1,0:T(8,128)S(1)} %get-tuple-element.120), channel_id=1, source_target_pairs={{1,0},{2,1},{3,2},{4,3},{5,4},{6,5},{7,6},{0,7},{9,8},{10,9},{11,1... | collective-permute-start | bytes 392 | tf_op jit(solution)/shard_map/ppermute | solution.py:21
  133.3 473.8 %copy-start.2 = (f32[5,16,512]{2,1,0:T(8,128)}, f32[5,16,512]{2,1,0:T(8,128)S(1)}, u32[]{:S(2)}) copy-start(f32[5,16,512]{2,1,0:T(8,128)S(1)} %get-tuple-element.145) | copy-start | bytes 491524
where the time goes:
time: 732 us; the launch traced here: 731 us
  blocking collectives  554 us (76%)
  starting transfers between devices  108 us (15%)
  other arithmetic  44.2 us (6%)
  waiting for transfers between devices  14.9 us (2%)
    all_gather x1, blocking collectives, per_device(): lax.all_gather(local_waves, ('axial', 'hoop'), axis=1, tiled=True)  473 us
    psum x1, blocking collectives, per_device(): summed = lax.psum(partial_value, 'act')  81.4 us
    ppermute x12, starting transfers between devices, padded(): lax.ppermute(head, axis, [((i + 1) % count, i) for i in range(ends)])  69.1 us
    ppermute x12, starting transfers between devices, padded(): lax.ppermute(tail, axis, [(i, (i + 1) % count) for i in range(ends)])  39.3 us
    reduce_sum x16, other arithmetic, pick_block(): return (running + jnp.sum(picked, axis=(0, 1)), None)  39.2 us
  transfers between devices with their start and end apart: 24, of which 5 were waited for; matrix products, arithmetic and copies ran while one was open for 1% of the time, Pallas kernels for 0%

commit v1 on v0

v1 whole, which is shorter than its diff:
```python
import functools

import jax
import jax.numpy as jnp
from jax import lax
from jax.experimental import pallas as pl
from jax.experimental.pallas import tpu as pltpu
from jax.sharding import PartitionSpec as P

STEPS = 3
HALO = 2 * STEPS


def exchange(cells, halo):
    na = lax.axis_size("axial")
    nh = lax.axis_size("hoop")
    from_above = lax.ppermute(cells[:, -halo:, :], "axial", [(i, i + 1) for i in range(na - 1)])
    from_below = lax.ppermute(cells[:, :halo, :], "axial", [(i + 1, i) for i in range(na - 1)])
    cells = jnp.concatenate([from_above, cells, from_below], axis=1)
    from_left = lax.ppermute(cells[:, :, -halo:], "hoop", [(j, (j + 1) % nh) for j in range(nh)])
    from_right = lax.ppermute(cells[:, :, :halo], "hoop", [((j + 1) % nh, j) for j in range(nh)])
    return jnp.concatenate([from_left, cells, from_right], axis=2)


def inner(f):
    return f[1:-1, 1:-1]


def advance(fields, moduli_map):
    speed_axial, speed_hoop, normal_axial, normal_hoop, shear_stress = fields
    m = [inner(moduli_map[i]) for i in range(6)]
    mobility_axial, mobility_hoop = m[0], m[1]
    na_c = inner(normal_axial)
    nh_c = inner(normal_hoop)
    ss_c = inner(shear_stress)
    speed_axial = inner(speed_axial) + mobility_axial * (
        (normal_axial[2:, 1:-1] - na_c) + (ss_c - shear_stress[1:-1, :-2])
    )
    speed_hoop = inner(speed_hoop) + mobility_hoop * (
        (normal_hoop[1:-1, 2:] - nh_c) + (ss_c - shear_stress[:-2, 1:-1])
    )
    stiff_axial, stiff_cross, stiff_hoop, stiff_shear = (inner(m[i]) for i in range(2, 6))
    va_c = inner(speed_axial)
    vh_c = inner(speed_hoop)
    strain_axial = va_c - speed_axial[:-2, 1:-1]
    strain_hoop = vh_c - speed_hoop[1:-1, :-2]
    normal_axial = inner(na_c) + stiff_axial * strain_axial + stiff_cross * strain_hoop
    normal_hoop = inner(nh_c) + stiff_cross * strain_axial + stiff_hoop * strain_hoop
    strain_shear = (speed_axial[1:-1, 2:] - va_c) + (speed_hoop[2:, 1:-1] - vh_c)
    shear_stress = inner(ss_c) + stiff_shear * strain_shear
    return (va_c, vh_c, normal_axial, normal_hoop, shear_stress), m


def image_kernel(rows_ref, delays_ref, out_ref):
    pairs, pix_rows, pix_cols = delays_ref.shape
    lanes = rows_ref.shape[1]

    def body(k, acc):
        d = delays_ref[k]
        low = jnp.broadcast_to(rows_ref[pl.ds(2 * k, 1), :], (pix_rows, pix_cols))
        high = jnp.broadcast_to(rows_ref[pl.ds(2 * k + 1, 1), :], (pix_rows, pix_cols))
        idx = d & (lanes - 1)
        got_low = jnp.take_along_axis(low, idx, axis=1, mode="promise_in_bounds")
        got_high = jnp.take_along_axis(high, idx, axis=1, mode="promise_in_bounds")
        return acc + jnp.where(d >= lanes, got_high, got_low)

    acc = lax.fori_loop(0, pairs, body, jnp.zeros((pix_rows, pix_cols), jnp.float32), unroll=8)
    out_ref[...] = acc


def image(rows, delays):
    pairs, pix_rows, pix_cols = delays.shape
    return pl.pallas_call(
        image_kernel,
        out_shape=jax.ShapeDtypeStruct((pix_rows, pix_cols), jnp.float32),
        in_specs=[pl.BlockSpec(memory_space=pltpu.VMEM)] * 2,
        out_specs=pl.BlockSpec(memory_space=pltpu.VMEM),
        cost_estimate=pl.CostEstimate(
            flops=8 * pairs * pix_rows * pix_cols,
            bytes_accessed=4 * (rows.size + delays.size + pix_rows * pix_cols),
            transcendentals=0,
        ),
    )(rows, delays)


def gather_waves(local_waves):
    inner_waves = lax.all_gather(local_waves, "hoop", axis=0, tiled=True)
    return lax.all_gather(inner_waves, "axial", axis=0, tiled=True)


def per_device(wave_state, layup_zone, moduli, sensors, history, receivers, delays):
    rows, cols = layup_zone.shape
    na = lax.axis_size("axial")
    stacked = jnp.concatenate(
        [wave_state[0], layup_zone.astype(jnp.float32)[None]], axis=0
    )
    padded = exchange(stacked, HALO)
    zone = padded[5].astype(jnp.int32)
    global_row = lax.axis_index("axial") * rows - HALO + lax.broadcasted_iota(
        jnp.int32, zone.shape, 0
    )
    inside = (global_row >= 0) & (global_row < na * rows)
    moduli_map = jnp.zeros((moduli.shape[1],) + zone.shape, jnp.float32)
    for zone_level in range(moduli.shape[0]):
        moduli_map = jnp.where(
            (zone == zone_level)[None], moduli[zone_level][:, None, None], moduli_map
        )
    moduli_map = jnp.where(inside[None], moduli_map, jnp.float32(0.0))
    fields = tuple(padded[c] for c in range(5))
    samples = []
    for step_index in range(STEPS):
        fields, moduli_map = advance(fields, moduli_map)
        moduli_map = [inner(m) for m in moduli_map]
        off = HALO - 2 * (step_index + 1)
        total = fields[2] + fields[3]
        tile = total[off:off + rows, off:off + cols]
        samples.append(tile.reshape(-1)[sensors])
        moduli_map = jnp.stack(moduli_map)
    next_state = jnp.stack(fields)[None]
    recorded = jnp.stack(samples, axis=1)[None]
    local_waves = jnp.concatenate([history[0], recorded[0]], axis=1)
    waveforms = gather_waves(local_waves)
    sample_count = waveforms.shape[1]
    chosen = waveforms[receivers[0]].reshape(2 * receivers.shape[1], sample_count // 2)
    partial_value = image(chosen, delays[0])
    summed = lax.psum(partial_value, "act")
    damage_map = summed * summed / (receivers.shape[1] * lax.axis_size("act"))
    return (next_state, recorded, damage_map)


def solution(mesh):
    return jax.shard_map(
        per_device,
        mesh=mesh,
        in_specs=(
            P("act", None, "axial", "hoop"),
            P("axial", "hoop"),
            P(),
            P(("axial", "hoop")),
            P("act", ("axial", "hoop"), None),
            P("act", None),
            P("act", None, "axial", "hoop"),
        ),
        out_specs=(
            P("act", None, "axial", "hoop"),
            P("act", ("axial", "hoop"), None),
            P("axial", "hoop"),
        ),
        check_vma=False,
    )
```

time: 732 us -> 132 us (0.18)
  blocking collectives: 554 us -> 89.9 us
  starting transfers between devices: 108 us -> 20.1 us
  other arithmetic: 44.2 us -> 5.44 us
  waiting for transfers between devices: 14.9 us -> 4.29 us
    all_gather x1 -> x2, blocking collectives: 473 us -> 61 us  [the longest x1 40.1 us: gather_waves(): inner_waves = lax.all_gather(local_waves, 'hoop', axis=0, tiled=True)]
    ppermute x24 -> x4, starting transfers between devices: 108 us -> 20.1 us  [the longest x1 11.3 us: exchange(): lax.ppermute(cells[:, :, :halo], 'hoop', [((j + 1) % nh, j) for j in rang...]
    psum x1, blocking collectives: 81.4 us -> 28.9 us  [per_device(): summed = lax.psum(partial_value, 'act')]
    reduce_sum x16 -> x0, other arithmetic: 39.2 us -> none  [pick_block(): return (running + jnp.sum(picked, axis=(0, 1)), None)]
    ppermute x24 -> x4, waiting for transfers between devices: 14.9 us -> 4.29 us  [the longest x1 2.69 us: exchange(): lax.ppermute(cells[:, :halo, :], 'axial', [(i + 1, i) for i in range(na -...]
  transfers between devices with their start and end apart: 24 -> 4, of which waited for: 5 -> 3; matrix products, arithmetic and copies ran while one was open for 1% -> 0% of each run, Pallas kernels for 0% -> 0%
where the time goes in v1:
time: 132 us; the launch traced here: 131 us
  blocking collectives  89.9 us (68%)
  starting transfers between devices  20.1 us (15%)
  local copies, waits for them, and re-layouts  6.42 us (5%)
  other arithmetic  5.44 us (4%)
  waiting for transfers between devices  4.29 us (3%)
  Pallas kernels  4.28 us (3%)
    all_gather x1, blocking collectives, gather_waves(): inner_waves = lax.all_gather(local_waves, 'hoop', axis=0, tiled=True)  40.1 us
    psum x1, blocking collectives, per_device(): summed = lax.psum(partial_value, 'act')  28.9 us
    all_gather x1, blocking collectives, gather_waves(): return lax.all_gather(inner_waves, 'axial', axis=0, tiled=True)  20.9 us
    ppermute x1, starting transfers between devices, exchange(): lax.ppermute(cells[:, :, :halo], 'hoop', [((j + 1) % nh, j) for j in rang...  11.3 us
    pallas_call x1, Pallas kernels, image(): pl.pallas_call(image_kernel, out_shape=jax.ShapeDtypeStruct((pix_rows, pi...  4.28 us
    ppermute x1, starting transfers between devices, exchange(): lax.ppermute(cells[:, -halo:, :], 'axial', [(i, i + 1) for i in range(na...  4.04 us
    ppermute x1, starting transfers between devices, exchange(): lax.ppermute(cells[:, :, -halo:], 'hoop', [(j, (j + 1) % nh) for j in ran...  3.55 us
    unnamed x21, local copies, waits for them, and re-layouts  2.74 us
  transfers between devices with their start and end apart: 4, of which 3 were waited for; matrix products, arithmetic and copies ran while one was open for 0% of the time, Pallas kernels for 0%

profile of v1, /device:TPU:1, one launch (start us, length us, event | category | flops | bytes accessed | tf_op | source)
XLA Modules:
  0.0 131.3 jit_solution(2164414777708092811)
XLA Ops:
  0.6 0.8 convert_bitcast_fusion
  1.4 0.0 copy-start
  1.4 1.0 fusion
  2.4 0.0 copy-start.3
  2.4 4.0 %collective-permute-start = (f32[6,6,512]{2,1,0:T(8,128)S(1)}, f32[6,6,512]{2,1,0:T(8,128)S(1)}, u32[]{:S(2)}, u32[]{:S(2)}) collective-permute-start(f32[6,6,512]{2,1,0:T(8,128)S(1)} %get-tuple-element.40), channel_id=1, source_target_pairs={{0,8},{8,16},{16,24},{24,32},{32,40},{40,48},{48,56},{56,64},{64,7... | collective-permute-start | bytes 221192 | tf_op jit(solution)/shard_map/ppermute | solution.py:17
  6.4 1.3 collective-permute-start.1
  7.7 0.0 copy-done.3
  7.8 0.0 copy-start.4
  7.8 0.6 copy-done.4
  8.4 0.0 copy-start.5
  8.4 0.6 copy-done.5
  9.1 0.0 collective-permute-done
  9.1 2.7 %collective-permute-done.1 = f32[6,6,512]{2,1,0:T(8,128)S(1)} collective-permute-done((f32[6,6,512]{2,1,0:T(8,128)S(1)}, f32[6,6,512]{2,1,0:T(8,128)S(1)}, u32[]{:S(2)}, u32[]{:S(2)}) %collective-permute-start.1) | collective-permute-done | bytes 73760 | tf_op jit(solution)/shard_map/ppermute | solution.py:18
  11.8 0.0 copy-done
  11.8 0.1 pad_maximum_fusion.4
  11.9 3.5 %collective-permute-start.2 = (f32[6,28,6]{2,1,0:T(8,128)S(1)}, f32[6,28,6]{2,1,0:T(8,128)S(1)}, u32[]{:S(2)}, u32[]{:S(2)}) collective-permute-start(f32[6,28,6]{2,1,0:T(8,128)S(1)} %get-tuple-element.34), channel_id=1, source_target_pairs={{0,1},{1,2},{2,3},{3,4},{4,5},{5,6},{6,7},{7,0},{8,9},{9,10},{10,1... | collective-permute-start | bytes 12104 | tf_op jit(solution)/shard_map/ppermute | solution.py:20
  15.5 11.3 %collective-permute-start.3 = (f32[6,28,6]{2,1,0:T(8,128)S(1)}, f32[6,28,6]{2,1,0:T(8,128)S(1)}, u32[]{:S(2)}, u32[]{:S(2)}) collective-permute-start(f32[6,28,6]{2,1,0:T(8,128)S(1)} %get-tuple-element.35), channel_id=1, source_target_pairs={{1,0},{2,1},{3,2},{4,3},{5,4},{6,5},{7,6},{0,7},{9,8},{10,9},{11,1... | collective-permute-start | bytes 12104 | tf_op jit(solution)/shard_map/ppermute | solution.py:21
  26.7 0.1 collective-permute-done.2
  26.8 1.5 %collective-permute-done.3 = f32[6,28,6]{2,1,0:T(8,128)S(1)} collective-permute-done((f32[6,28,6]{2,1,0:T(8,128)S(1)}, f32[6,28,6]{2,1,0:T(8,128)S(1)}, u32[]{:S(2)}, u32[]{:S(2)}) %collective-permute-start.3) | collective-permute-done | bytes 4064 | tf_op jit(solution)/shard_map/ppermute | solution.py:21
  28.3 0.3 pad_maximum_fusion
  28.6 0.1 compare_bitcast_fusion.7
  28.8 0.6 select_select_fusion
  29.4 0.1 slice_bitcast_fusion.6
  29.5 0.3 fusion.6
  29.8 0.2 fusion.28
  29.9 0.2 fusion.30
  30.1 0.1 fusion.31
  30.2 0.2 fusion.25
  30.5 0.2 fusion.10
  30.7 0.2 fusion.16
  30.9 0.6 gather_fusion
  31.5 0.1 copy.21
  31.6 0.2 fusion.9
  31.8 0.1 add_bitcast_fusion
  32.0 0.6 gather_fusion.1
  32.7 0.1 copy.22
  32.8 0.0 copy-start.2
  32.8 0.6 gather_fusion.2
  33.4 0.1 copy.23
  33.5 0.1 bitcast_dynamic-update-slice_fusion.3
  33.6 0.0 copy-done.2
  33.6 0.1 maximum_bitcast_fusion
  33.7 40.1 %all-gather = f32[8,4,256]{2,1,0:T(4,128)S(1)} all-gather(f32[1,4,256]{2,1,0:T(4,128)S(1)} %maximum_bitcast_fusion), channel_id=1, replica_groups=mesh['act'=4,'axial'=16,'hoop'=8] {'hoop'}, dimensions={0}, use_global_device_ids=true | all-gather | bytes 36864 | tf_op jit(solution)/shard_map/all_gather | solution.py:87
  73.8 20.9 %all_gather.7 = f32[512,256]{1,0:T(8,128)S(1)} all-gather(f32[32,256]{1,0:T(8,128)S(1)} %reshape.102), channel_id=1, replica_groups=mesh['act'=4,'axial'=16,'hoop'=8] {'axial'}, dimensions={0}, use_global_device_ids=true | all-gather | bytes 557056 | tf_op jit(solution)/shard_map/all_gather | solution.py:88
  94.7 0.8 gather_fusion.3
  95.4 0.7 reshape.65.rows_ref
  96.1 4.3 %shard_map.94 = f32[16,128]{1,0:T(8,128)} custom-call(f32[256,128]{1,0:T(8,128)} %reshape.65.rows_ref, s32[128,16,128]{2,1,0:T(8,128)} %bitcast.98), custom_call_target="tpu_custom_call" | custom-call | flops 2097152 | bytes 1187840 | tf_op jit(solution)/shard_map/pallas_call | solution.py:73
  100.4 28.9 %psum.7 = f32[16,128]{1,0:T(8,128)S(1)} all-reduce(f32[16,128]{1,0:T(8,128)} %shard_map.94), channel_id=1, replica_groups=mesh['act'=4,'axial'=16,'hoop'=8] {'act'}, use_global_device_ids=true, to_apply=%region_0.1 | all-reduce | flops 2048 | bytes 16384 | tf_op jit(solution)/shard_map/psum | solution.py:126
  129.3 0.6 multiply_multiply_fusion
  129.9 0.6 copy.24
  130.4 0.1 bitcast_dynamic-update-slice_fusion.2
  130.5 0.1 fusion.36
  130.7 0.0 copy-start.1
  130.7 0.7 copy-done.1
  (13 shorter events, 0.1 us)
Async XLA Ops:
  1.4 10.4 %copy-start = (f32[1,5,16,512]{3,2,1,0:T(8,128)S(1)}, f32[1,5,16,512]{3,2,1,0:T(8,128)}, u32[]{:S(2)}) copy-start(f32[1,5,16,512]{3,2,1,0:T(8,128)} %param.7) | copy-start | bytes 491524
  2.4 5.4 %copy-start.3 = (f32[8,6]{1,0:T(8,128)S(1)}, f32[8,6]{1,0:T(8,128)}, u32[]{:S(2)}) copy-start(f32[8,6]{1,0:T(8,128)} %param.9) | copy-start | bytes 580
  2.4 6.7 %collective-permute-start = (f32[6,6,512]{2,1,0:T(8,128)S(1)}, f32[6,6,512]{2,1,0:T(8,128)S(1)}, u32[]{:S(2)}, u32[]{:S(2)}) collective-permute-start(f32[6,6,512]{2,1,0:T(8,128)S(1)} %get-tuple-element.40), channel_id=1, source_target_pairs={{0,8},{8,16},{16,24},{24,32},{32,40},{40,48},{48,56},{56,64},{64,7... | collective-permute-start | bytes 221192 | tf_op jit(solution)/shard_map/ppermute | solution.py:17
  6.4 5.4 %collective-permute-start.1 = (f32[6,6,512]{2,1,0:T(8,128)S(1)}, f32[6,6,512]{2,1,0:T(8,128)S(1)}, u32[]{:S(2)}, u32[]{:S(2)}) collective-permute-start(f32[6,6,512]{2,1,0:T(8,128)S(1)} %get-tuple-element.41), channel_id=1, source_target_pairs={{8,0},{16,8},{24,16},{32,24},{40,32},{48,40},{56,48},{64,56},{72,6... | collective-permute-start | bytes 221192 | tf_op jit(solution)/shard_map/ppermute | solution.py:18
  7.8 0.7 copy-start.4
  8.4 0.7 copy-start.5
  11.9 14.9 %collective-permute-start.2 = (f32[6,28,6]{2,1,0:T(8,128)S(1)}, f32[6,28,6]{2,1,0:T(8,128)S(1)}, u32[]{:S(2)}, u32[]{:S(2)}) collective-permute-start(f32[6,28,6]{2,1,0:T(8,128)S(1)} %get-tuple-element.34), channel_id=1, source_target_pairs={{0,1},{1,2},{2,3},{3,4},{4,5},{5,6},{6,7},{7,0},{8,9},{9,10},{10,1... | collective-permute-start | bytes 12104 | tf_op jit(solution)/shard_map/ppermute | solution.py:20
  15.5 12.9 %collective-permute-start.3 = (f32[6,28,6]{2,1,0:T(8,128)S(1)}, f32[6,28,6]{2,1,0:T(8,128)S(1)}, u32[]{:S(2)}, u32[]{:S(2)}) collective-permute-start(f32[6,28,6]{2,1,0:T(8,128)S(1)} %get-tuple-element.35), channel_id=1, source_target_pairs={{1,0},{2,1},{3,2},{4,3},{5,4},{6,5},{7,6},{0,7},{9,8},{10,9},{11,1... | collective-permute-start | bytes 12104 | tf_op jit(solution)/shard_map/ppermute | solution.py:21
  32.8 0.8 copy-start.2
  130.7 0.7 copy-start.1

commit v2 on v1

--- a/solution.py
+++ b/solution.py
@@ -83,9 +83,22 @@
     )(rows, delays)
 
 
+def gather_doubling(block, axis):
+    count = lax.axis_size(axis)
+    me = lax.axis_index(axis)
+    stride = 1
+    while stride < count:
+        other = lax.ppermute(block, axis, [(i, i ^ stride) for i in range(count)])
+        lower = (me // stride) % 2 == 0
+        block = jnp.where(
+            lower, jnp.concatenate([block, other]), jnp.concatenate([other, block])
+        )
+        stride *= 2
+    return block
+
+
 def gather_waves(local_waves):
-    inner_waves = lax.all_gather(local_waves, "hoop", axis=0, tiled=True)
-    return lax.all_gather(inner_waves, "axial", axis=0, tiled=True)
+    return gather_doubling(gather_doubling(local_waves, "hoop"), "axial")
 
 
 def per_device(wave_state, layup_zone, moduli, sensors, history, receivers, delays):

time: 132 us -> 114 us (0.86)
  the two profiles are of different devices: /device:TPU:1 before, /device:TPU:506 now
where the time goes in v2:
time: 114 us; the launch traced here: 113 us
  waiting for transfers between devices  53 us (46%)
  starting transfers between devices  28.7 us (25%)
  blocking collectives  14.7 us (13%)
  local copies, waits for them, and re-layouts  5.68 us (5%)
  other arithmetic  5.61 us (5%)
  Pallas kernels  4.28 us (4%)
  between operations  1.17 us (1%)
    ppermute x7, waiting for transfers between devices, gather_doubling(): other = lax.ppermute(block, axis, [(i, i ^ stride) for i in range(count)])  36.7 us
    psum x1, blocking collectives, per_device(): summed = lax.psum(partial_value, 'act')  14.7 us
    ppermute x7, starting transfers between devices, gather_doubling(): other = lax.ppermute(block, axis, [(i, i ^ stride) for i in range(count)])  14.1 us
    ppermute x1, waiting for transfers between devices, exchange(): lax.ppermute(cells[:, :, :halo], 'hoop', [((j + 1) % nh, j) for j in rang...  10.6 us
    ppermute x1, starting transfers between devices, exchange(): lax.ppermute(cells[:, :, -halo:], 'hoop', [(j, (j + 1) % nh) for j in ran...  6.79 us
    ppermute x1, waiting for transfers between devices, exchange(): lax.ppermute(cells[:, :halo, :], 'axial', [(i + 1, i) for i in range(na -...  5.11 us
    pallas_call x1, Pallas kernels, image(): pl.pallas_call(image_kernel, out_shape=jax.ShapeDtypeStruct((pix_rows, pi...  4.28 us
    ppermute x1, starting transfers between devices, exchange(): lax.ppermute(cells[:, -halo:, :], 'axial', [(i, i + 1) for i in range(na...  3.06 us
  transfers between devices with their start and end apart: 11, of which 10 were waited for; matrix products, arithmetic and copies ran while one was open for 1% of the time, Pallas kernels for 0%

profile of v2, /device:TPU:506, one launch (start us, length us, event | category | flops | bytes accessed | tf_op | source)
XLA Modules:
  0.0 113.1 jit_solution(2157013728459116838)
XLA Ops:
  0.6 0.8 convert_bitcast_fusion
  1.4 1.0 fusion
  2.4 0.0 copy-start.3
  2.4 3.1 %collective-permute-start = (f32[6,6,512]{2,1,0:T(8,128)S(1)}, f32[6,6,512]{2,1,0:T(8,128)S(1)}, u32[]{:S(2)}, u32[]{:S(2)}) collective-permute-start(f32[6,6,512]{2,1,0:T(8,128)S(1)} %get-tuple-element.37), channel_id=1, source_target_pairs={{0,8},{8,16},{16,24},{24,32},{32,40},{40,48},{48,56},{56,64},{64,7... | collective-permute-start | bytes 221192 | tf_op jit(solution)/shard_map/ppermute | solution.py:17
  5.5 2.8 %collective-permute-start.1 = (f32[6,6,512]{2,1,0:T(8,128)S(1)}, f32[6,6,512]{2,1,0:T(8,128)S(1)}, u32[]{:S(2)}, u32[]{:S(2)}) collective-permute-start(f32[6,6,512]{2,1,0:T(8,128)S(1)} %get-tuple-element.38), channel_id=1, source_target_pairs={{8,0},{16,8},{24,16},{32,24},{40,32},{48,40},{56,48},{64,56},{72,6... | collective-permute-start | bytes 221192 | tf_op jit(solution)/shard_map/ppermute | solution.py:18
  8.3 0.0 copy-done.3
  8.3 0.0 copy-start.4
  8.3 0.6 copy-done.4
  9.0 0.0 collective-permute-done
  9.0 5.1 %collective-permute-done.1 = f32[6,6,512]{2,1,0:T(8,128)S(1)} collective-permute-done((f32[6,6,512]{2,1,0:T(8,128)S(1)}, f32[6,6,512]{2,1,0:T(8,128)S(1)}, u32[]{:S(2)}, u32[]{:S(2)}) %collective-permute-start.1) | collective-permute-done | bytes 73760 | tf_op jit(solution)/shard_map/ppermute | solution.py:18
  14.1 0.0 copy-done
  14.1 0.1 pad_maximum_fusion.4
  14.2 6.8 %collective-permute-start.2 = (f32[6,28,6]{2,1,0:T(8,128)S(1)}, f32[6,28,6]{2,1,0:T(8,128)S(1)}, u32[]{:S(2)}, u32[]{:S(2)}) collective-permute-start(f32[6,28,6]{2,1,0:T(8,128)S(1)} %get-tuple-element.31), channel_id=1, source_target_pairs={{0,1},{1,2},{2,3},{3,4},{4,5},{5,6},{6,7},{7,0},{8,9},{9,10},{10,1... | collective-permute-start | bytes 12104 | tf_op jit(solution)/shard_map/ppermute | solution.py:20
  21.0 1.9 %collective-permute-start.3 = (f32[6,28,6]{2,1,0:T(8,128)S(1)}, f32[6,28,6]{2,1,0:T(8,128)S(1)}, u32[]{:S(2)}, u32[]{:S(2)}) collective-permute-start(f32[6,28,6]{2,1,0:T(8,128)S(1)} %get-tuple-element.32), channel_id=1, source_target_pairs={{1,0},{2,1},{3,2},{4,3},{5,4},{6,5},{7,6},{0,7},{9,8},{10,9},{11,1... | collective-permute-start | bytes 12104 | tf_op jit(solution)/shard_map/ppermute | solution.py:21
  22.9 0.6 collective-permute-done.2
  23.5 10.6 %collective-permute-done.3 = f32[6,28,6]{2,1,0:T(8,128)S(1)} collective-permute-done((f32[6,28,6]{2,1,0:T(8,128)S(1)}, f32[6,28,6]{2,1,0:T(8,128)S(1)}, u32[]{:S(2)}, u32[]{:S(2)}) %collective-permute-start.3) | collective-permute-done | bytes 4064 | tf_op jit(solution)/shard_map/ppermute | solution.py:21
  34.1 0.3 pad_maximum_fusion
  34.4 0.1 compare_bitcast_fusion.7
  34.5 0.6 select_select_fusion
  35.2 0.1 slice_bitcast_fusion.6
  35.2 0.3 fusion.6
  35.5 0.2 fusion.28
  35.7 0.2 fusion.30
  35.9 0.1 fusion.31
  36.0 0.2 fusion.25
  36.3 0.2 fusion.10
  36.5 0.2 fusion.16
  36.7 0.6 gather_fusion
  37.3 0.1 copy.16
  37.4 0.2 fusion.9
  37.6 0.1 add_bitcast_fusion
  37.8 0.6 gather_fusion.1
  38.4 0.1 copy.17
  38.5 0.6 gather_fusion.2
  39.2 0.1 copy.18
  39.3 0.6 copy-done.1
  39.9 0.1 pad_maximum_fusion.6
  39.9 1.9 %collective-permute-start.4 = (f32[4,256]{1,0:T(4,128)S(1)}, f32[4,256]{1,0:T(4,128)S(1)}, u32[]{:S(2)}, u32[]{:S(2)}) collective-permute-start(f32[4,256]{1,0:T(4,128)S(1)} %pad_maximum_fusion.6), channel_id=1, source_target_pairs={{0,1},{1,0},{2,3},{3,2},{4,5},{5,4},{6,7},{7,6},{8,9},{9,8},{10,11... | collective-permute-start | bytes 12296 | tf_op jit(solution)/shard_map/ppermute | solution.py:91
  41.9 0.0 copy-done.5
  41.9 3.5 %collective-permute-done.4 = f32[4,256]{1,0:T(4,128)S(1)} collective-permute-done((f32[4,256]{1,0:T(4,128)S(1)}, f32[4,256]{1,0:T(4,128)S(1)}, u32[]{:S(2)}, u32[]{:S(2)}) %collective-permute-start.4) | collective-permute-done | bytes 4128 | tf_op jit(solution)/shard_map/ppermute | solution.py:91
  45.4 0.1 maximum_select_fusion.6
  45.5 1.9 %collective-permute-start.5 = (f32[8,256]{1,0:T(8,128)S(1)}, f32[8,256]{1,0:T(8,128)S(1)}, u32[]{:S(2)}, u32[]{:S(2)}) collective-permute-start(f32[8,256]{1,0:T(8,128)S(1)} %maximum_select_fusion.6), channel_id=1, source_target_pairs={{0,2},{1,3},{2,0},{3,1},{4,6},{5,7},{6,4},{7,5},{8,10},{9,11},{10,... | collective-permute-start | bytes 24584 | tf_op jit(solution)/shard_map/ppermute | solution.py:91
  47.6 4.4 %collective-permute-done.5 = f32[8,256]{1,0:T(8,128)S(1)} collective-permute-done((f32[8,256]{1,0:T(8,128)S(1)}, f32[8,256]{1,0:T(8,128)S(1)}, u32[]{:S(2)}, u32[]{:S(2)}) %collective-permute-start.5) | collective-permute-done | bytes 8224 | tf_op jit(solution)/shard_map/ppermute | solution.py:91
  51.9 1.9 %collective-permute-start.6 = (f32[16,256]{1,0:T(8,128)S(1)}, f32[16,256]{1,0:T(8,128)S(1)}, u32[]{:S(2)}, u32[]{:S(2)}) collective-permute-start(f32[16,256]{1,0:T(8,128)S(1)} %maximum_select_fusion.5), channel_id=1, source_target_pairs={{0,4},{1,5},{2,6},{3,7},{4,0},{5,1},{6,2},{7,3},{8,12},{9,13},{10,... | collective-permute-start | bytes 49160 | tf_op jit(solution)/shard_map/ppermute | solution.py:91
  53.9 0.1 bitcast_dynamic-update-slice_fusion.3
  53.9 7.5 %collective-permute-done.6 = f32[16,256]{1,0:T(8,128)S(1)} collective-permute-done((f32[16,256]{1,0:T(8,128)S(1)}, f32[16,256]{1,0:T(8,128)S(1)}, u32[]{:S(2)}, u32[]{:S(2)}) %collective-permute-start.6) | collective-permute-done | bytes 16416 | tf_op jit(solution)/shard_map/ppermute | solution.py:91
  61.5 1.9 %collective-permute-start.7 = (f32[32,256]{1,0:T(8,128)S(1)}, f32[32,256]{1,0:T(8,128)S(1)}, u32[]{:S(2)}, u32[]{:S(2)}) collective-permute-start(f32[32,256]{1,0:T(8,128)S(1)} %maximum_select_fusion.4), channel_id=1, source_target_pairs={{0,8},{8,0},{16,24},{24,16},{32,40},{40,32},{48,56},{56,48},{64,72... | collective-permute-start | bytes 98312 | tf_op jit(solution)/shard_map/ppermute | solution.py:91
  63.4 0.1 bitcast_dynamic-update-slice_fusion.2
  63.5 3.8 %collective-permute-done.7 = f32[32,256]{1,0:T(8,128)S(1)} collective-permute-done((f32[32,256]{1,0:T(8,128)S(1)}, f32[32,256]{1,0:T(8,128)S(1)}, u32[]{:S(2)}, u32[]{:S(2)}) %collective-permute-start.7) | collective-permute-done | bytes 32800 | tf_op jit(solution)/shard_map/ppermute | solution.py:91
  67.3 1.9 %collective-permute-start.8 = (f32[64,256]{1,0:T(8,128)S(1)}, f32[64,256]{1,0:T(8,128)S(1)}, u32[]{:S(2)}, u32[]{:S(2)}) collective-permute-start(f32[64,256]{1,0:T(8,128)S(1)} %maximum_select_fusion.3), channel_id=1, source_target_pairs={{0,16},{8,24},{16,0},{24,8},{32,48},{40,56},{48,32},{56,40},{64,80... | collective-permute-start | bytes 196616 | tf_op jit(solution)/shard_map/ppermute | solution.py:91
  69.2 5.7 %collective-permute-done.8 = f32[64,256]{1,0:T(8,128)S(1)} collective-permute-done((f32[64,256]{1,0:T(8,128)S(1)}, f32[64,256]{1,0:T(8,128)S(1)}, u32[]{:S(2)}, u32[]{:S(2)}) %collective-permute-start.8) | collective-permute-done | bytes 65568 | tf_op jit(solution)/shard_map/ppermute | solution.py:91
  75.0 2.4 %collective-permute-start.9 = (f32[128,256]{1,0:T(8,128)S(1)}, f32[128,256]{1,0:T(8,128)S(1)}, u32[]{:S(2)}, u32[]{:S(2)}) collective-permute-start(f32[128,256]{1,0:T(8,128)S(1)} %maximum_select_fusion.2), channel_id=1, source_target_pairs={{0,32},{8,40},{16,48},{24,56},{32,0},{40,8},{48,16},{56,24},{64,96... | collective-permute-start | bytes 393224 | tf_op jit(solution)/shard_map/ppermute | solution.py:91
  77.4 4.8 %collective-permute-done.9 = f32[128,256]{1,0:T(8,128)S(1)} collective-permute-done((f32[128,256]{1,0:T(8,128)S(1)}, f32[128,256]{1,0:T(8,128)S(1)}, u32[]{:S(2)}, u32[]{:S(2)}) %collective-permute-start.9) | collective-permute-done | bytes 131104 | tf_op jit(solution)/shard_map/ppermute | solution.py:91
  82.3 2.1 %collective-permute-start.10 = (f32[256,256]{1,0:T(8,128)S(1)}, f32[256,256]{1,0:T(8,128)S(1)}, u32[]{:S(2)}, u32[]{:S(2)}) collective-permute-start(f32[256,256]{1,0:T(8,128)S(1)} %maximum_select_fusion.1), channel_id=1, source_target_pairs={{0,64},{8,72},{16,80},{24,88},{32,96},{40,104},{48,112},{56,120},{... | collective-permute-start | bytes 786440 | tf_op jit(solution)/shard_map/ppermute | solution.py:91
  84.4 0.6 copy.19
  85.0 0.1 fusion.36
  85.1 0.0 copy-start.2
  85.1 6.9 %collective-permute-done.10 = f32[256,256]{1,0:T(8,128)S(1)} collective-permute-done((f32[256,256]{1,0:T(8,128)S(1)}, f32[256,256]{1,0:T(8,128)S(1)}, u32[]{:S(2)}, u32[]{:S(2)}) %collective-permute-start.10) | collective-permute-done | bytes 262176 | tf_op jit(solution)/shard_map/ppermute | solution.py:91
  92.1 0.0 copy-done.2
  92.1 0.8 gather_fusion.3
  92.9 0.6 reshape.65.rows_ref
  93.5 4.3 %shard_map.94 = f32[16,128]{1,0:T(8,128)} custom-call(f32[256,128]{1,0:T(8,128)} %reshape.65.rows_ref, s32[128,16,128]{2,1,0:T(8,128)} %bitcast.96), custom_call_target="tpu_custom_call" | custom-call | flops 2097152 | bytes 1187840 | tf_op jit(solution)/shard_map/pallas_call | solution.py:73
  97.8 14.7 %psum.7 = f32[16,128]{1,0:T(8,128)S(1)} all-reduce(f32[16,128]{1,0:T(8,128)} %shard_map.94), channel_id=1, replica_groups=mesh['act'=4,'axial'=16,'hoop'=8] {'act'}, use_global_device_ids=true, to_apply=%region_0.1 | all-reduce | flops 2048 | bytes 16384 | tf_op jit(solution)/shard_map/psum | solution.py:139
  112.5 0.6 multiply_multiply_fusion
  (21 shorter events, 0.2 us)
Async XLA Ops:
  1.4 12.7 %copy-start = (f32[1,5,16,512]{3,2,1,0:T(8,128)S(1)}, f32[1,5,16,512]{3,2,1,0:T(8,128)}, u32[]{:S(2)}) copy-start(f32[1,5,16,512]{3,2,1,0:T(8,128)} %param.7) | copy-start | bytes 491524
  2.4 5.9 %copy-start.3 = (f32[8,6]{1,0:T(8,128)S(1)}, f32[8,6]{1,0:T(8,128)}, u32[]{:S(2)}) copy-start(f32[8,6]{1,0:T(8,128)} %param.9) | copy-start | bytes 580
  2.4 6.6 %collective-permute-start = (f32[6,6,512]{2,1,0:T(8,128)S(1)}, f32[6,6,512]{2,1,0:T(8,128)S(1)}, u32[]{:S(2)}, u32[]{:S(2)}) collective-permute-start(f32[6,6,512]{2,1,0:T(8,128)S(1)} %get-tuple-element.37), channel_id=1, source_target_pairs={{0,8},{8,16},{16,24},{24,32},{32,40},{40,48},{48,56},{56,64},{64,7... | collective-permute-start | bytes 221192 | tf_op jit(solution)/shard_map/ppermute | solution.py:17
  5.5 8.6 %collective-permute-start.1 = (f32[6,6,512]{2,1,0:T(8,128)S(1)}, f32[6,6,512]{2,1,0:T(8,128)S(1)}, u32[]{:S(2)}, u32[]{:S(2)}) collective-permute-start(f32[6,6,512]{2,1,0:T(8,128)S(1)} %get-tuple-element.38), channel_id=1, source_target_pairs={{8,0},{16,8},{24,16},{32,24},{40,32},{48,40},{56,48},{64,56},{72,6... | collective-permute-start | bytes 221192 | tf_op jit(solution)/shard_map/ppermute | solution.py:18
  8.3 0.7 copy-start.4
  14.2 9.3 %collective-permute-start.2 = (f32[6,28,6]{2,1,0:T(8,128)S(1)}, f32[6,28,6]{2,1,0:T(8,128)S(1)}, u32[]{:S(2)}, u32[]{:S(2)}) collective-permute-start(f32[6,28,6]{2,1,0:T(8,128)S(1)} %get-tuple-element.31), channel_id=1, source_target_pairs={{0,1},{1,2},{2,3},{3,4},{4,5},{5,6},{6,7},{7,0},{8,9},{9,10},{10,1... | collective-permute-start | bytes 12104 | tf_op jit(solution)/shard_map/ppermute | solution.py:20
  21.0 13.1 %collective-permute-start.3 = (f32[6,28,6]{2,1,0:T(8,128)S(1)}, f32[6,28,6]{2,1,0:T(8,128)S(1)}, u32[]{:S(2)}, u32[]{:S(2)}) collective-permute-start(f32[6,28,6]{2,1,0:T(8,128)S(1)} %get-tuple-element.32), channel_id=1, source_target_pairs={{1,0},{2,1},{3,2},{4,3},{5,4},{6,5},{7,6},{0,7},{9,8},{10,9},{11,1... | collective-permute-start | bytes 12104 | tf_op jit(solution)/shard_map/ppermute | solution.py:21
  39.2 0.7 copy-start.1
  39.9 2.0 %copy-start.5 = (s32[1,128]{1,0:T(1,128)S(1)}, s32[1,128]{1,0:T(1,128)}, u32[]{:S(2)}) copy-start(s32[1,128]{1,0:T(1,128)} %param.12) | copy-start | bytes 1540
  39.9 5.5 %collective-permute-start.4 = (f32[4,256]{1,0:T(4,128)S(1)}, f32[4,256]{1,0:T(4,128)S(1)}, u32[]{:S(2)}, u32[]{:S(2)}) collective-permute-start(f32[4,256]{1,0:T(4,128)S(1)} %pad_maximum_fusion.6), channel_id=1, source_target_pairs={{0,1},{1,0},{2,3},{3,2},{4,5},{5,4},{6,7},{7,6},{8,9},{9,8},{10,11... | collective-permute-start | bytes 12296 | tf_op jit(solution)/shard_map/ppermute | solution.py:91
  45.5 6.4 %collective-permute-start.5 = (f32[8,256]{1,0:T(8,128)S(1)}, f32[8,256]{1,0:T(8,128)S(1)}, u32[]{:S(2)}, u32[]{:S(2)}) collective-permute-start(f32[8,256]{1,0:T(8,128)S(1)} %maximum_select_fusion.6), channel_id=1, source_target_pairs={{0,2},{1,3},{2,0},{3,1},{4,6},{5,7},{6,4},{7,5},{8,10},{9,11},{10,... | collective-permute-start | bytes 24584 | tf_op jit(solution)/shard_map/ppermute | solution.py:91
  51.9 9.5 %collective-permute-start.6 = (f32[16,256]{1,0:T(8,128)S(1)}, f32[16,256]{1,0:T(8,128)S(1)}, u32[]{:S(2)}, u32[]{:S(2)}) collective-permute-start(f32[16,256]{1,0:T(8,128)S(1)} %maximum_select_fusion.5), channel_id=1, source_target_pairs={{0,4},{1,5},{2,6},{3,7},{4,0},{5,1},{6,2},{7,3},{8,12},{9,13},{10,... | collective-permute-start | bytes 49160 | tf_op jit(solution)/shard_map/ppermute | solution.py:91
  61.5 5.8 %collective-permute-start.7 = (f32[32,256]{1,0:T(8,128)S(1)}, f32[32,256]{1,0:T(8,128)S(1)}, u32[]{:S(2)}, u32[]{:S(2)}) collective-permute-start(f32[32,256]{1,0:T(8,128)S(1)} %maximum_select_fusion.4), channel_id=1, source_target_pairs={{0,8},{8,0},{16,24},{24,16},{32,40},{40,32},{48,56},{56,48},{64,72... | collective-permute-start | bytes 98312 | tf_op jit(solution)/shard_map/ppermute | solution.py:91
  67.3 7.7 %collective-permute-start.8 = (f32[64,256]{1,0:T(8,128)S(1)}, f32[64,256]{1,0:T(8,128)S(1)}, u32[]{:S(2)}, u32[]{:S(2)}) collective-permute-start(f32[64,256]{1,0:T(8,128)S(1)} %maximum_select_fusion.3), channel_id=1, source_target_pairs={{0,16},{8,24},{16,0},{24,8},{32,48},{40,56},{48,32},{56,40},{64,80... | collective-permute-start | bytes 196616 | tf_op jit(solution)/shard_map/ppermute | solution.py:91
  75.0 7.3 %collective-permute-start.9 = (f32[128,256]{1,0:T(8,128)S(1)}, f32[128,256]{1,0:T(8,128)S(1)}, u32[]{:S(2)}, u32[]{:S(2)}) collective-permute-start(f32[128,256]{1,0:T(8,128)S(1)} %maximum_select_fusion.2), channel_id=1, source_target_pairs={{0,32},{8,40},{16,48},{24,56},{32,0},{40,8},{48,16},{56,24},{64,96... | collective-permute-start | bytes 393224 | tf_op jit(solution)/shard_map/ppermute | solution.py:91
  82.3 9.8 %collective-permute-start.10 = (f32[256,256]{1,0:T(8,128)S(1)}, f32[256,256]{1,0:T(8,128)S(1)}, u32[]{:S(2)}, u32[]{:S(2)}) collective-permute-start(f32[256,256]{1,0:T(8,128)S(1)} %maximum_select_fusion.1), channel_id=1, source_target_pairs={{0,64},{8,72},{16,80},{24,88},{32,96},{40,104},{48,112},{56,120},{... | collective-permute-start | bytes 786440 | tf_op jit(solution)/shard_map/ppermute | solution.py:91
  85.1 7.0 %copy-start.2 = (f32[5,16,512]{2,1,0:T(8,128)}, f32[5,16,512]{2,1,0:T(8,128)S(1)}, u32[]{:S(2)}) copy-start(f32[5,16,512]{2,1,0:T(8,128)S(1)} %fusion.36) | copy-start | bytes 491524

commit v3 on v2

--- a/solution.py
+++ b/solution.py
@@ -81,6 +81,39 @@
             transcendentals=0,
         ),
     )(rows, delays)
+
+
+def trace_kernel(first, samples, tr_ref, delays_ref, acc_ref, out_ref):
+    pairs = delays_ref.shape[0]
+
+    def body(k, acc):
+        d = delays_ref[k]
+        add = jnp.zeros_like(acc)
+        for t in range(samples - 1, -1, -1):
+            add = jnp.where(d == first + t, tr_ref[samples * k + t], add)
+        return acc + add
+
+    out_ref[...] = lax.fori_loop(0, pairs, body, acc_ref[...], unroll=8)
+
+
+def add_traces(first, tr, delays, acc):
+    pairs, pix_rows, pix_cols = delays.shape
+    samples = tr.shape[1]
+    return pl.pallas_call(
+        functools.partial(trace_kernel, first, samples),
+        out_shape=jax.ShapeDtypeStruct((pix_rows, pix_cols), jnp.float32),
+        in_specs=[
+            pl.BlockSpec(memory_space=pltpu.SMEM),
+            pl.BlockSpec(memory_space=pltpu.VMEM),
+            pl.BlockSpec(memory_space=pltpu.VMEM),
+        ],
+        out_specs=pl.BlockSpec(memory_space=pltpu.VMEM),
+        cost_estimate=pl.CostEstimate(
+            flops=7 * pairs * pix_rows * pix_cols,
+            bytes_accessed=4 * (delays.size + 2 * pix_rows * pix_cols),
+            transcendentals=0,
+        ),
+    )(tr.reshape(-1), delays, acc)
 
 
 def gather_doubling(block, axis):
@@ -131,11 +164,17 @@
         moduli_map = jnp.stack(moduli_map)
     next_state = jnp.stack(fields)[None]
     recorded = jnp.stack(samples, axis=1)[None]
-    local_waves = jnp.concatenate([history[0], recorded[0]], axis=1)
-    waveforms = gather_waves(local_waves)
-    sample_count = waveforms.shape[1]
-    chosen = waveforms[receivers[0]].reshape(2 * receivers.shape[1], sample_count // 2)
+    hist = history[0]
+    hist_count = hist.shape[1]
+    sample_count = hist_count + STEPS
+    padded_hist = jnp.concatenate(
+        [hist, jnp.zeros((hist.shape[0], sample_count - hist_count), jnp.float32)], axis=1
+    )
+    all_hist = gather_waves(padded_hist)
+    all_traces = gather_waves(recorded[0])
+    chosen = all_hist[receivers[0]].reshape(2 * receivers.shape[1], sample_count // 2)
     partial_value = image(chosen, delays[0])
+    partial_value = add_traces(hist_count, all_traces[receivers[0]], delays[0], partial_value)
     summed = lax.psum(partial_value, "act")
     damage_map = summed * summed / (receivers.shape[1] * lax.axis_size("act"))
     return (next_state, recorded, damage_map)

time: 114 us -> 146 us (1.28)
  the two profiles are of different devices: /device:TPU:506 before, /device:TPU:1 now
where the time goes in v3:
time: 146 us; the launch traced here: 145 us
  starting transfers between devices  73.7 us (50%)
  blocking collectives  27.6 us (19%)
  waiting for transfers between devices  23.8 us (16%)
  local copies, waits for them, and re-layouts  6.58 us (5%)
  Pallas kernels  6.48 us (4%)
  other arithmetic  5.83 us (4%)
    ppermute x14, starting transfers between devices, gather_doubling(): other = lax.ppermute(block, axis, [(i, i ^ stride) for i in range(count)])  55.2 us
    psum x1, blocking collectives, per_device(): summed = lax.psum(partial_value, 'act')  27.6 us
    ppermute x14, waiting for transfers between devices, gather_doubling(): other = lax.ppermute(block, axis, [(i, i ^ stride) for i in range(count)])  20.5 us
    ppermute x1, starting transfers between devices, exchange(): lax.ppermute(cells[:, :, :halo], 'hoop', [((j + 1) % nh, j) for j in rang...  10.6 us
    ppermute x1, starting transfers between devices, exchange(): lax.ppermute(cells[:, -halo:, :], 'axial', [(i, i + 1) for i in range(na...  4.66 us
    pallas_call x1, Pallas kernels, image(): pl.pallas_call(image_kernel, out_shape=jax.ShapeDtypeStruct((pix_rows, pi...  4.28 us
    ppermute x1, waiting for transfers between devices, exchange(): lax.ppermute(cells[:, :, -halo:], 'hoop', [(j, (j + 1) % nh) for j in ran...  3.35 us
  transfers between devices with their start and end apart: 18, of which 10 were waited for; matrix products, arithmetic and copies ran while one was open for 5% of the time, Pallas kernels for 0%

profile of v3, /device:TPU:1, one launch (start us, length us, event | category | flops | bytes accessed | tf_op | source)
XLA Modules:
  0.0 145.4 jit_solution(1496203734101000122)
XLA Ops:
  0.6 0.8 convert_bitcast_fusion
  1.4 0.9 fusion
  2.3 1.3 collective-permute-start.1
  3.6 4.7 %collective-permute-start = (f32[6,6,512]{2,1,0:T(8,128)S(1)}, f32[6,6,512]{2,1,0:T(8,128)S(1)}, u32[]{:S(2)}, u32[]{:S(2)}) collective-permute-start(f32[6,6,512]{2,1,0:T(8,128)S(1)} %get-tuple-element.40), channel_id=1, source_target_pairs={{0,8},{8,16},{16,24},{24,32},{32,40},{40,48},{48,56},{56,64},{64,7... | collective-permute-start | bytes 221192 | tf_op jit(solution)/shard_map/ppermute | solution.py:17
  8.4 3.7 %collective-permute-start.11 = (f32[4,256]{1,0:T(4,128)S(1)}, f32[4,256]{1,0:T(4,128)S(1)}, u32[]{:S(2)}, u32[]{:S(2)}) collective-permute-start(f32[4,256]{1,0:T(4,128)S(1)} %concatenate.113), channel_id=1, source_target_pairs={{0,1},{1,0},{2,3},{3,2},{4,5},{5,4},{6,7},{7,6},{8,9},{9,8},{10,11... | collective-permute-start | bytes 12296 | tf_op jit(solution)/shard_map/ppermute | solution.py:124
  12.1 0.6 copy-done.5
  12.8 0.3 collective-permute-done.11
  13.1 4.9 %collective-permute-start.12 = (f32[8,256]{1,0:T(8,128)S(1)}, f32[8,256]{1,0:T(8,128)S(1)}, u32[]{:S(2)}, u32[]{:S(2)}) collective-permute-start(f32[8,256]{1,0:T(8,128)S(1)} %maximum_select_fusion.6), channel_id=1, source_target_pairs={{0,2},{1,3},{2,0},{3,1},{4,6},{5,7},{6,4},{7,5},{8,10},{9,11},{10,... | collective-permute-start | bytes 24584 | tf_op jit(solution)/shard_map/ppermute | solution.py:124
  18.0 1.0 collective-permute-done.12
  19.0 8.8 %collective-permute-start.13 = (f32[16,256]{1,0:T(8,128)S(1)}, f32[16,256]{1,0:T(8,128)S(1)}, u32[]{:S(2)}, u32[]{:S(2)}) collective-permute-start(f32[16,256]{1,0:T(8,128)S(1)} %maximum_select_fusion.5), channel_id=1, source_target_pairs={{0,4},{1,5},{2,6},{3,7},{4,0},{5,1},{6,2},{7,3},{8,12},{9,13},{10,... | collective-permute-start | bytes 49160 | tf_op jit(solution)/shard_map/ppermute | solution.py:124
  27.9 1.0 collective-permute-done.13
  28.9 3.2 %collective-permute-start.14 = (f32[32,256]{1,0:T(8,128)S(1)}, f32[32,256]{1,0:T(8,128)S(1)}, u32[]{:S(2)}, u32[]{:S(2)}) collective-permute-start(f32[32,256]{1,0:T(8,128)S(1)} %maximum_select_fusion.4), channel_id=1, source_target_pairs={{0,8},{8,0},{16,24},{24,16},{32,40},{40,32},{48,56},{56,48},{64,72... | collective-permute-start | bytes 98312 | tf_op jit(solution)/shard_map/ppermute | solution.py:124
  32.2 0.1 pad_maximum_fusion.4
  32.3 10.6 %collective-permute-start.3 = (f32[6,28,6]{2,1,0:T(8,128)S(1)}, f32[6,28,6]{2,1,0:T(8,128)S(1)}, u32[]{:S(2)}, u32[]{:S(2)}) collective-permute-start(f32[6,28,6]{2,1,0:T(8,128)S(1)} %get-tuple-element.35), channel_id=1, source_target_pairs={{1,0},{2,1},{3,2},{4,3},{5,4},{6,5},{7,6},{0,7},{9,8},{10,9},{11,1... | collective-permute-start | bytes 12104 | tf_op jit(solution)/shard_map/ppermute | solution.py:21
  42.9 1.9 %collective-permute-start.2 = (f32[6,28,6]{2,1,0:T(8,128)S(1)}, f32[6,28,6]{2,1,0:T(8,128)S(1)}, u32[]{:S(2)}, u32[]{:S(2)}) collective-permute-start(f32[6,28,6]{2,1,0:T(8,128)S(1)} %get-tuple-element.34), channel_id=1, source_target_pairs={{0,1},{1,2},{2,3},{3,4},{4,5},{5,6},{6,7},{7,0},{8,9},{9,10},{10,1... | collective-permute-start | bytes 12104 | tf_op jit(solution)/shard_map/ppermute | solution.py:20
  44.8 6.6 %collective-permute-start.15 = (f32[64,256]{1,0:T(8,128)S(1)}, f32[64,256]{1,0:T(8,128)S(1)}, u32[]{:S(2)}, u32[]{:S(2)}) collective-permute-start(f32[64,256]{1,0:T(8,128)S(1)} %maximum_select_fusion.3), channel_id=1, source_target_pairs={{0,16},{8,24},{16,0},{24,8},{32,48},{40,56},{48,32},{56,40},{64,80... | collective-permute-start | bytes 196616 | tf_op jit(solution)/shard_map/ppermute | solution.py:124
  51.5 3.4 %collective-permute-done.2 = f32[6,28,6]{2,1,0:T(8,128)S(1)} collective-permute-done((f32[6,28,6]{2,1,0:T(8,128)S(1)}, f32[6,28,6]{2,1,0:T(8,128)S(1)}, u32[]{:S(2)}, u32[]{:S(2)}) %collective-permute-start.2) | collective-permute-done | bytes 4064 | tf_op jit(solution)/shard_map/ppermute | solution.py:20
  54.8 0.3 pad_maximum_fusion
  55.1 0.1 compare_bitcast_fusion.7
  55.3 0.6 select_select_fusion
  56.0 0.3 fusion.6
  56.3 0.2 fusion.28
  56.4 0.2 fusion.30
  56.6 0.2 fusion.25
  56.9 0.2 fusion.16
  57.1 0.2 fusion.10
  57.3 0.1 fusion.31
  57.4 0.2 fusion.9
  57.6 0.1 add_bitcast_fusion
  57.8 0.6 gather_fusion.2
  58.4 0.6 gather_fusion.1
  59.1 0.6 gather_fusion
  59.7 1.9 %collective-permute-start.4 = (f32[4,3]{0,1:T(4,128)S(1)}, f32[4,3]{0,1:T(4,128)S(1)}, u32[]{:S(2)}, u32[]{:S(2)}) collective-permute-start(f32[4,3]{0,1:T(4,128)S(1)} %get-tuple-element.59), channel_id=1, source_target_pairs={{0,1},{1,0},{2,3},{3,2},{4,5},{5,4},{6,7},{7,6},{8,9},{9,8},{10,11... | collective-permute-start | bytes 152 | tf_op jit(solution)/shard_map/ppermute | solution.py:124
  61.6 2.4 %collective-permute-done.4 = f32[4,3]{0,1:T(4,128)S(1)} collective-permute-done((f32[4,3]{0,1:T(4,128)S(1)}, f32[4,3]{0,1:T(4,128)S(1)}, u32[]{:S(2)}, u32[]{:S(2)}) %collective-permute-start.4) | collective-permute-done | bytes 80 | tf_op jit(solution)/shard_map/ppermute | solution.py:124
  64.0 0.1 maximum_select_fusion.8
  64.1 1.9 %collective-permute-start.5 = (f32[8,3]{0,1:T(4,128)S(1)}, f32[8,3]{0,1:T(4,128)S(1)}, u32[]{:S(2)}, u32[]{:S(2)}) collective-permute-start(f32[8,3]{0,1:T(4,128)S(1)} %maximum_select_fusion.8), channel_id=1, source_target_pairs={{0,2},{1,3},{2,0},{3,1},{4,6},{5,7},{6,4},{7,5},{8,10},{9,11},{10,... | collective-permute-start | bytes 296 | tf_op jit(solution)/shard_map/ppermute | solution.py:124
  66.0 0.1 bitcast_dynamic-update-slice_fusion.3
  66.1 3.2 %collective-permute-done.5 = f32[8,3]{0,1:T(4,128)S(1)} collective-permute-done((f32[8,3]{0,1:T(4,128)S(1)}, f32[8,3]{0,1:T(4,128)S(1)}, u32[]{:S(2)}, u32[]{:S(2)}) %collective-permute-start.5) | collective-permute-done | bytes 128 | tf_op jit(solution)/shard_map/ppermute | solution.py:124
  69.3 0.1 maximum_select_fusion.9
  69.4 3.4 %collective-permute-start.6 = (f32[16,3]{0,1:T(4,128)S(1)}, f32[16,3]{0,1:T(4,128)S(1)}, u32[]{:S(2)}, u32[]{:S(2)}) collective-permute-start(f32[16,3]{0,1:T(4,128)S(1)} %maximum_select_fusion.9), channel_id=1, source_target_pairs={{0,4},{1,5},{2,6},{3,7},{4,0},{5,1},{6,2},{7,3},{8,12},{9,13},{10,... | collective-permute-start | bytes 584 | tf_op jit(solution)/shard_map/ppermute | solution.py:124
  72.8 0.1 bitcast_dynamic-update-slice_fusion.2
  72.9 4.8 %collective-permute-done.6 = f32[16,3]{0,1:T(4,128)S(1)} collective-permute-done((f32[16,3]{0,1:T(4,128)S(1)}, f32[16,3]{0,1:T(4,128)S(1)}, u32[]{:S(2)}, u32[]{:S(2)}) %collective-permute-start.6) | collective-permute-done | bytes 224 | tf_op jit(solution)/shard_map/ppermute | solution.py:124
  77.6 0.1 maximum_select_fusion.10
  77.7 2.1 %collective-permute-start.7 = (f32[32,3]{0,1:T(4,128)S(1)}, f32[32,3]{0,1:T(4,128)S(1)}, u32[]{:S(2)}, u32[]{:S(2)}) collective-permute-start(f32[32,3]{0,1:T(4,128)S(1)} %maximum_select_fusion.10), channel_id=1, source_target_pairs={{0,8},{8,0},{16,24},{24,16},{32,40},{40,32},{48,56},{56,48},{64,72... | collective-permute-start | bytes 1160 | tf_op jit(solution)/shard_map/ppermute | solution.py:124
  79.8 2.2 %collective-permute-done.7 = f32[32,3]{0,1:T(4,128)S(1)} collective-permute-done((f32[32,3]{0,1:T(4,128)S(1)}, f32[32,3]{0,1:T(4,128)S(1)}, u32[]{:S(2)}, u32[]{:S(2)}) %collective-permute-start.7) | collective-permute-done | bytes 416 | tf_op jit(solution)/shard_map/ppermute | solution.py:124
  82.1 6.6 %collective-permute-start.8 = (f32[64,3]{0,1:T(4,128)S(1)}, f32[64,3]{0,1:T(4,128)S(1)}, u32[]{:S(2)}, u32[]{:S(2)}) collective-permute-start(f32[64,3]{0,1:T(4,128)S(1)} %maximum_select_fusion.11), channel_id=1, source_target_pairs={{0,16},{8,24},{16,0},{24,8},{32,48},{40,56},{48,32},{56,40},{64,80... | collective-permute-start | bytes 2312 | tf_op jit(solution)/shard_map/ppermute | solution.py:124
  88.8 0.9 collective-permute-done.8
  89.8 3.1 %collective-permute-start.9 = (f32[128,3]{0,1:T(4,128)S(1)}, f32[128,3]{0,1:T(4,128)S(1)}, u32[]{:S(2)}, u32[]{:S(2)}) collective-permute-start(f32[128,3]{0,1:T(4,128)S(1)} %maximum_select_fusion.12), channel_id=1, source_target_pairs={{0,32},{8,40},{16,48},{24,56},{32,0},{40,8},{48,16},{56,24},{64,96... | collective-permute-start | bytes 4616 | tf_op jit(solution)/shard_map/ppermute | solution.py:124
  92.9 2.2 %collective-permute-start.16 = (f32[128,256]{1,0:T(8,128)S(1)}, f32[128,256]{1,0:T(8,128)S(1)}, u32[]{:S(2)}, u32[]{:S(2)}) collective-permute-start(f32[128,256]{1,0:T(8,128)S(1)} %maximum_select_fusion.2), channel_id=1, source_target_pairs={{0,32},{8,40},{16,48},{24,56},{32,0},{40,8},{48,16},{56,24},{64,96... | collective-permute-start | bytes 393224 | tf_op jit(solution)/shard_map/ppermute | solution.py:124
  95.1 0.1 fusion.36
  95.2 0.6 copy.21
  95.9 4.6 %collective-permute-start.10 = (f32[256,3]{0,1:T(4,128)S(1)}, f32[256,3]{0,1:T(4,128)S(1)}, u32[]{:S(2)}, u32[]{:S(2)}) collective-permute-start(f32[256,3]{0,1:T(4,128)S(1)} %maximum_select_fusion.7), channel_id=1, source_target_pairs={{0,64},{8,72},{16,80},{24,88},{32,96},{40,104},{48,112},{56,120},{... | collective-permute-start | bytes 9224 | tf_op jit(solution)/shard_map/ppermute | solution.py:124
  100.6 2.1 %collective-permute-start.17 = (f32[256,256]{1,0:T(8,128)S(1)}, f32[256,256]{1,0:T(8,128)S(1)}, u32[]{:S(2)}, u32[]{:S(2)}) collective-permute-start(f32[256,256]{1,0:T(8,128)S(1)} %maximum_select_fusion.1), channel_id=1, source_target_pairs={{0,64},{8,72},{16,80},{24,88},{32,96},{40,104},{48,112},{56,120},{... | collective-permute-start | bytes 786440 | tf_op jit(solution)/shard_map/ppermute | solution.py:124
  102.7 0.1 copy.19
  102.9 0.1 copy.20
  103.1 0.6 gather_fusion.3
  103.7 0.8 reshape.68.tr_ref
  104.5 4.7 %collective-permute-done.17 = f32[256,256]{1,0:T(8,128)S(1)} collective-permute-done((f32[256,256]{1,0:T(8,128)S(1)}, f32[256,256]{1,0:T(8,128)S(1)}, u32[]{:S(2)}, u32[]{:S(2)}) %collective-permute-start.17) | collective-permute-done | bytes 262176 | tf_op jit(solution)/shard_map/ppermute | solution.py:124
  109.3 0.8 gather_fusion.4
  110.0 0.7 reshape.69.rows_ref
  110.7 4.3 %shard_map.94.acc_ref = f32[16,128]{1,0:T(8,128)} custom-call(f32[256,128]{1,0:T(8,128)} %reshape.69.rows_ref, s32[128,16,128]{2,1,0:T(8,128)} %bitcast.93), custom_call_target="tpu_custom_call" | custom-call | flops 2097152 | bytes 1187840 | tf_op jit(solution)/shard_map/pallas_call | solution.py:73
  115.0 2.2 %shard_map.95 = f32[16,128]{1,0:T(8,128)} custom-call(f32[384]{0:T(512)} %reshape.68.tr_ref, s32[128,16,128]{2,1,0:T(8,128)} %bitcast.94, f32[16,128]{1,0:T(8,128)} %shard_map.94.acc_ref), custom_call_target="tpu_custom_call" | custom-call | flops 1835008 | bytes 1064960 | tf_op jit(solution)/shard_map/pallas_call | solution.py:102
  117.2 27.6 %psum.7 = f32[16,128]{1,0:T(8,128)S(1)} all-reduce(f32[16,128]{1,0:T(8,128)} %shard_map.95), channel_id=1, replica_groups=mesh['act'=4,'axial'=16,'hoop'=8] {'act'}, use_global_device_ids=true, to_apply=%region_0.1 | all-reduce | flops 2048 | bytes 16384 | tf_op jit(solution)/shard_map/psum | solution.py:178
  144.8 0.6 multiply_multiply_fusion
  (45 shorter events, 0.5 us)
Async XLA Ops:
  2.3 6.0 %copy-start.2 = (f32[1,4,253]{2,1,0:T(4,128)S(1)}, f32[1,4,253]{2,1,0:T(4,128)}, u32[]{:S(2)}) copy-start(f32[1,4,253]{2,1,0:T(4,128)} %param.11) | copy-start | bytes 12148
  2.3 29.8 %collective-permute-start.1 = (f32[6,6,512]{2,1,0:T(8,128)S(1)}, f32[6,6,512]{2,1,0:T(8,128)S(1)}, u32[]{:S(2)}, u32[]{:S(2)}) collective-permute-start(f32[6,6,512]{2,1,0:T(8,128)S(1)} %get-tuple-element.41), channel_id=1, source_target_pairs={{8,0},{16,8},{24,16},{32,24},{40,32},{48,40},{56,48},{64,56},{72,6... | collective-permute-start | bytes 221192 | tf_op jit(solution)/shard_map/ppermute | solution.py:18
  3.6 28.5 %collective-permute-start = (f32[6,6,512]{2,1,0:T(8,128)S(1)}, f32[6,6,512]{2,1,0:T(8,128)S(1)}, u32[]{:S(2)}, u32[]{:S(2)}) collective-permute-start(f32[6,6,512]{2,1,0:T(8,128)S(1)} %get-tuple-element.40), channel_id=1, source_target_pairs={{0,8},{8,16},{16,24},{24,32},{32,40},{40,48},{48,56},{56,64},{64,7... | collective-permute-start | bytes 221192 | tf_op jit(solution)/shard_map/ppermute | solution.py:17
  8.3 3.8 %copy-start.3 = (f32[8,6]{1,0:T(8,128)S(1)}, f32[8,6]{1,0:T(8,128)}, u32[]{:S(2)}) copy-start(f32[8,6]{1,0:T(8,128)} %param.9) | copy-start | bytes 580
  8.4 3.8 %copy-start.4 = (s32[4]{0:T(128)S(1)}, s32[4]{0:T(128)}, u32[]{:S(2)}) copy-start(s32[4]{0:T(128)} %param.10) | copy-start | bytes 52
  8.4 4.7 %collective-permute-start.11 = (f32[4,256]{1,0:T(4,128)S(1)}, f32[4,256]{1,0:T(4,128)S(1)}, u32[]{:S(2)}, u32[]{:S(2)}) collective-permute-start(f32[4,256]{1,0:T(4,128)S(1)} %concatenate.113), channel_id=1, source_target_pairs={{0,1},{1,0},{2,3},{3,2},{4,5},{5,4},{6,7},{7,6},{8,9},{9,8},{10,11... | collective-permute-start | bytes 12296 | tf_op jit(solution)/shard_map/ppermute | solution.py:124
  12.1 0.7 copy-start.5
  13.1 5.9 %collective-permute-start.12 = (f32[8,256]{1,0:T(8,128)S(1)}, f32[8,256]{1,0:T(8,128)S(1)}, u32[]{:S(2)}, u32[]{:S(2)}) collective-permute-start(f32[8,256]{1,0:T(8,128)S(1)} %maximum_select_fusion.6), channel_id=1, source_target_pairs={{0,2},{1,3},{2,0},{3,1},{4,6},{5,7},{6,4},{7,5},{8,10},{9,11},{10,... | collective-permute-start | bytes 24584 | tf_op jit(solution)/shard_map/ppermute | solution.py:124
  18.0 14.2 %copy-start = (f32[1,5,16,512]{3,2,1,0:T(8,128)S(1)}, f32[1,5,16,512]{3,2,1,0:T(8,128)}, u32[]{:S(2)}) copy-start(f32[1,5,16,512]{3,2,1,0:T(8,128)} %param.7) | copy-start | bytes 491524
  19.0 9.9 %collective-permute-start.13 = (f32[16,256]{1,0:T(8,128)S(1)}, f32[16,256]{1,0:T(8,128)S(1)}, u32[]{:S(2)}, u32[]{:S(2)}) collective-permute-start(f32[16,256]{1,0:T(8,128)S(1)} %maximum_select_fusion.5), channel_id=1, source_target_pairs={{0,4},{1,5},{2,6},{3,7},{4,0},{5,1},{6,2},{7,3},{8,12},{9,13},{10,... | collective-permute-start | bytes 49160 | tf_op jit(solution)/shard_map/ppermute | solution.py:124
  28.9 15.9 %collective-permute-start.14 = (f32[32,256]{1,0:T(8,128)S(1)}, f32[32,256]{1,0:T(8,128)S(1)}, u32[]{:S(2)}, u32[]{:S(2)}) collective-permute-start(f32[32,256]{1,0:T(8,128)S(1)} %maximum_select_fusion.4), channel_id=1, source_target_pairs={{0,8},{8,0},{16,24},{24,16},{32,40},{40,32},{48,56},{56,48},{64,72... | collective-permute-start | bytes 98312 | tf_op jit(solution)/shard_map/ppermute | solution.py:124
  32.3 19.2 %collective-permute-start.3 = (f32[6,28,6]{2,1,0:T(8,128)S(1)}, f32[6,28,6]{2,1,0:T(8,128)S(1)}, u32[]{:S(2)}, u32[]{:S(2)}) collective-permute-start(f32[6,28,6]{2,1,0:T(8,128)S(1)} %get-tuple-element.35), channel_id=1, source_target_pairs={{1,0},{2,1},{3,2},{4,3},{5,4},{6,5},{7,6},{0,7},{9,8},{10,9},{11,1... | collective-permute-start | bytes 12104 | tf_op jit(solution)/shard_map/ppermute | solution.py:21
  42.9 12.0 %collective-permute-start.2 = (f32[6,28,6]{2,1,0:T(8,128)S(1)}, f32[6,28,6]{2,1,0:T(8,128)S(1)}, u32[]{:S(2)}, u32[]{:S(2)}) collective-permute-start(f32[6,28,6]{2,1,0:T(8,128)S(1)} %get-tuple-element.34), channel_id=1, source_target_pairs={{0,1},{1,2},{2,3},{3,4},{4,5},{5,6},{6,7},{7,0},{8,9},{9,10},{10,1... | collective-permute-start | bytes 12104 | tf_op jit(solution)/shard_map/ppermute | solution.py:20
  44.8 48.1 %collective-permute-start.15 = (f32[64,256]{1,0:T(8,128)S(1)}, f32[64,256]{1,0:T(8,128)S(1)}, u32[]{:S(2)}, u32[]{:S(2)}) collective-permute-start(f32[64,256]{1,0:T(8,128)S(1)} %maximum_select_fusion.3), channel_id=1, source_target_pairs={{0,16},{8,24},{16,0},{24,8},{32,48},{40,56},{48,32},{56,40},{64,80... | collective-permute-start | bytes 196616 | tf_op jit(solution)/shard_map/ppermute | solution.py:124
  59.7 4.3 %collective-permute-start.4 = (f32[4,3]{0,1:T(4,128)S(1)}, f32[4,3]{0,1:T(4,128)S(1)}, u32[]{:S(2)}, u32[]{:S(2)}) collective-permute-start(f32[4,3]{0,1:T(4,128)S(1)} %get-tuple-element.59), channel_id=1, source_target_pairs={{0,1},{1,0},{2,3},{3,2},{4,5},{5,4},{6,7},{7,6},{8,9},{9,8},{10,11... | collective-permute-start | bytes 152 | tf_op jit(solution)/shard_map/ppermute | solution.py:124
  64.1 5.2 %collective-permute-start.5 = (f32[8,3]{0,1:T(4,128)S(1)}, f32[8,3]{0,1:T(4,128)S(1)}, u32[]{:S(2)}, u32[]{:S(2)}) collective-permute-start(f32[8,3]{0,1:T(4,128)S(1)} %maximum_select_fusion.8), channel_id=1, source_target_pairs={{0,2},{1,3},{2,0},{3,1},{4,6},{5,7},{6,4},{7,5},{8,10},{9,11},{10,... | collective-permute-start | bytes 296 | tf_op jit(solution)/shard_map/ppermute | solution.py:124
  69.4 8.2 %collective-permute-start.6 = (f32[16,3]{0,1:T(4,128)S(1)}, f32[16,3]{0,1:T(4,128)S(1)}, u32[]{:S(2)}, u32[]{:S(2)}) collective-permute-start(f32[16,3]{0,1:T(4,128)S(1)} %maximum_select_fusion.9), channel_id=1, source_target_pairs={{0,4},{1,5},{2,6},{3,7},{4,0},{5,1},{6,2},{7,3},{8,12},{9,13},{10,... | collective-permute-start | bytes 584 | tf_op jit(solution)/shard_map/ppermute | solution.py:124
  77.7 4.3 %collective-permute-start.7 = (f32[32,3]{0,1:T(4,128)S(1)}, f32[32,3]{0,1:T(4,128)S(1)}, u32[]{:S(2)}, u32[]{:S(2)}) collective-permute-start(f32[32,3]{0,1:T(4,128)S(1)} %maximum_select_fusion.10), channel_id=1, source_target_pairs={{0,8},{8,0},{16,24},{24,16},{32,40},{40,32},{48,56},{56,48},{64,72... | collective-permute-start | bytes 1160 | tf_op jit(solution)/shard_map/ppermute | solution.py:124
  82.1 7.6 %collective-permute-start.8 = (f32[64,3]{0,1:T(4,128)S(1)}, f32[64,3]{0,1:T(4,128)S(1)}, u32[]{:S(2)}, u32[]{:S(2)}) collective-permute-start(f32[64,3]{0,1:T(4,128)S(1)} %maximum_select_fusion.11), channel_id=1, source_target_pairs={{0,16},{8,24},{16,0},{24,8},{32,48},{40,56},{48,32},{56,40},{64,80... | collective-permute-start | bytes 2312 | tf_op jit(solution)/shard_map/ppermute | solution.py:124
  89.8 6.1 %collective-permute-start.9 = (f32[128,3]{0,1:T(4,128)S(1)}, f32[128,3]{0,1:T(4,128)S(1)}, u32[]{:S(2)}, u32[]{:S(2)}) collective-permute-start(f32[128,3]{0,1:T(4,128)S(1)} %maximum_select_fusion.12), channel_id=1, source_target_pairs={{0,32},{8,40},{16,48},{24,56},{32,0},{40,8},{48,16},{56,24},{64,96... | collective-permute-start | bytes 4616 | tf_op jit(solution)/shard_map/ppermute | solution.py:124
  92.9 7.6 %collective-permute-start.16 = (f32[128,256]{1,0:T(8,128)S(1)}, f32[128,256]{1,0:T(8,128)S(1)}, u32[]{:S(2)}, u32[]{:S(2)}) collective-permute-start(f32[128,256]{1,0:T(8,128)S(1)} %maximum_select_fusion.2), channel_id=1, source_target_pairs={{0,32},{8,40},{16,48},{24,56},{32,0},{40,8},{48,16},{56,24},{64,96... | collective-permute-start | bytes 393224 | tf_op jit(solution)/shard_map/ppermute | solution.py:124
  95.2 5.3 %copy-start.1 = (f32[5,16,512]{2,1,0:T(8,128)}, f32[5,16,512]{2,1,0:T(8,128)S(1)}, u32[]{:S(2)}) copy-start(f32[5,16,512]{2,1,0:T(8,128)S(1)} %fusion.36) | copy-start | bytes 491524
  95.9 6.8 %collective-permute-start.10 = (f32[256,3]{0,1:T(4,128)S(1)}, f32[256,3]{0,1:T(4,128)S(1)}, u32[]{:S(2)}, u32[]{:S(2)}) collective-permute-start(f32[256,3]{0,1:T(4,128)S(1)} %maximum_select_fusion.7), channel_id=1, source_target_pairs={{0,64},{8,72},{16,80},{24,88},{32,96},{40,104},{48,112},{56,120},{... | collective-permute-start | bytes 9224 | tf_op jit(solution)/shard_map/ppermute | solution.py:124
  100.6 8.6 %collective-permute-start.17 = (f32[256,256]{1,0:T(8,128)S(1)}, f32[256,256]{1,0:T(8,128)S(1)}, u32[]{:S(2)}, u32[]{:S(2)}) collective-permute-start(f32[256,256]{1,0:T(8,128)S(1)} %maximum_select_fusion.1), channel_id=1, source_target_pairs={{0,64},{8,72},{16,80},{24,88},{32,96},{40,104},{48,112},{56,120},{... | collective-permute-start | bytes 786440 | tf_op jit(solution)/shard_map/ppermute | solution.py:124

commit v4 on v2

--- a/solution.py
+++ b/solution.py
@@ -101,6 +101,17 @@
     return gather_doubling(gather_doubling(local_waves, "hoop"), "axial")
 
 
+def act_sum(partial_value):
+    count = lax.axis_size("act")
+    stride = 1
+    while stride < count:
+        partial_value = partial_value + lax.ppermute(
+            partial_value, "act", [(i, i ^ stride) for i in range(count)]
+        )
+        stride *= 2
+    return partial_value
+
+
 def per_device(wave_state, layup_zone, moduli, sensors, history, receivers, delays):
     rows, cols = layup_zone.shape
     na = lax.axis_size("axial")
@@ -136,7 +147,7 @@
     sample_count = waveforms.shape[1]
     chosen = waveforms[receivers[0]].reshape(2 * receivers.shape[1], sample_count // 2)
     partial_value = image(chosen, delays[0])
-    summed = lax.psum(partial_value, "act")
+    summed = act_sum(partial_value)
     damage_map = summed * summed / (receivers.shape[1] * lax.axis_size("act"))
     return (next_state, recorded, damage_map)
 

time: 114 us -> 117 us (1.026)
  blocking collectives: 14.7 us -> 0 us
  waiting for transfers between devices: 53 us -> 66.6 us
  starting transfers between devices: 28.7 us -> 32.6 us
    psum x1 -> x0, blocking collectives: 14.7 us -> none  [per_device(): summed = lax.psum(partial_value, 'act')]
    ppermute x0 -> x2, waiting for transfers between devices: none -> 13 us  [act_sum(): lax.ppermute(partial_value, 'act', [(i, i ^ stride) for i in range(count)])]
    ppermute x0 -> x2, starting transfers between devices: none -> 3.95 us  [act_sum(): lax.ppermute(partial_value, 'act', [(i, i ^ stride) for i in range(count)])]
  transfers between devices with their start and end apart: 11 -> 13, of which waited for: 10 -> 12; matrix products, arithmetic and copies ran while one was open for 1% -> 1% of each run, Pallas kernels for 0% -> 0%
where the time goes in v4:
time: 117 us; the launch traced here: 116 us
  waiting for transfers between devices  66.6 us (57%)
  starting transfers between devices  32.6 us (28%)
  local copies, waits for them, and re-layouts  5.7 us (5%)
  other arithmetic  5.62 us (5%)
  Pallas kernels  4.28 us (4%)
  between operations  1.18 us (1%)
    ppermute x7, waiting for transfers between devices, gather_doubling(): other = lax.ppermute(block, axis, [(i, i ^ stride) for i in range(count)])  37.4 us
    ppermute x7, starting transfers between devices, gather_doubling(): other = lax.ppermute(block, axis, [(i, i ^ stride) for i in range(count)])  14.1 us
    ppermute x2, waiting for transfers between devices, act_sum(): lax.ppermute(partial_value, 'act', [(i, i ^ stride) for i in range(count)])  13 us
    ppermute x1, waiting for transfers between devices, exchange(): lax.ppermute(cells[:, :, :halo], 'hoop', [((j + 1) % nh, j) for j in rang...  10.6 us
    ppermute x1, starting transfers between devices, exchange(): lax.ppermute(cells[:, :, -halo:], 'hoop', [(j, (j + 1) % nh) for j in ran...  6.79 us
    ppermute x1, waiting for transfers between devices, exchange(): lax.ppermute(cells[:, :halo, :], 'axial', [(i + 1, i) for i in range(na -...  5.11 us
    pallas_call x1, Pallas kernels, image(): pl.pallas_call(image_kernel, out_shape=jax.ShapeDtypeStruct((pix_rows, pi...  4.28 us
    ppermute x2, starting transfers between devices, act_sum(): lax.ppermute(partial_value, 'act', [(i, i ^ stride) for i in range(count)])  3.95 us
  transfers between devices with their start and end apart: 13, of which 12 were waited for; matrix products, arithmetic and copies ran while one was open for 1% of the time, Pallas kernels for 0%

profile of v4, /device:TPU:506, one launch (start us, length us, event | category | flops | bytes accessed | tf_op | source)
XLA Modules:
  0.0 116.1 jit_solution(8881885863053456079)
XLA Ops:
  0.6 0.8 convert_bitcast_fusion
  1.4 1.0 fusion
  2.4 0.0 copy-start.4
  2.4 3.1 %collective-permute-start = (f32[6,6,512]{2,1,0:T(8,128)S(1)}, f32[6,6,512]{2,1,0:T(8,128)S(1)}, u32[]{:S(2)}, u32[]{:S(2)}) collective-permute-start(f32[6,6,512]{2,1,0:T(8,128)S(1)} %get-tuple-element.37), channel_id=1, source_target_pairs={{0,8},{8,16},{16,24},{24,32},{32,40},{40,48},{48,56},{56,64},{64,7... | collective-permute-start | bytes 221192 | tf_op jit(solution)/shard_map/ppermute | solution.py:17
  5.5 2.8 %collective-permute-start.1 = (f32[6,6,512]{2,1,0:T(8,128)S(1)}, f32[6,6,512]{2,1,0:T(8,128)S(1)}, u32[]{:S(2)}, u32[]{:S(2)}) collective-permute-start(f32[6,6,512]{2,1,0:T(8,128)S(1)} %get-tuple-element.38), channel_id=1, source_target_pairs={{8,0},{16,8},{24,16},{32,24},{40,32},{48,40},{56,48},{64,56},{72,6... | collective-permute-start | bytes 221192 | tf_op jit(solution)/shard_map/ppermute | solution.py:18
  8.3 0.0 copy-start.5
  8.3 0.6 copy-done.5
  9.0 0.0 collective-permute-done
  9.0 5.1 %collective-permute-done.1 = f32[6,6,512]{2,1,0:T(8,128)S(1)} collective-permute-done((f32[6,6,512]{2,1,0:T(8,128)S(1)}, f32[6,6,512]{2,1,0:T(8,128)S(1)}, u32[]{:S(2)}, u32[]{:S(2)}) %collective-permute-start.1) | collective-permute-done | bytes 73760 | tf_op jit(solution)/shard_map/ppermute | solution.py:18
  14.1 0.1 pad_maximum_fusion.4
  14.2 6.8 %collective-permute-start.2 = (f32[6,28,6]{2,1,0:T(8,128)S(1)}, f32[6,28,6]{2,1,0:T(8,128)S(1)}, u32[]{:S(2)}, u32[]{:S(2)}) collective-permute-start(f32[6,28,6]{2,1,0:T(8,128)S(1)} %get-tuple-element.31), channel_id=1, source_target_pairs={{0,1},{1,2},{2,3},{3,4},{4,5},{5,6},{6,7},{7,0},{8,9},{9,10},{10,1... | collective-permute-start | bytes 12104 | tf_op jit(solution)/shard_map/ppermute | solution.py:20
  21.0 1.9 %collective-permute-start.3 = (f32[6,28,6]{2,1,0:T(8,128)S(1)}, f32[6,28,6]{2,1,0:T(8,128)S(1)}, u32[]{:S(2)}, u32[]{:S(2)}) collective-permute-start(f32[6,28,6]{2,1,0:T(8,128)S(1)} %get-tuple-element.32), channel_id=1, source_target_pairs={{1,0},{2,1},{3,2},{4,3},{5,4},{6,5},{7,6},{0,7},{9,8},{10,9},{11,1... | collective-permute-start | bytes 12104 | tf_op jit(solution)/shard_map/ppermute | solution.py:21
  22.9 0.6 collective-permute-done.2
  23.5 10.6 %collective-permute-done.3 = f32[6,28,6]{2,1,0:T(8,128)S(1)} collective-permute-done((f32[6,28,6]{2,1,0:T(8,128)S(1)}, f32[6,28,6]{2,1,0:T(8,128)S(1)}, u32[]{:S(2)}, u32[]{:S(2)}) %collective-permute-start.3) | collective-permute-done | bytes 4064 | tf_op jit(solution)/shard_map/ppermute | solution.py:21
  34.1 0.3 pad_maximum_fusion
  34.4 0.1 compare_bitcast_fusion.7
  34.5 0.6 select_select_fusion
  35.2 0.1 slice_bitcast_fusion.6
  35.2 0.3 fusion.6
  35.5 0.2 fusion.28
  35.7 0.2 fusion.30
  35.9 0.1 fusion.31
  36.0 0.2 fusion.25
  36.3 0.2 fusion.10
  36.5 0.2 fusion.16
  36.7 0.6 gather_fusion
  37.3 0.1 copy.16
  37.4 0.2 fusion.9
  37.6 0.1 add_bitcast_fusion
  37.8 0.6 gather_fusion.1
  38.4 0.1 copy.17
  38.5 0.6 gather_fusion.2
  39.2 0.1 copy.18
  39.3 0.6 copy-done.2
  39.9 0.1 pad_maximum_fusion.6
  39.9 1.9 %collective-permute-start.4 = (f32[4,256]{1,0:T(4,128)S(1)}, f32[4,256]{1,0:T(4,128)S(1)}, u32[]{:S(2)}, u32[]{:S(2)}) collective-permute-start(f32[4,256]{1,0:T(4,128)S(1)} %pad_maximum_fusion.6), channel_id=1, source_target_pairs={{0,1},{1,0},{2,3},{3,2},{4,5},{5,4},{6,7},{7,6},{8,9},{9,8},{10,11... | collective-permute-start | bytes 12296 | tf_op jit(solution)/shard_map/ppermute | solution.py:91
  41.9 3.6 %collective-permute-done.4 = f32[4,256]{1,0:T(4,128)S(1)} collective-permute-done((f32[4,256]{1,0:T(4,128)S(1)}, f32[4,256]{1,0:T(4,128)S(1)}, u32[]{:S(2)}, u32[]{:S(2)}) %collective-permute-start.4) | collective-permute-done | bytes 4128 | tf_op jit(solution)/shard_map/ppermute | solution.py:91
  45.4 0.1 maximum_select_fusion.6
  45.5 1.9 %collective-permute-start.5 = (f32[8,256]{1,0:T(8,128)S(1)}, f32[8,256]{1,0:T(8,128)S(1)}, u32[]{:S(2)}, u32[]{:S(2)}) collective-permute-start(f32[8,256]{1,0:T(8,128)S(1)} %maximum_select_fusion.6), channel_id=1, source_target_pairs={{0,2},{1,3},{2,0},{3,1},{4,6},{5,7},{6,4},{7,5},{8,10},{9,11},{10,... | collective-permute-start | bytes 24584 | tf_op jit(solution)/shard_map/ppermute | solution.py:91
  47.5 0.0 copy-start.6
  47.5 4.5 %collective-permute-done.5 = f32[8,256]{1,0:T(8,128)S(1)} collective-permute-done((f32[8,256]{1,0:T(8,128)S(1)}, f32[8,256]{1,0:T(8,128)S(1)}, u32[]{:S(2)}, u32[]{:S(2)}) %collective-permute-start.5) | collective-permute-done | bytes 8224 | tf_op jit(solution)/shard_map/ppermute | solution.py:91
  51.9 1.9 %collective-permute-start.6 = (f32[16,256]{1,0:T(8,128)S(1)}, f32[16,256]{1,0:T(8,128)S(1)}, u32[]{:S(2)}, u32[]{:S(2)}) collective-permute-start(f32[16,256]{1,0:T(8,128)S(1)} %maximum_select_fusion.5), channel_id=1, source_target_pairs={{0,4},{1,5},{2,6},{3,7},{4,0},{5,1},{6,2},{7,3},{8,12},{9,13},{10,... | collective-permute-start | bytes 49160 | tf_op jit(solution)/shard_map/ppermute | solution.py:91
  53.9 7.6 %collective-permute-done.6 = f32[16,256]{1,0:T(8,128)S(1)} collective-permute-done((f32[16,256]{1,0:T(8,128)S(1)}, f32[16,256]{1,0:T(8,128)S(1)}, u32[]{:S(2)}, u32[]{:S(2)}) %collective-permute-start.6) | collective-permute-done | bytes 16416 | tf_op jit(solution)/shard_map/ppermute | solution.py:91
  61.5 1.9 %collective-permute-start.7 = (f32[32,256]{1,0:T(8,128)S(1)}, f32[32,256]{1,0:T(8,128)S(1)}, u32[]{:S(2)}, u32[]{:S(2)}) collective-permute-start(f32[32,256]{1,0:T(8,128)S(1)} %maximum_select_fusion.4), channel_id=1, source_target_pairs={{0,8},{8,0},{16,24},{24,16},{32,40},{40,32},{48,56},{56,48},{64,72... | collective-permute-start | bytes 98312 | tf_op jit(solution)/shard_map/ppermute | solution.py:91
  63.5 3.8 %collective-permute-done.7 = f32[32,256]{1,0:T(8,128)S(1)} collective-permute-done((f32[32,256]{1,0:T(8,128)S(1)}, f32[32,256]{1,0:T(8,128)S(1)}, u32[]{:S(2)}, u32[]{:S(2)}) %collective-permute-start.7) | collective-permute-done | bytes 32800 | tf_op jit(solution)/shard_map/ppermute | solution.py:91
  67.3 1.9 %collective-permute-start.8 = (f32[64,256]{1,0:T(8,128)S(1)}, f32[64,256]{1,0:T(8,128)S(1)}, u32[]{:S(2)}, u32[]{:S(2)}) collective-permute-start(f32[64,256]{1,0:T(8,128)S(1)} %maximum_select_fusion.3), channel_id=1, source_target_pairs={{0,16},{8,24},{16,0},{24,8},{32,48},{40,56},{48,32},{56,40},{64,80... | collective-permute-start | bytes 196616 | tf_op jit(solution)/shard_map/ppermute | solution.py:91
  69.2 0.1 bitcast_dynamic-update-slice_fusion.3
  69.3 5.7 %collective-permute-done.8 = f32[64,256]{1,0:T(8,128)S(1)} collective-permute-done((f32[64,256]{1,0:T(8,128)S(1)}, f32[64,256]{1,0:T(8,128)S(1)}, u32[]{:S(2)}, u32[]{:S(2)}) %collective-permute-start.8) | collective-permute-done | bytes 65568 | tf_op jit(solution)/shard_map/ppermute | solution.py:91
  75.0 2.4 %collective-permute-start.9 = (f32[128,256]{1,0:T(8,128)S(1)}, f32[128,256]{1,0:T(8,128)S(1)}, u32[]{:S(2)}, u32[]{:S(2)}) collective-permute-start(f32[128,256]{1,0:T(8,128)S(1)} %maximum_select_fusion.2), channel_id=1, source_target_pairs={{0,32},{8,40},{16,48},{24,56},{32,0},{40,8},{48,16},{56,24},{64,96... | collective-permute-start | bytes 393224 | tf_op jit(solution)/shard_map/ppermute | solution.py:91
  77.4 0.1 bitcast_dynamic-update-slice_fusion.2
  77.5 4.8 %collective-permute-done.9 = f32[128,256]{1,0:T(8,128)S(1)} collective-permute-done((f32[128,256]{1,0:T(8,128)S(1)}, f32[128,256]{1,0:T(8,128)S(1)}, u32[]{:S(2)}, u32[]{:S(2)}) %collective-permute-start.9) | collective-permute-done | bytes 131104 | tf_op jit(solution)/shard_map/ppermute | solution.py:91
  82.3 2.1 %collective-permute-start.10 = (f32[256,256]{1,0:T(8,128)S(1)}, f32[256,256]{1,0:T(8,128)S(1)}, u32[]{:S(2)}, u32[]{:S(2)}) collective-permute-start(f32[256,256]{1,0:T(8,128)S(1)} %maximum_select_fusion.1), channel_id=1, source_target_pairs={{0,64},{8,72},{16,80},{24,88},{32,96},{40,104},{48,112},{56,120},{... | collective-permute-start | bytes 786440 | tf_op jit(solution)/shard_map/ppermute | solution.py:91
  84.4 7.6 %collective-permute-done.10 = f32[256,256]{1,0:T(8,128)S(1)} collective-permute-done((f32[256,256]{1,0:T(8,128)S(1)}, f32[256,256]{1,0:T(8,128)S(1)}, u32[]{:S(2)}, u32[]{:S(2)}) %collective-permute-start.10) | collective-permute-done | bytes 262176 | tf_op jit(solution)/shard_map/ppermute | solution.py:91
  92.1 0.8 gather_fusion.3
  92.8 0.7 reshape.65.rows_ref
  93.5 4.3 %shard_map.94 = f32[16,128]{1,0:T(8,128)} custom-call(f32[256,128]{1,0:T(8,128)} %reshape.65.rows_ref, s32[128,16,128]{2,1,0:T(8,128)} %bitcast.96), custom_call_target="tpu_custom_call" | custom-call | flops 2097152 | bytes 1187840 | tf_op jit(solution)/shard_map/pallas_call | solution.py:73
  97.8 2.0 %collective-permute-start.11 = (f32[16,128]{1,0:T(8,128)}, f32[16,128]{1,0:T(8,128)S(1)}, u32[]{:S(2)}, u32[]{:S(2)}) collective-permute-start(f32[16,128]{1,0:T(8,128)} %shard_map.94), channel_id=1, source_target_pairs={{0,128},{128,0},{256,384},{384,256},{1,129},{129,1},{257,385},{385... | collective-permute-start | bytes 24584 | tf_op jit(solution)/shard_map/ppermute | solution.py:108
  99.8 0.1 fusion.36
  100.0 0.0 copy-start.3
  100.0 1.2 %collective-permute-done.11 = f32[16,128]{1,0:T(8,128)S(1)} collective-permute-done((f32[16,128]{1,0:T(8,128)}, f32[16,128]{1,0:T(8,128)S(1)}, u32[]{:S(2)}, u32[]{:S(2)}) %collective-permute-start.11) | collective-permute-done | bytes 8224 | tf_op jit(solution)/shard_map/ppermute | solution.py:108
  101.2 1.9 %collective-permute-start.12 = (f32[16,128]{1,0:T(8,128)S(1)}, f32[16,128]{1,0:T(8,128)S(1)}, u32[]{:S(2)}, u32[]{:S(2)}) collective-permute-start(f32[16,128]{1,0:T(8,128)S(1)} %add.205), channel_id=1, source_target_pairs={{0,256},{128,384},{256,0},{384,128},{1,257},{129,385},{257,1},{385... | collective-permute-start | bytes 24584 | tf_op jit(solution)/shard_map/ppermute | solution.py:108
  103.1 0.6 copy.19
  103.7 11.7 %collective-permute-done.12 = f32[16,128]{1,0:T(8,128)S(1)} collective-permute-done((f32[16,128]{1,0:T(8,128)S(1)}, f32[16,128]{1,0:T(8,128)S(1)}, u32[]{:S(2)}, u32[]{:S(2)}) %collective-permute-start.12) | collective-permute-done | bytes 8224 | tf_op jit(solution)/shard_map/ppermute | solution.py:108
  115.5 0.6 multiply_multiply_fusion
  (27 shorter events, 0.2 us)
Async XLA Ops:
  1.4 12.7 %copy-start = (f32[1,5,16,512]{3,2,1,0:T(8,128)S(1)}, f32[1,5,16,512]{3,2,1,0:T(8,128)}, u32[]{:S(2)}) copy-start(f32[1,5,16,512]{3,2,1,0:T(8,128)} %param.7) | copy-start | bytes 491524
  2.4 5.9 %copy-start.4 = (f32[8,6]{1,0:T(8,128)S(1)}, f32[8,6]{1,0:T(8,128)}, u32[]{:S(2)}) copy-start(f32[8,6]{1,0:T(8,128)} %param.9) | copy-start | bytes 580
  2.4 6.6 %collective-permute-start = (f32[6,6,512]{2,1,0:T(8,128)S(1)}, f32[6,6,512]{2,1,0:T(8,128)S(1)}, u32[]{:S(2)}, u32[]{:S(2)}) collective-permute-start(f32[6,6,512]{2,1,0:T(8,128)S(1)} %get-tuple-element.37), channel_id=1, source_target_pairs={{0,8},{8,16},{16,24},{24,32},{32,40},{40,48},{48,56},{56,64},{64,7... | collective-permute-start | bytes 221192 | tf_op jit(solution)/shard_map/ppermute | solution.py:17
  5.5 8.6 %collective-permute-start.1 = (f32[6,6,512]{2,1,0:T(8,128)S(1)}, f32[6,6,512]{2,1,0:T(8,128)S(1)}, u32[]{:S(2)}, u32[]{:S(2)}) collective-permute-start(f32[6,6,512]{2,1,0:T(8,128)S(1)} %get-tuple-element.38), channel_id=1, source_target_pairs={{8,0},{16,8},{24,16},{32,24},{40,32},{48,40},{56,48},{64,56},{72,6... | collective-permute-start | bytes 221192 | tf_op jit(solution)/shard_map/ppermute | solution.py:18
  8.3 0.7 copy-start.5
  14.2 9.3 %collective-permute-start.2 = (f32[6,28,6]{2,1,0:T(8,128)S(1)}, f32[6,28,6]{2,1,0:T(8,128)S(1)}, u32[]{:S(2)}, u32[]{:S(2)}) collective-permute-start(f32[6,28,6]{2,1,0:T(8,128)S(1)} %get-tuple-element.31), channel_id=1, source_target_pairs={{0,1},{1,2},{2,3},{3,4},{4,5},{5,6},{6,7},{7,0},{8,9},{9,10},{10,1... | collective-permute-start | bytes 12104 | tf_op jit(solution)/shard_map/ppermute | solution.py:20
  21.0 13.1 %collective-permute-start.3 = (f32[6,28,6]{2,1,0:T(8,128)S(1)}, f32[6,28,6]{2,1,0:T(8,128)S(1)}, u32[]{:S(2)}, u32[]{:S(2)}) collective-permute-start(f32[6,28,6]{2,1,0:T(8,128)S(1)} %get-tuple-element.32), channel_id=1, source_target_pairs={{1,0},{2,1},{3,2},{4,3},{5,4},{6,5},{7,6},{0,7},{9,8},{10,9},{11,1... | collective-permute-start | bytes 12104 | tf_op jit(solution)/shard_map/ppermute | solution.py:21
  39.2 0.7 copy-start.2
  39.9 5.5 %collective-permute-start.4 = (f32[4,256]{1,0:T(4,128)S(1)}, f32[4,256]{1,0:T(4,128)S(1)}, u32[]{:S(2)}, u32[]{:S(2)}) collective-permute-start(f32[4,256]{1,0:T(4,128)S(1)} %pad_maximum_fusion.6), channel_id=1, source_target_pairs={{0,1},{1,0},{2,3},{3,2},{4,5},{5,4},{6,7},{7,6},{8,9},{9,8},{10,11... | collective-permute-start | bytes 12296 | tf_op jit(solution)/shard_map/ppermute | solution.py:91
  45.5 6.4 %collective-permute-start.5 = (f32[8,256]{1,0:T(8,128)S(1)}, f32[8,256]{1,0:T(8,128)S(1)}, u32[]{:S(2)}, u32[]{:S(2)}) collective-permute-start(f32[8,256]{1,0:T(8,128)S(1)} %maximum_select_fusion.6), channel_id=1, source_target_pairs={{0,2},{1,3},{2,0},{3,1},{4,6},{5,7},{6,4},{7,5},{8,10},{9,11},{10,... | collective-permute-start | bytes 24584 | tf_op jit(solution)/shard_map/ppermute | solution.py:91
  47.5 6.4 %copy-start.6 = (s32[1,128]{1,0:T(1,128)S(1)}, s32[1,128]{1,0:T(1,128)}, u32[]{:S(2)}) copy-start(s32[1,128]{1,0:T(1,128)} %param.12) | copy-start | bytes 1540
  51.9 9.5 %collective-permute-start.6 = (f32[16,256]{1,0:T(8,128)S(1)}, f32[16,256]{1,0:T(8,128)S(1)}, u32[]{:S(2)}, u32[]{:S(2)}) collective-permute-start(f32[16,256]{1,0:T(8,128)S(1)} %maximum_select_fusion.5), channel_id=1, source_target_pairs={{0,4},{1,5},{2,6},{3,7},{4,0},{5,1},{6,2},{7,3},{8,12},{9,13},{10,... | collective-permute-start | bytes 49160 | tf_op jit(solution)/shard_map/ppermute | solution.py:91
  61.5 5.8 %collective-permute-start.7 = (f32[32,256]{1,0:T(8,128)S(1)}, f32[32,256]{1,0:T(8,128)S(1)}, u32[]{:S(2)}, u32[]{:S(2)}) collective-permute-start(f32[32,256]{1,0:T(8,128)S(1)} %maximum_select_fusion.4), channel_id=1, source_target_pairs={{0,8},{8,0},{16,24},{24,16},{32,40},{40,32},{48,56},{56,48},{64,72... | collective-permute-start | bytes 98312 | tf_op jit(solution)/shard_map/ppermute | solution.py:91
  67.3 7.7 %collective-permute-start.8 = (f32[64,256]{1,0:T(8,128)S(1)}, f32[64,256]{1,0:T(8,128)S(1)}, u32[]{:S(2)}, u32[]{:S(2)}) collective-permute-start(f32[64,256]{1,0:T(8,128)S(1)} %maximum_select_fusion.3), channel_id=1, source_target_pairs={{0,16},{8,24},{16,0},{24,8},{32,48},{40,56},{48,32},{56,40},{64,80... | collective-permute-start | bytes 196616 | tf_op jit(solution)/shard_map/ppermute | solution.py:91
  75.0 7.3 %collective-permute-start.9 = (f32[128,256]{1,0:T(8,128)S(1)}, f32[128,256]{1,0:T(8,128)S(1)}, u32[]{:S(2)}, u32[]{:S(2)}) collective-permute-start(f32[128,256]{1,0:T(8,128)S(1)} %maximum_select_fusion.2), channel_id=1, source_target_pairs={{0,32},{8,40},{16,48},{24,56},{32,0},{40,8},{48,16},{56,24},{64,96... | collective-permute-start | bytes 393224 | tf_op jit(solution)/shard_map/ppermute | solution.py:91
  82.3 9.8 %collective-permute-start.10 = (f32[256,256]{1,0:T(8,128)S(1)}, f32[256,256]{1,0:T(8,128)S(1)}, u32[]{:S(2)}, u32[]{:S(2)}) collective-permute-start(f32[256,256]{1,0:T(8,128)S(1)} %maximum_select_fusion.1), channel_id=1, source_target_pairs={{0,64},{8,72},{16,80},{24,88},{32,96},{40,104},{48,112},{56,120},{... | collective-permute-start | bytes 786440 | tf_op jit(solution)/shard_map/ppermute | solution.py:91
  97.8 3.4 %copy-start.1 = (f32[16,128]{1,0:T(8,128)S(1)}, f32[16,128]{1,0:T(8,128)}, u32[]{:S(2)}) copy-start(f32[16,128]{1,0:T(8,128)} %shard_map.94) | copy-start | bytes 24580
  97.8 3.4 %collective-permute-start.11 = (f32[16,128]{1,0:T(8,128)}, f32[16,128]{1,0:T(8,128)S(1)}, u32[]{:S(2)}, u32[]{:S(2)}) collective-permute-start(f32[16,128]{1,0:T(8,128)} %shard_map.94), channel_id=1, source_target_pairs={{0,128},{128,0},{256,384},{384,256},{1,129},{129,1},{257,385},{385... | collective-permute-start | bytes 24584 | tf_op jit(solution)/shard_map/ppermute | solution.py:108
  100.0 16.1 %copy-start.3 = (f32[5,16,512]{2,1,0:T(8,128)}, f32[5,16,512]{2,1,0:T(8,128)S(1)}, u32[]{:S(2)}) copy-start(f32[5,16,512]{2,1,0:T(8,128)S(1)} %fusion.36) | copy-start | bytes 491524
  101.2 14.2 %collective-permute-start.12 = (f32[16,128]{1,0:T(8,128)S(1)}, f32[16,128]{1,0:T(8,128)S(1)}, u32[]{:S(2)}, u32[]{:S(2)}) collective-permute-start(f32[16,128]{1,0:T(8,128)S(1)} %add.205), channel_id=1, source_target_pairs={{0,256},{128,384},{256,0},{384,128},{1,257},{129,385},{257,1},{385... | collective-permute-start | bytes 24584 | tf_op jit(solution)/shard_map/ppermute | solution.py:108

commit v5 on v1

--- a/solution.py
+++ b/solution.py
@@ -83,9 +83,28 @@
     )(rows, delays)
 
 
+def gather_radix(block, axis, radix):
+    count = lax.axis_size(axis)
+    me = lax.axis_index(axis)
+    stride = 1
+    while stride < count:
+        width = min(radix, count // stride)
+        digit = (me // stride) % width
+        received = [block]
+        for shift in range(1, width):
+            pairs = []
+            for i in range(count):
+                own = (i // stride) % width
+                pairs.append((i, i + ((own + shift) % width - own) * stride))
+            received.append(lax.ppermute(block, axis, pairs))
+        order = (digit - jnp.arange(width, dtype=jnp.int32)) % width
+        block = jnp.stack(received)[order].reshape((-1,) + block.shape[1:])
+        stride *= width
+    return block
+
+
 def gather_waves(local_waves):
-    inner_waves = lax.all_gather(local_waves, "hoop", axis=0, tiled=True)
-    return lax.all_gather(inner_waves, "axial", axis=0, tiled=True)
+    return gather_radix(gather_radix(local_waves, "hoop", 4), "axial", 4)
 
 
 def per_device(wave_state, layup_zone, moduli, sensors, history, receivers, delays):

time: 132 us -> 115 us (0.87)
  blocking collectives: 89.9 us -> 23.4 us
  starting transfers between devices: 20.1 us -> 59.7 us
  waiting for transfers between devices: 4.29 us -> 11.6 us
    all_gather x2 -> x0, blocking collectives: 61 us -> none  [the longest x1 40.1 us: gather_waves(): inner_waves = lax.all_gather(local_waves, 'hoop', axis=0, tiled=True)]
    ppermute x0 -> x10, starting transfers between devices: none -> 39.5 us  [gather_radix(): received.append(lax.ppermute(block, axis, pairs))]
    ppermute x0 -> x10, waiting for transfers between devices: none -> 6.23 us  [gather_radix(): received.append(lax.ppermute(block, axis, pairs))]
    psum x1, blocking collectives: 28.9 us -> 23.4 us  [per_device(): summed = lax.psum(partial_value, 'act')]
    gather x0 -> x4, local copies, waits for them, and re-layouts: none -> 2.26 us  [gather_radix(): block = jnp.stack(received)[order].reshape((-1,) + block.shape[1:])]
    unnamed x21 -> x20, local copies, waits for them, and re-layouts: 2.74 us -> 1.37 us
  transfers between devices with their start and end apart: 4 -> 14, of which waited for: 3 -> 7; matrix products, arithmetic and copies ran while one was open for 0% -> 1% of each run, Pallas kernels for 0% -> 0%
where the time goes in v5:
time: 115 us; the launch traced here: 113 us
  starting transfers between devices  59.7 us (52%)
  blocking collectives  23.4 us (20%)
  waiting for transfers between devices  11.6 us (10%)
  local copies, waits for them, and re-layouts  7.32 us (6%)
  other arithmetic  5.64 us (5%)
  Pallas kernels  4.28 us (4%)
  between operations  1.21 us (1%)
    ppermute x10, starting transfers between devices, gather_radix(): received.append(lax.ppermute(block, axis, pairs))  39.5 us
    psum x1, blocking collectives, per_device(): summed = lax.psum(partial_value, 'act')  23.4 us
    ppermute x1, starting transfers between devices, exchange(): lax.ppermute(cells[:, :, :halo], 'hoop', [((j + 1) % nh, j) for j in rang...  11.3 us
    ppermute x10, waiting for transfers between devices, gather_radix(): received.append(lax.ppermute(block, axis, pairs))  6.23 us
    pallas_call x1, Pallas kernels, image(): pl.pallas_call(image_kernel, out_shape=jax.ShapeDtypeStruct((pix_rows, pi...  4.28 us
    ppermute x1, starting transfers between devices, exchange(): lax.ppermute(cells[:, -halo:, :], 'axial', [(i, i + 1) for i in range(na...  4.17 us
    ppermute x1, waiting for transfers between devices, exchange(): lax.ppermute(cells[:, :halo, :], 'axial', [(i + 1, i) for i in range(na -...  3.74 us
    ppermute x1, starting transfers between devices, exchange(): lax.ppermute(cells[:, :, -halo:], 'hoop', [(j, (j + 1) % nh) for j in ran...  3.55 us
  transfers between devices with their start and end apart: 14, of which 7 were waited for; matrix products, arithmetic and copies ran while one was open for 1% of the time, Pallas kernels for 0%

profile of v5, /device:TPU:1, one launch (start us, length us, event | category | flops | bytes accessed | tf_op | source)
XLA Modules:
  0.0 113.2 jit_solution(2977190136361174544)
XLA Ops:
  0.6 0.8 convert_bitcast_fusion
  1.4 1.0 fusion
  2.4 0.0 copy-start
  2.4 4.2 %collective-permute-start = (f32[6,6,512]{2,1,0:T(8,128)S(1)}, f32[6,6,512]{2,1,0:T(8,128)S(1)}, u32[]{:S(2)}, u32[]{:S(2)}) collective-permute-start(f32[6,6,512]{2,1,0:T(8,128)S(1)} %get-tuple-element.37), channel_id=1, source_target_pairs={{0,8},{8,16},{16,24},{24,32},{32,40},{40,48},{48,56},{56,64},{64,7... | collective-permute-start | bytes 221192 | tf_op jit(solution)/shard_map/ppermute | solution.py:17
  6.6 1.3 %collective-permute-start.1 = (f32[6,6,512]{2,1,0:T(8,128)S(1)}, f32[6,6,512]{2,1,0:T(8,128)S(1)}, u32[]{:S(2)}, u32[]{:S(2)}) collective-permute-start(f32[6,6,512]{2,1,0:T(8,128)S(1)} %get-tuple-element.38), channel_id=1, source_target_pairs={{8,0},{16,8},{24,16},{32,24},{40,32},{48,40},{56,48},{64,56},{72,6... | collective-permute-start | bytes 221192 | tf_op jit(solution)/shard_map/ppermute | solution.py:18
  8.2 0.0 collective-permute-done
  8.2 3.7 %collective-permute-done.1 = f32[6,6,512]{2,1,0:T(8,128)S(1)} collective-permute-done((f32[6,6,512]{2,1,0:T(8,128)S(1)}, f32[6,6,512]{2,1,0:T(8,128)S(1)}, u32[]{:S(2)}, u32[]{:S(2)}) %collective-permute-start.1) | collective-permute-done | bytes 73760 | tf_op jit(solution)/shard_map/ppermute | solution.py:18
  11.9 0.1 pad_maximum_fusion.6
  12.0 3.5 %collective-permute-start.2 = (f32[6,28,6]{2,1,0:T(8,128)S(1)}, f32[6,28,6]{2,1,0:T(8,128)S(1)}, u32[]{:S(2)}, u32[]{:S(2)}) collective-permute-start(f32[6,28,6]{2,1,0:T(8,128)S(1)} %get-tuple-element.31), channel_id=1, source_target_pairs={{0,1},{1,2},{2,3},{3,4},{4,5},{5,6},{6,7},{7,0},{8,9},{9,10},{10,1... | collective-permute-start | bytes 12104 | tf_op jit(solution)/shard_map/ppermute | solution.py:20
  15.6 11.3 %collective-permute-start.3 = (f32[6,28,6]{2,1,0:T(8,128)S(1)}, f32[6,28,6]{2,1,0:T(8,128)S(1)}, u32[]{:S(2)}, u32[]{:S(2)}) collective-permute-start(f32[6,28,6]{2,1,0:T(8,128)S(1)} %get-tuple-element.32), channel_id=1, source_target_pairs={{1,0},{2,1},{3,2},{4,3},{5,4},{6,5},{7,6},{0,7},{9,8},{10,9},{11,1... | collective-permute-start | bytes 12104 | tf_op jit(solution)/shard_map/ppermute | solution.py:21
  26.9 0.1 collective-permute-done.2
  27.0 1.5 %collective-permute-done.3 = f32[6,28,6]{2,1,0:T(8,128)S(1)} collective-permute-done((f32[6,28,6]{2,1,0:T(8,128)S(1)}, f32[6,28,6]{2,1,0:T(8,128)S(1)}, u32[]{:S(2)}, u32[]{:S(2)}) %collective-permute-start.3) | collective-permute-done | bytes 4064 | tf_op jit(solution)/shard_map/ppermute | solution.py:21
  28.5 0.3 pad_maximum_fusion.1
  28.8 0.1 compare_bitcast_fusion.7
  28.9 0.6 select_select_fusion
  29.5 0.1 slice_bitcast_fusion.6
  29.6 0.3 fusion.6
  29.9 0.2 fusion.28
  30.1 0.2 fusion.30
  30.3 0.1 fusion.31
  30.4 0.2 fusion.25
  30.6 0.2 fusion.10
  30.8 0.2 fusion.16
  31.0 0.6 gather_fusion
  31.7 0.1 copy.16
  31.8 0.2 fusion.9
  32.0 0.1 add_bitcast_fusion
  32.2 0.6 gather_fusion.1
  32.8 0.1 copy.17
  32.9 0.6 gather_fusion.2
  33.5 0.1 copy.18
  33.6 0.6 copy-done.1
  34.2 0.1 pad_maximum_fusion.10
  34.3 1.9 %collective-permute-start.4 = (f32[4,256]{1,0:T(4,128)S(1)}, f32[4,256]{1,0:T(4,128)S(1)}, u32[]{:S(2)}, u32[]{:S(2)}) collective-permute-start(f32[4,256]{1,0:T(4,128)S(1)} %pad_maximum_fusion.10), channel_id=1, source_target_pairs={{0,1},{1,2},{2,3},{3,0},{4,5},{5,6},{6,7},{7,4},{8,9},{9,10},{10,1... | collective-permute-start | bytes 12296 | tf_op jit(solution)/shard_map/ppermute | solution.py:99
  36.2 2.0 %collective-permute-start.5 = (f32[4,256]{1,0:T(4,128)S(1)}, f32[4,256]{1,0:T(4,128)S(1)}, u32[]{:S(2)}, u32[]{:S(2)}) collective-permute-start(f32[4,256]{1,0:T(4,128)S(1)} %pad_maximum_fusion.10), channel_id=1, source_target_pairs={{0,2},{1,3},{2,0},{3,1},{4,6},{5,7},{6,4},{7,5},{8,10},{9,11},{10,... | collective-permute-start | bytes 12296 | tf_op jit(solution)/shard_map/ppermute | solution.py:99
  38.2 5.1 %collective-permute-start.6 = (f32[4,256]{1,0:T(4,128)S(1)}, f32[4,256]{1,0:T(4,128)S(1)}, u32[]{:S(2)}, u32[]{:S(2)}) collective-permute-start(f32[4,256]{1,0:T(4,128)S(1)} %pad_maximum_fusion.10), channel_id=1, source_target_pairs={{0,3},{1,0},{2,1},{3,2},{4,7},{5,4},{6,5},{7,6},{8,11},{9,8},{10,9... | collective-permute-start | bytes 12296 | tf_op jit(solution)/shard_map/ppermute | solution.py:99
  43.3 0.1 bitcast_dynamic-update-slice_fusion.3
  43.4 0.1 bitcast_dynamic-update-slice_fusion.2
  43.5 0.1 fusion.51
  43.6 0.0 collective-permute-done.4
  43.6 0.0 collective-permute-done.5
  43.6 1.1 %collective-permute-done.6 = f32[4,256]{1,0:T(4,128)S(1)} collective-permute-done((f32[4,256]{1,0:T(4,128)S(1)}, f32[4,256]{1,0:T(4,128)S(1)}, u32[]{:S(2)}, u32[]{:S(2)}) %collective-permute-start.6) | collective-permute-done | bytes 4128 | tf_op jit(solution)/shard_map/ppermute | solution.py:99
  44.7 0.6 gather_fusion.3
  45.3 8.7 %collective-permute-start.7 = (f32[16,256]{1,0:T(8,128)S(1)}, f32[16,256]{1,0:T(8,128)S(1)}, u32[]{:S(2)}, u32[]{:S(2)}) collective-permute-start(f32[16,256]{1,0:T(8,128)S(1)} %reshape.273), channel_id=1, source_target_pairs={{0,4},{1,5},{2,6},{3,7},{4,0},{5,1},{6,2},{7,3},{8,12},{9,13},{10,... | collective-permute-start | bytes 49160 | tf_op jit(solution)/shard_map/ppermute | solution.py:99
  54.0 1.2 %collective-permute-done.7 = f32[16,256]{1,0:T(8,128)S(1)} collective-permute-done((f32[16,256]{1,0:T(8,128)S(1)}, f32[16,256]{1,0:T(8,128)S(1)}, u32[]{:S(2)}, u32[]{:S(2)}) %collective-permute-start.7) | collective-permute-done | bytes 16416 | tf_op jit(solution)/shard_map/ppermute | solution.py:99
  55.2 0.5 gather_fusion.4
  55.7 3.4 %collective-permute-start.8 = (f32[32,256]{1,0:T(8,128)S(1)}, f32[32,256]{1,0:T(8,128)S(1)}, u32[]{:S(2)}, u32[]{:S(2)}) collective-permute-start(f32[32,256]{1,0:T(8,128)S(1)} %bitcast.127), channel_id=1, source_target_pairs={{0,8},{8,16},{16,24},{24,0},{32,40},{40,48},{48,56},{56,32},{64,72... | collective-permute-start | bytes 98312 | tf_op jit(solution)/shard_map/ppermute | solution.py:99
  59.2 6.2 %collective-permute-start.9 = (f32[32,256]{1,0:T(8,128)S(1)}, f32[32,256]{1,0:T(8,128)S(1)}, u32[]{:S(2)}, u32[]{:S(2)}) collective-permute-start(f32[32,256]{1,0:T(8,128)S(1)} %bitcast.128), channel_id=1, source_target_pairs={{0,16},{8,24},{16,0},{24,8},{32,48},{40,56},{48,32},{56,40},{64,80... | collective-permute-start | bytes 98312 | tf_op jit(solution)/shard_map/ppermute | solution.py:99
  65.4 1.9 %collective-permute-start.10 = (f32[32,256]{1,0:T(8,128)S(1)}, f32[32,256]{1,0:T(8,128)S(1)}, u32[]{:S(2)}, u32[]{:S(2)}) collective-permute-start(f32[32,256]{1,0:T(8,128)S(1)} %bitcast.129), channel_id=1, source_target_pairs={{0,24},{8,0},{16,8},{24,16},{32,56},{40,32},{48,40},{56,48},{64,88... | collective-permute-start | bytes 98312 | tf_op jit(solution)/shard_map/ppermute | solution.py:99
  67.3 0.6 copy.19
  67.9 2.1 %collective-permute-done.10 = f32[32,256]{1,0:T(8,128)S(1)} collective-permute-done((f32[32,256]{1,0:T(8,128)S(1)}, f32[32,256]{1,0:T(8,128)S(1)}, u32[]{:S(2)}, u32[]{:S(2)}) %collective-permute-start.10) | collective-permute-done | bytes 32800 | tf_op jit(solution)/shard_map/ppermute | solution.py:99
  70.1 0.6 gather_fusion.5
  70.6 3.1 %collective-permute-start.11 = (f32[128,256]{1,0:T(8,128)S(1)}, f32[128,256]{1,0:T(8,128)S(1)}, u32[]{:S(2)}, u32[]{:S(2)}) collective-permute-start(f32[128,256]{1,0:T(8,128)S(1)} %bitcast.123), channel_id=1, source_target_pairs={{0,32},{8,40},{16,48},{24,56},{32,64},{40,72},{48,80},{56,88},{64,... | collective-permute-start | bytes 393224 | tf_op jit(solution)/shard_map/ppermute | solution.py:99
  73.8 3.2 %collective-permute-start.12 = (f32[128,256]{1,0:T(8,128)S(1)}, f32[128,256]{1,0:T(8,128)S(1)}, u32[]{:S(2)}, u32[]{:S(2)}) collective-permute-start(f32[128,256]{1,0:T(8,128)S(1)} %bitcast.124), channel_id=1, source_target_pairs={{0,64},{8,72},{16,80},{24,88},{32,96},{40,104},{48,112},{56,120},{... | collective-permute-start | bytes 393224 | tf_op jit(solution)/shard_map/ppermute | solution.py:99
  76.9 4.0 %collective-permute-start.13 = (f32[128,256]{1,0:T(8,128)S(1)}, f32[128,256]{1,0:T(8,128)S(1)}, u32[]{:S(2)}, u32[]{:S(2)}) collective-permute-start(f32[128,256]{1,0:T(8,128)S(1)} %bitcast.125), channel_id=1, source_target_pairs={{0,96},{8,104},{16,112},{24,120},{32,0},{40,8},{48,16},{56,24},{64... | collective-permute-start | bytes 393224 | tf_op jit(solution)/shard_map/ppermute | solution.py:99
  80.9 0.1 fusion.36
  81.0 0.0 copy-start.2
  81.1 1.8 %collective-permute-done.13 = f32[128,256]{1,0:T(8,128)S(1)} collective-permute-done((f32[128,256]{1,0:T(8,128)S(1)}, f32[128,256]{1,0:T(8,128)S(1)}, u32[]{:S(2)}, u32[]{:S(2)}) %collective-permute-start.13) | collective-permute-done | bytes 131104 | tf_op jit(solution)/shard_map/ppermute | solution.py:99
  82.9 0.6 gather_fusion.6
  83.5 0.8 gather_fusion.7
  84.2 0.7 reshape.277.rows_ref
  84.9 4.3 %shard_map.94 = f32[16,128]{1,0:T(8,128)} custom-call(f32[256,128]{1,0:T(8,128)} %reshape.277.rows_ref, s32[128,16,128]{2,1,0:T(8,128)} %bitcast.122), custom_call_target="tpu_custom_call" | custom-call | flops 2097152 | bytes 1187840 | tf_op jit(solution)/shard_map/pallas_call | solution.py:73
  89.2 23.4 %psum.7 = f32[16,128]{1,0:T(8,128)S(1)} all-reduce(f32[16,128]{1,0:T(8,128)} %shard_map.94), channel_id=1, replica_groups=mesh['act'=4,'axial'=16,'hoop'=8] {'act'}, use_global_device_ids=true, to_apply=%region_0.1 | all-reduce | flops 2048 | bytes 16384 | tf_op jit(solution)/shard_map/psum | solution.py:145
  112.6 0.6 multiply_multiply_fusion
  (38 shorter events, 0.3 us)
Async XLA Ops:
  1.4 6.5 %copy-start.3 = (f32[8,6]{1,0:T(8,128)S(1)}, f32[8,6]{1,0:T(8,128)}, u32[]{:S(2)}) copy-start(f32[8,6]{1,0:T(8,128)} %param.9) | copy-start | bytes 580
  1.4 6.6 %copy-start.4 = (s32[4]{0:T(128)S(1)}, s32[4]{0:T(128)}, u32[]{:S(2)}) copy-start(s32[4]{0:T(128)} %param.10) | copy-start | bytes 52
  1.4 6.6 %copy-start.5 = (s32[1,128]{1,0:T(1,128)S(1)}, s32[1,128]{1,0:T(1,128)}, u32[]{:S(2)}) copy-start(s32[1,128]{1,0:T(1,128)} %param.12) | copy-start | bytes 1540
  2.4 9.6 %copy-start = (f32[1,5,16,512]{3,2,1,0:T(8,128)S(1)}, f32[1,5,16,512]{3,2,1,0:T(8,128)}, u32[]{:S(2)}) copy-start(f32[1,5,16,512]{3,2,1,0:T(8,128)} %param.7) | copy-start | bytes 491524
  2.4 5.8 %collective-permute-start = (f32[6,6,512]{2,1,0:T(8,128)S(1)}, f32[6,6,512]{2,1,0:T(8,128)S(1)}, u32[]{:S(2)}, u32[]{:S(2)}) collective-permute-start(f32[6,6,512]{2,1,0:T(8,128)S(1)} %get-tuple-element.37), channel_id=1, source_target_pairs={{0,8},{8,16},{16,24},{24,32},{32,40},{40,48},{48,56},{56,64},{64,7... | collective-permute-start | bytes 221192 | tf_op jit(solution)/shard_map/ppermute | solution.py:17
  6.6 5.4 %collective-permute-start.1 = (f32[6,6,512]{2,1,0:T(8,128)S(1)}, f32[6,6,512]{2,1,0:T(8,128)S(1)}, u32[]{:S(2)}, u32[]{:S(2)}) collective-permute-start(f32[6,6,512]{2,1,0:T(8,128)S(1)} %get-tuple-element.38), channel_id=1, source_target_pairs={{8,0},{16,8},{24,16},{32,24},{40,32},{48,40},{56,48},{64,56},{72,6... | collective-permute-start | bytes 221192 | tf_op jit(solution)/shard_map/ppermute | solution.py:18
  12.0 14.9 %collective-permute-start.2 = (f32[6,28,6]{2,1,0:T(8,128)S(1)}, f32[6,28,6]{2,1,0:T(8,128)S(1)}, u32[]{:S(2)}, u32[]{:S(2)}) collective-permute-start(f32[6,28,6]{2,1,0:T(8,128)S(1)} %get-tuple-element.31), channel_id=1, source_target_pairs={{0,1},{1,2},{2,3},{3,4},{4,5},{5,6},{6,7},{7,0},{8,9},{9,10},{10,1... | collective-permute-start | bytes 12104 | tf_op jit(solution)/shard_map/ppermute | solution.py:20
  15.6 12.9 %collective-permute-start.3 = (f32[6,28,6]{2,1,0:T(8,128)S(1)}, f32[6,28,6]{2,1,0:T(8,128)S(1)}, u32[]{:S(2)}, u32[]{:S(2)}) collective-permute-start(f32[6,28,6]{2,1,0:T(8,128)S(1)} %get-tuple-element.32), channel_id=1, source_target_pairs={{1,0},{2,1},{3,2},{4,3},{5,4},{6,5},{7,6},{0,7},{9,8},{10,9},{11,1... | collective-permute-start | bytes 12104 | tf_op jit(solution)/shard_map/ppermute | solution.py:21
  33.5 0.7 copy-start.1
  34.3 9.3 %collective-permute-start.4 = (f32[4,256]{1,0:T(4,128)S(1)}, f32[4,256]{1,0:T(4,128)S(1)}, u32[]{:S(2)}, u32[]{:S(2)}) collective-permute-start(f32[4,256]{1,0:T(4,128)S(1)} %pad_maximum_fusion.10), channel_id=1, source_target_pairs={{0,1},{1,2},{2,3},{3,0},{4,5},{5,6},{6,7},{7,4},{8,9},{9,10},{10,1... | collective-permute-start | bytes 12296 | tf_op jit(solution)/shard_map/ppermute | solution.py:99
  36.2 7.3 %collective-permute-start.5 = (f32[4,256]{1,0:T(4,128)S(1)}, f32[4,256]{1,0:T(4,128)S(1)}, u32[]{:S(2)}, u32[]{:S(2)}) collective-permute-start(f32[4,256]{1,0:T(4,128)S(1)} %pad_maximum_fusion.10), channel_id=1, source_target_pairs={{0,2},{1,3},{2,0},{3,1},{4,6},{5,7},{6,4},{7,5},{8,10},{9,11},{10,... | collective-permute-start | bytes 12296 | tf_op jit(solution)/shard_map/ppermute | solution.py:99
  38.2 6.5 %collective-permute-start.6 = (f32[4,256]{1,0:T(4,128)S(1)}, f32[4,256]{1,0:T(4,128)S(1)}, u32[]{:S(2)}, u32[]{:S(2)}) collective-permute-start(f32[4,256]{1,0:T(4,128)S(1)} %pad_maximum_fusion.10), channel_id=1, source_target_pairs={{0,3},{1,0},{2,1},{3,2},{4,7},{5,4},{6,5},{7,6},{8,11},{9,8},{10,9... | collective-permute-start | bytes 12296 | tf_op jit(solution)/shard_map/ppermute | solution.py:99
  45.3 9.9 %collective-permute-start.7 = (f32[16,256]{1,0:T(8,128)S(1)}, f32[16,256]{1,0:T(8,128)S(1)}, u32[]{:S(2)}, u32[]{:S(2)}) collective-permute-start(f32[16,256]{1,0:T(8,128)S(1)} %reshape.273), channel_id=1, source_target_pairs={{0,4},{1,5},{2,6},{3,7},{4,0},{5,1},{6,2},{7,3},{8,12},{9,13},{10,... | collective-permute-start | bytes 49160 | tf_op jit(solution)/shard_map/ppermute | solution.py:99
  55.7 12.2 %collective-permute-start.8 = (f32[32,256]{1,0:T(8,128)S(1)}, f32[32,256]{1,0:T(8,128)S(1)}, u32[]{:S(2)}, u32[]{:S(2)}) collective-permute-start(f32[32,256]{1,0:T(8,128)S(1)} %bitcast.127), channel_id=1, source_target_pairs={{0,8},{8,16},{16,24},{24,0},{32,40},{40,48},{48,56},{56,32},{64,72... | collective-permute-start | bytes 98312 | tf_op jit(solution)/shard_map/ppermute | solution.py:99
  59.2 8.7 %collective-permute-start.9 = (f32[32,256]{1,0:T(8,128)S(1)}, f32[32,256]{1,0:T(8,128)S(1)}, u32[]{:S(2)}, u32[]{:S(2)}) collective-permute-start(f32[32,256]{1,0:T(8,128)S(1)} %bitcast.128), channel_id=1, source_target_pairs={{0,16},{8,24},{16,0},{24,8},{32,48},{40,56},{48,32},{56,40},{64,80... | collective-permute-start | bytes 98312 | tf_op jit(solution)/shard_map/ppermute | solution.py:99
  65.4 4.7 %collective-permute-start.10 = (f32[32,256]{1,0:T(8,128)S(1)}, f32[32,256]{1,0:T(8,128)S(1)}, u32[]{:S(2)}, u32[]{:S(2)}) collective-permute-start(f32[32,256]{1,0:T(8,128)S(1)} %bitcast.129), channel_id=1, source_target_pairs={{0,24},{8,0},{16,8},{24,16},{32,56},{40,32},{48,40},{56,48},{64,88... | collective-permute-start | bytes 98312 | tf_op jit(solution)/shard_map/ppermute | solution.py:99
  70.6 10.4 %collective-permute-start.11 = (f32[128,256]{1,0:T(8,128)S(1)}, f32[128,256]{1,0:T(8,128)S(1)}, u32[]{:S(2)}, u32[]{:S(2)}) collective-permute-start(f32[128,256]{1,0:T(8,128)S(1)} %bitcast.123), channel_id=1, source_target_pairs={{0,32},{8,40},{16,48},{24,56},{32,64},{40,72},{48,80},{56,88},{64,... | collective-permute-start | bytes 393224 | tf_op jit(solution)/shard_map/ppermute | solution.py:99
  73.8 7.3 %collective-permute-start.12 = (f32[128,256]{1,0:T(8,128)S(1)}, f32[128,256]{1,0:T(8,128)S(1)}, u32[]{:S(2)}, u32[]{:S(2)}) collective-permute-start(f32[128,256]{1,0:T(8,128)S(1)} %bitcast.124), channel_id=1, source_target_pairs={{0,64},{8,72},{16,80},{24,88},{32,96},{40,104},{48,112},{56,120},{... | collective-permute-start | bytes 393224 | tf_op jit(solution)/shard_map/ppermute | solution.py:99
  76.9 5.9 %collective-permute-start.13 = (f32[128,256]{1,0:T(8,128)S(1)}, f32[128,256]{1,0:T(8,128)S(1)}, u32[]{:S(2)}, u32[]{:S(2)}) collective-permute-start(f32[128,256]{1,0:T(8,128)S(1)} %bitcast.125), channel_id=1, source_target_pairs={{0,96},{8,104},{16,112},{24,120},{32,0},{40,8},{48,16},{56,24},{64... | collective-permute-start | bytes 393224 | tf_op jit(solution)/shard_map/ppermute | solution.py:99
  81.0 1.8 %copy-start.2 = (f32[5,16,512]{2,1,0:T(8,128)}, f32[5,16,512]{2,1,0:T(8,128)S(1)}, u32[]{:S(2)}) copy-start(f32[5,16,512]{2,1,0:T(8,128)S(1)} %fusion.36) | copy-start | bytes 491524

commit v6 on v1

--- a/solution.py
+++ b/solution.py
@@ -84,8 +84,10 @@
 
 
 def gather_waves(local_waves):
-    inner_waves = lax.all_gather(local_waves, "hoop", axis=0, tiled=True)
-    return lax.all_gather(inner_waves, "axial", axis=0, tiled=True)
+    count = lax.axis_size("axial") * lax.axis_size("hoop")
+    spread = jnp.broadcast_to(local_waves[None], (count,) + local_waves.shape)
+    gathered = lax.all_to_all(spread, ("axial", "hoop"), 0, 0, tiled=True)
+    return gathered.reshape((-1,) + local_waves.shape[1:])
 
 
 def per_device(wave_state, layup_zone, moduli, sensors, history, receivers, delays):

time: 132 us -> 114 us (0.86)
  the two profiles are of different devices: /device:TPU:1 before, /device:TPU:32 now
where the time goes in v6:
time: 114 us; the launch traced here: 113 us
  starting transfers between devices  37 us (32%)
  waiting for transfers between devices  35 us (31%)
  blocking collectives  23.7 us (21%)
  local copies, waits for them, and re-layouts  6.73 us (6%)
  other arithmetic  5.43 us (5%)
  Pallas kernels  4.28 us (4%)
    all_to_all x1, waiting for transfers between devices, gather_waves(): gathered = lax.all_to_all(spread, ('axial', 'hoop'), 0, 0, tiled=True)  27.3 us
    all_to_all x1, starting transfers between devices, gather_waves(): gathered = lax.all_to_all(spread, ('axial', 'hoop'), 0, 0, tiled=True)  25.1 us
    psum x1, blocking collectives, per_device(): summed = lax.psum(partial_value, 'act')  23.7 us
    ppermute x1, waiting for transfers between devices, exchange(): lax.ppermute(cells[:, :halo, :], 'axial', [(i + 1, i) for i in range(na -...  4.32 us
    pallas_call x1, Pallas kernels, image(): pl.pallas_call(image_kernel, out_shape=jax.ShapeDtypeStruct((pix_rows, pi...  4.28 us
    ppermute x1, starting transfers between devices, exchange(): lax.ppermute(cells[:, :, -halo:], 'hoop', [(j, (j + 1) % nh) for j in ran...  3.83 us
    ppermute x1, starting transfers between devices, exchange(): lax.ppermute(cells[:, -halo:, :], 'axial', [(i, i + 1) for i in range(na...  3.49 us
    ppermute x1, starting transfers between devices, exchange(): lax.ppermute(cells[:, :, :halo], 'hoop', [((j + 1) % nh, j) for j in rang...  3.29 us
  transfers between devices with their start and end apart: 5, of which 5 were waited for; matrix products, arithmetic and copies ran while one was open for 1% of the time, Pallas kernels for 0%

profile of v6, /device:TPU:32, one launch (start us, length us, event | category | flops | bytes accessed | tf_op | source)
XLA Modules:
  0.0 113.1 jit_solution(2665766635214124190)
XLA Ops:
  0.6 0.8 convert_bitcast_fusion
  1.4 0.0 copy-start
  1.4 1.0 fusion
  2.4 0.0 copy-start.3
  2.4 3.5 %collective-permute-start = (f32[6,6,512]{2,1,0:T(8,128)S(1)}, f32[6,6,512]{2,1,0:T(8,128)S(1)}, u32[]{:S(2)}, u32[]{:S(2)}) collective-permute-start(f32[6,6,512]{2,1,0:T(8,128)S(1)} %get-tuple-element.37), channel_id=1, source_target_pairs={{0,8},{8,16},{16,24},{24,32},{32,40},{40,48},{48,56},{56,64},{64,7... | collective-permute-start | bytes 221192 | tf_op jit(solution)/shard_map/ppermute | solution.py:17
  5.9 1.3 %collective-permute-start.1 = (f32[6,6,512]{2,1,0:T(8,128)S(1)}, f32[6,6,512]{2,1,0:T(8,128)S(1)}, u32[]{:S(2)}, u32[]{:S(2)}) collective-permute-start(f32[6,6,512]{2,1,0:T(8,128)S(1)} %get-tuple-element.38), channel_id=1, source_target_pairs={{8,0},{16,8},{24,16},{32,24},{40,32},{48,40},{56,48},{64,56},{72,6... | collective-permute-start | bytes 221192 | tf_op jit(solution)/shard_map/ppermute | solution.py:18
  7.2 0.0 copy-done.3
  7.2 0.0 copy-start.4
  7.2 0.6 copy-done.4
  7.9 0.2 collective-permute-done
  8.1 4.3 %collective-permute-done.1 = f32[6,6,512]{2,1,0:T(8,128)S(1)} collective-permute-done((f32[6,6,512]{2,1,0:T(8,128)S(1)}, f32[6,6,512]{2,1,0:T(8,128)S(1)}, u32[]{:S(2)}, u32[]{:S(2)}) %collective-permute-start.1) | collective-permute-done | bytes 73760 | tf_op jit(solution)/shard_map/ppermute | solution.py:18
  12.4 0.0 copy-done
  12.4 0.1 pad_maximum_fusion.4
  12.5 3.8 %collective-permute-start.2 = (f32[6,28,6]{2,1,0:T(8,128)S(1)}, f32[6,28,6]{2,1,0:T(8,128)S(1)}, u32[]{:S(2)}, u32[]{:S(2)}) collective-permute-start(f32[6,28,6]{2,1,0:T(8,128)S(1)} %get-tuple-element.31), channel_id=1, source_target_pairs={{0,1},{1,2},{2,3},{3,4},{4,5},{5,6},{6,7},{7,0},{8,9},{9,10},{10,1... | collective-permute-start | bytes 12104 | tf_op jit(solution)/shard_map/ppermute | solution.py:20
  16.3 3.3 %collective-permute-start.3 = (f32[6,28,6]{2,1,0:T(8,128)S(1)}, f32[6,28,6]{2,1,0:T(8,128)S(1)}, u32[]{:S(2)}, u32[]{:S(2)}) collective-permute-start(f32[6,28,6]{2,1,0:T(8,128)S(1)} %get-tuple-element.32), channel_id=1, source_target_pairs={{1,0},{2,1},{3,2},{4,3},{5,4},{6,5},{7,6},{0,7},{9,8},{10,9},{11,1... | collective-permute-start | bytes 12104 | tf_op jit(solution)/shard_map/ppermute | solution.py:21
  19.7 0.6 collective-permute-done.2
  20.3 2.6 %collective-permute-done.3 = f32[6,28,6]{2,1,0:T(8,128)S(1)} collective-permute-done((f32[6,28,6]{2,1,0:T(8,128)S(1)}, f32[6,28,6]{2,1,0:T(8,128)S(1)}, u32[]{:S(2)}, u32[]{:S(2)}) %collective-permute-start.3) | collective-permute-done | bytes 4064 | tf_op jit(solution)/shard_map/ppermute | solution.py:21
  22.9 0.3 pad_maximum_fusion
  23.2 0.1 compare_bitcast_fusion.7
  23.3 0.6 select_select_fusion
  23.9 0.1 slice_bitcast_fusion.6
  24.0 0.3 fusion.6
  24.3 0.2 fusion.28
  24.4 0.2 fusion.30
  24.7 0.1 fusion.31
  24.7 0.2 fusion.25
  25.0 0.2 fusion.10
  25.2 0.2 fusion.16
  25.4 0.6 gather_fusion
  26.0 0.1 copy.16
  26.1 0.2 fusion.9
  26.4 0.1 add_bitcast_fusion
  26.5 0.6 gather_fusion.1
  27.2 0.1 copy.17
  27.3 0.6 gather_fusion.2
  27.9 0.0 copy-start.2
  27.9 0.1 copy.18
  28.0 0.6 copy-done.2
  28.6 0.1 pad_maximum_fusion.6
  28.7 0.9 broadcast_in_dim.199
  29.5 0.0 copy-start.5
  29.5 25.1 %all-to-all-start = ((f32[128,4,256]{2,1,0:T(4,128)}), f32[128,4,256]{2,1,0:T(4,128)S(1)}, u32[]{:S(2)}, u32[]{:S(2)}) async-start(f32[128,4,256]{2,1,0:T(4,128)} %broadcast_in_dim.199), calls=%async_computation | async-start | bytes 1048576 | tf_op jit(solution)/shard_map/all_to_all | solution.py:89
  54.6 0.0 copy-done.5
  54.7 0.6 copy.19
  55.3 0.1 bitcast_dynamic-update-slice_fusion.3
  55.3 0.1 bitcast_dynamic-update-slice_fusion.2
  55.4 0.1 fusion.36
  55.6 0.0 copy-start.1
  55.6 27.3 %all-to-all-done = f32[128,4,256]{2,1,0:T(4,128)S(1)} async-done(((f32[128,4,256]{2,1,0:T(4,128)}), f32[128,4,256]{2,1,0:T(4,128)S(1)}, u32[]{:S(2)}, u32[]{:S(2)}) %all-to-all-start) | async-done | bytes 524320 | tf_op jit(solution)/shard_map/all_to_all | solution.py:89
  82.9 0.2 reshape.69
  83.1 0.0 copy-done.1
  83.1 0.8 gather_fusion.3
  83.9 0.7 reshape.70.rows_ref
  84.5 4.3 %shard_map.94 = f32[16,128]{1,0:T(8,128)} custom-call(f32[256,128]{1,0:T(8,128)} %reshape.70.rows_ref, s32[128,16,128]{2,1,0:T(8,128)} %bitcast.96), custom_call_target="tpu_custom_call" | custom-call | flops 2097152 | bytes 1187840 | tf_op jit(solution)/shard_map/pallas_call | solution.py:73
  88.8 23.7 %psum.7 = f32[16,128]{1,0:T(8,128)S(1)} all-reduce(f32[16,128]{1,0:T(8,128)} %shard_map.94), channel_id=1, replica_groups=mesh['act'=4,'axial'=16,'hoop'=8] {'act'}, use_global_device_ids=true, to_apply=%region_0.1 | all-reduce | flops 2048 | bytes 16384 | tf_op jit(solution)/shard_map/psum | solution.py:128
  112.5 0.6 multiply_multiply_fusion
  (12 shorter events, 0.1 us)
Async XLA Ops:
  1.4 11.0 %copy-start = (f32[1,5,16,512]{3,2,1,0:T(8,128)S(1)}, f32[1,5,16,512]{3,2,1,0:T(8,128)}, u32[]{:S(2)}) copy-start(f32[1,5,16,512]{3,2,1,0:T(8,128)} %param.7) | copy-start | bytes 491524
  2.4 4.8 %copy-start.3 = (f32[8,6]{1,0:T(8,128)S(1)}, f32[8,6]{1,0:T(8,128)}, u32[]{:S(2)}) copy-start(f32[8,6]{1,0:T(8,128)} %param.9) | copy-start | bytes 580
  2.4 5.7 %collective-permute-start = (f32[6,6,512]{2,1,0:T(8,128)S(1)}, f32[6,6,512]{2,1,0:T(8,128)S(1)}, u32[]{:S(2)}, u32[]{:S(2)}) collective-permute-start(f32[6,6,512]{2,1,0:T(8,128)S(1)} %get-tuple-element.37), channel_id=1, source_target_pairs={{0,8},{8,16},{16,24},{24,32},{32,40},{40,48},{48,56},{56,64},{64,7... | collective-permute-start | bytes 221192 | tf_op jit(solution)/shard_map/ppermute | solution.py:17
  5.9 6.5 %collective-permute-start.1 = (f32[6,6,512]{2,1,0:T(8,128)S(1)}, f32[6,6,512]{2,1,0:T(8,128)S(1)}, u32[]{:S(2)}, u32[]{:S(2)}) collective-permute-start(f32[6,6,512]{2,1,0:T(8,128)S(1)} %get-tuple-element.38), channel_id=1, source_target_pairs={{8,0},{16,8},{24,16},{32,24},{40,32},{48,40},{56,48},{64,56},{72,6... | collective-permute-start | bytes 221192 | tf_op jit(solution)/shard_map/ppermute | solution.py:18
  7.2 0.7 copy-start.4
  12.5 7.8 %collective-permute-start.2 = (f32[6,28,6]{2,1,0:T(8,128)S(1)}, f32[6,28,6]{2,1,0:T(8,128)S(1)}, u32[]{:S(2)}, u32[]{:S(2)}) collective-permute-start(f32[6,28,6]{2,1,0:T(8,128)S(1)} %get-tuple-element.31), channel_id=1, source_target_pairs={{0,1},{1,2},{2,3},{3,4},{4,5},{5,6},{6,7},{7,0},{8,9},{9,10},{10,1... | collective-permute-start | bytes 12104 | tf_op jit(solution)/shard_map/ppermute | solution.py:20
  16.3 6.5 %collective-permute-start.3 = (f32[6,28,6]{2,1,0:T(8,128)S(1)}, f32[6,28,6]{2,1,0:T(8,128)S(1)}, u32[]{:S(2)}, u32[]{:S(2)}) collective-permute-start(f32[6,28,6]{2,1,0:T(8,128)S(1)} %get-tuple-element.32), channel_id=1, source_target_pairs={{1,0},{2,1},{3,2},{4,3},{5,4},{6,5},{7,6},{0,7},{9,8},{10,9},{11,1... | collective-permute-start | bytes 12104 | tf_op jit(solution)/shard_map/ppermute | solution.py:21
  27.9 0.7 copy-start.2
  29.5 25.1 %copy-start.5 = (s32[1,128]{1,0:T(1,128)S(1)}, s32[1,128]{1,0:T(1,128)}, u32[]{:S(2)}) copy-start(s32[1,128]{1,0:T(1,128)} %param.12) | copy-start | bytes 1540
  29.5 53.4 %all-to-all-start = ((f32[128,4,256]{2,1,0:T(4,128)}), f32[128,4,256]{2,1,0:T(4,128)S(1)}, u32[]{:S(2)}, u32[]{:S(2)}) async-start(f32[128,4,256]{2,1,0:T(4,128)} %broadcast_in_dim.199), calls=%async_computation | async-start | bytes 1048576 | tf_op jit(solution)/shard_map/all_to_all | solution.py:89
  55.6 27.5 %copy-start.1 = (f32[5,16,512]{2,1,0:T(8,128)}, f32[5,16,512]{2,1,0:T(8,128)S(1)}, u32[]{:S(2)}) copy-start(f32[5,16,512]{2,1,0:T(8,128)S(1)} %fusion.36) | copy-start | bytes 491524

commit v7 on v1

--- a/solution.py
+++ b/solution.py
@@ -83,9 +83,15 @@
     )(rows, delays)
 
 
+def a2a_gather(block, axes, count):
+    spread = jnp.broadcast_to(block[None], (count,) + block.shape)
+    gathered = lax.all_to_all(spread, axes, 0, 0, tiled=True)
+    return gathered.reshape((-1,) + block.shape[1:])
+
+
 def gather_waves(local_waves):
-    inner_waves = lax.all_gather(local_waves, "hoop", axis=0, tiled=True)
-    return lax.all_gather(inner_waves, "axial", axis=0, tiled=True)
+    inner_waves = a2a_gather(local_waves, "hoop", lax.axis_size("hoop"))
+    return a2a_gather(inner_waves, "axial", lax.axis_size("axial"))
 
 
 def per_device(wave_state, layup_zone, moduli, sensors, history, receivers, delays):
@@ -123,7 +129,10 @@
     sample_count = waveforms.shape[1]
     chosen = waveforms[receivers[0]].reshape(2 * receivers.shape[1], sample_count // 2)
     partial_value = image(chosen, delays[0])
-    summed = lax.psum(partial_value, "act")
+    parts = lax.all_gather(partial_value, "act")
+    summed = parts[0]
+    for a in range(1, parts.shape[0]):
+        summed = summed + parts[a]
     damage_map = summed * summed / (receivers.shape[1] * lax.axis_size("act"))
     return (next_state, recorded, damage_map)
 

time: 132 us -> 99.3 us (0.75)
  blocking collectives: 89.9 us -> 20.5 us
  starting transfers between devices: 20.1 us -> 37.8 us
  waiting for transfers between devices: 4.29 us -> 21.9 us
  local copies, waits for them, and re-layouts: 6.42 us -> 7.82 us
    all_gather x2 -> x1, blocking collectives: 61 us -> 20.5 us  [per_device(): parts = lax.all_gather(partial_value, 'act')]
    psum x1 -> x0, blocking collectives: 28.9 us -> none  [per_device(): summed = lax.psum(partial_value, 'act')]
    all_to_all x0 -> x2, starting transfers between devices: none -> 17.7 us  [a2a_gather(): gathered = lax.all_to_all(spread, axes, 0, 0, tiled=True)]
    all_to_all x0 -> x2, waiting for transfers between devices: none -> 17.6 us  [a2a_gather(): gathered = lax.all_to_all(spread, axes, 0, 0, tiled=True)]
    broadcast_in_dim x0 -> x3, local copies, waits for them, and re-layouts: none -> 1.5 us  [a2a_gather(): spread = jnp.broadcast_to(block[None], (count,) + block.shape)]
    unnamed x21 -> x20, local copies, waits for them, and re-layouts: 2.74 us -> 2.66 us
  transfers between devices with their start and end apart: 4 -> 6, of which waited for: 3 -> 5; matrix products, arithmetic and copies ran while one was open for 0% -> 1% of each run, Pallas kernels for 0% -> 0%
where the time goes in v7:
time: 99.3 us; the launch traced here: 98.7 us
  starting transfers between devices  37.8 us (38%)
  waiting for transfers between devices  21.9 us (22%)
  blocking collectives  20.5 us (21%)
  local copies, waits for them, and re-layouts  7.82 us (8%)
  other arithmetic  5.45 us (5%)
  Pallas kernels  4.28 us (4%)
    all_gather x1, blocking collectives, per_device(): parts = lax.all_gather(partial_value, 'act')  20.5 us
    all_to_all x2, starting transfers between devices, a2a_gather(): gathered = lax.all_to_all(spread, axes, 0, 0, tiled=True)  17.7 us
    all_to_all x2, waiting for transfers between devices, a2a_gather(): gathered = lax.all_to_all(spread, axes, 0, 0, tiled=True)  17.6 us
    ppermute x1, starting transfers between devices, exchange(): lax.ppermute(cells[:, :, :halo], 'hoop', [((j + 1) % nh, j) for j in rang...  11.3 us
    pallas_call x1, Pallas kernels, image(): pl.pallas_call(image_kernel, out_shape=jax.ShapeDtypeStruct((pix_rows, pi...  4.28 us
    ppermute x1, starting transfers between devices, exchange(): lax.ppermute(cells[:, -halo:, :], 'axial', [(i, i + 1) for i in range(na...  4.04 us
    ppermute x1, starting transfers between devices, exchange(): lax.ppermute(cells[:, :, -halo:], 'hoop', [(j, (j + 1) % nh) for j in ran...  3.55 us
    ppermute x1, waiting for transfers between devices, exchange(): lax.ppermute(cells[:, :halo, :], 'axial', [(i + 1, i) for i in range(na -...  2.69 us
  transfers between devices with their start and end apart: 6, of which 5 were waited for; matrix products, arithmetic and copies ran while one was open for 1% of the time, Pallas kernels for 0%

profile of v7, /device:TPU:1, one launch (start us, length us, event | category | flops | bytes accessed | tf_op | source)
XLA Modules:
  0.0 98.7 jit_solution(11161418594402573065)
XLA Ops:
  0.6 0.8 convert_bitcast_fusion
  1.4 0.0 copy-start
  1.4 1.0 fusion
  2.4 0.0 copy-start.3
  2.4 4.0 %collective-permute-start = (f32[6,6,512]{2,1,0:T(8,128)S(1)}, f32[6,6,512]{2,1,0:T(8,128)S(1)}, u32[]{:S(2)}, u32[]{:S(2)}) collective-permute-start(f32[6,6,512]{2,1,0:T(8,128)S(1)} %get-tuple-element.37), channel_id=1, source_target_pairs={{0,8},{8,16},{16,24},{24,32},{32,40},{40,48},{48,56},{56,64},{64,7... | collective-permute-start | bytes 221192 | tf_op jit(solution)/shard_map/ppermute | solution.py:17
  6.4 1.3 %collective-permute-start.1 = (f32[6,6,512]{2,1,0:T(8,128)S(1)}, f32[6,6,512]{2,1,0:T(8,128)S(1)}, u32[]{:S(2)}, u32[]{:S(2)}) collective-permute-start(f32[6,6,512]{2,1,0:T(8,128)S(1)} %get-tuple-element.38), channel_id=1, source_target_pairs={{8,0},{16,8},{24,16},{32,24},{40,32},{48,40},{56,48},{64,56},{72,6... | collective-permute-start | bytes 221192 | tf_op jit(solution)/shard_map/ppermute | solution.py:18
  7.7 0.0 copy-done.3
  7.8 0.0 copy-start.4
  7.8 0.6 copy-done.4
  8.4 0.0 copy-start.5
  8.4 0.6 copy-done.5
  9.1 0.0 collective-permute-done
  9.1 2.7 %collective-permute-done.1 = f32[6,6,512]{2,1,0:T(8,128)S(1)} collective-permute-done((f32[6,6,512]{2,1,0:T(8,128)S(1)}, f32[6,6,512]{2,1,0:T(8,128)S(1)}, u32[]{:S(2)}, u32[]{:S(2)}) %collective-permute-start.1) | collective-permute-done | bytes 73760 | tf_op jit(solution)/shard_map/ppermute | solution.py:18
  11.8 0.0 copy-done
  11.8 0.1 pad_maximum_fusion.4
  11.9 3.5 %collective-permute-start.2 = (f32[6,28,6]{2,1,0:T(8,128)S(1)}, f32[6,28,6]{2,1,0:T(8,128)S(1)}, u32[]{:S(2)}, u32[]{:S(2)}) collective-permute-start(f32[6,28,6]{2,1,0:T(8,128)S(1)} %get-tuple-element.31), channel_id=1, source_target_pairs={{0,1},{1,2},{2,3},{3,4},{4,5},{5,6},{6,7},{7,0},{8,9},{9,10},{10,1... | collective-permute-start | bytes 12104 | tf_op jit(solution)/shard_map/ppermute | solution.py:20
  15.5 11.3 %collective-permute-start.3 = (f32[6,28,6]{2,1,0:T(8,128)S(1)}, f32[6,28,6]{2,1,0:T(8,128)S(1)}, u32[]{:S(2)}, u32[]{:S(2)}) collective-permute-start(f32[6,28,6]{2,1,0:T(8,128)S(1)} %get-tuple-element.32), channel_id=1, source_target_pairs={{1,0},{2,1},{3,2},{4,3},{5,4},{6,5},{7,6},{0,7},{9,8},{10,9},{11,1... | collective-permute-start | bytes 12104 | tf_op jit(solution)/shard_map/ppermute | solution.py:21
  26.7 0.1 collective-permute-done.2
  26.8 1.5 %collective-permute-done.3 = f32[6,28,6]{2,1,0:T(8,128)S(1)} collective-permute-done((f32[6,28,6]{2,1,0:T(8,128)S(1)}, f32[6,28,6]{2,1,0:T(8,128)S(1)}, u32[]{:S(2)}, u32[]{:S(2)}) %collective-permute-start.3) | collective-permute-done | bytes 4064 | tf_op jit(solution)/shard_map/ppermute | solution.py:21
  28.3 0.3 pad_maximum_fusion
  28.6 0.1 compare_bitcast_fusion.7
  28.8 0.6 select_select_fusion
  29.4 0.1 slice_bitcast_fusion.6
  29.5 0.3 fusion.6
  29.8 0.2 fusion.28
  29.9 0.2 fusion.30
  30.2 0.1 fusion.31
  30.2 0.2 fusion.25
  30.5 0.2 fusion.10
  30.7 0.2 fusion.16
  30.9 0.6 gather_fusion
  31.5 0.1 copy.16
  31.6 0.2 fusion.9
  31.9 0.1 bitcast_dynamic-update-slice_fusion.3
  31.9 0.1 add_bitcast_fusion
  32.1 0.6 gather_fusion.1
  32.7 0.1 copy.17
  32.8 0.6 gather_fusion.2
  33.5 0.0 copy-start.2
  33.5 0.1 copy.18
  33.6 0.6 copy-done.2
  34.2 0.1 pad_maximum_fusion.6
  34.2 0.6 broadcast_in_dim.206
  34.9 9.7 %all-to-all-start = ((f32[8,4,256]{2,1,0:T(4,128)}), f32[8,4,256]{2,1,0:T(4,128)S(1)}, u32[]{:S(2)}, u32[]{:S(2)}) async-start(f32[8,4,256]{2,1,0:T(4,128)} %broadcast_in_dim.206), calls=%async_computation | async-start | bytes 65536 | tf_op jit(solution)/shard_map/all_to_all | solution.py:88
  44.6 0.1 bitcast_dynamic-update-slice_fusion.2
  44.7 9.4 %all-to-all-done = f32[8,4,256]{2,1,0:T(4,128)S(1)} async-done(((f32[8,4,256]{2,1,0:T(4,128)}), f32[8,4,256]{2,1,0:T(4,128)S(1)}, u32[]{:S(2)}, u32[]{:S(2)}) %all-to-all-start) | async-done | bytes 32800 | tf_op jit(solution)/shard_map/all_to_all | solution.py:88
  54.1 0.9 broadcast_in_dim.208
  54.9 8.0 %all-to-all-start.1 = ((f32[16,32,256]{2,1,0:T(8,128)}), f32[16,32,256]{2,1,0:T(8,128)S(1)}, u32[]{:S(2)}, u32[]{:S(2)}) async-start(f32[16,32,256]{2,1,0:T(8,128)} %broadcast_in_dim.208), calls=%async_computation.1 | async-start | bytes 1048576 | tf_op jit(solution)/shard_map/all_to_all | solution.py:88
  62.9 0.6 copy.19
  63.5 0.1 fusion.36
  63.6 0.0 copy-start.1
  63.6 8.2 %all-to-all-done.1 = f32[16,32,256]{2,1,0:T(8,128)S(1)} async-done(((f32[16,32,256]{2,1,0:T(8,128)}), f32[16,32,256]{2,1,0:T(8,128)S(1)}, u32[]{:S(2)}, u32[]{:S(2)}) %all-to-all-start.1) | async-done | bytes 524320 | tf_op jit(solution)/shard_map/all_to_all | solution.py:88
  71.9 0.8 gather_fusion.3
  72.6 0.0 copy-done.1
  72.6 0.7 reshape.75.rows_ref
  73.3 4.3 %shard_map.94 = f32[16,128]{1,0:T(8,128)} custom-call(f32[256,128]{1,0:T(8,128)} %reshape.75.rows_ref, s32[128,16,128]{2,1,0:T(8,128)} %bitcast.98), custom_call_target="tpu_custom_call" | custom-call | flops 2097152 | bytes 1187840 | tf_op jit(solution)/shard_map/pallas_call | solution.py:73
  77.6 20.5 %all-gather = f32[64,128]{1,0:T(8,128)S(1)} all-gather(f32[16,128]{1,0:T(8,128)} %shard_map.94), channel_id=2, replica_groups=mesh['act'=4,'axial'=16,'hoop'=8] {'act'}, dimensions={0}, use_global_device_ids=true | all-gather | bytes 40960 | tf_op jit(solution)/shard_map/all_gather | solution.py:132
  98.1 0.6 fusion.41
  (13 shorter events, 0.1 us)
Async XLA Ops:
  1.4 10.4 %copy-start = (f32[1,5,16,512]{3,2,1,0:T(8,128)S(1)}, f32[1,5,16,512]{3,2,1,0:T(8,128)}, u32[]{:S(2)}) copy-start(f32[1,5,16,512]{3,2,1,0:T(8,128)} %param.7) | copy-start | bytes 491524
  2.4 5.4 %copy-start.3 = (f32[8,6]{1,0:T(8,128)S(1)}, f32[8,6]{1,0:T(8,128)}, u32[]{:S(2)}) copy-start(f32[8,6]{1,0:T(8,128)} %param.9) | copy-start | bytes 580
  2.4 6.7 %collective-permute-start = (f32[6,6,512]{2,1,0:T(8,128)S(1)}, f32[6,6,512]{2,1,0:T(8,128)S(1)}, u32[]{:S(2)}, u32[]{:S(2)}) collective-permute-start(f32[6,6,512]{2,1,0:T(8,128)S(1)} %get-tuple-element.37), channel_id=1, source_target_pairs={{0,8},{8,16},{16,24},{24,32},{32,40},{40,48},{48,56},{56,64},{64,7... | collective-permute-start | bytes 221192 | tf_op jit(solution)/shard_map/ppermute | solution.py:17
  6.4 5.4 %collective-permute-start.1 = (f32[6,6,512]{2,1,0:T(8,128)S(1)}, f32[6,6,512]{2,1,0:T(8,128)S(1)}, u32[]{:S(2)}, u32[]{:S(2)}) collective-permute-start(f32[6,6,512]{2,1,0:T(8,128)S(1)} %get-tuple-element.38), channel_id=1, source_target_pairs={{8,0},{16,8},{24,16},{32,24},{40,32},{48,40},{56,48},{64,56},{72,6... | collective-permute-start | bytes 221192 | tf_op jit(solution)/shard_map/ppermute | solution.py:18
  7.8 0.7 copy-start.4
  8.4 0.7 copy-start.5
  11.9 14.9 %collective-permute-start.2 = (f32[6,28,6]{2,1,0:T(8,128)S(1)}, f32[6,28,6]{2,1,0:T(8,128)S(1)}, u32[]{:S(2)}, u32[]{:S(2)}) collective-permute-start(f32[6,28,6]{2,1,0:T(8,128)S(1)} %get-tuple-element.31), channel_id=1, source_target_pairs={{0,1},{1,2},{2,3},{3,4},{4,5},{5,6},{6,7},{7,0},{8,9},{9,10},{10,1... | collective-permute-start | bytes 12104 | tf_op jit(solution)/shard_map/ppermute | solution.py:20
  15.5 12.9 %collective-permute-start.3 = (f32[6,28,6]{2,1,0:T(8,128)S(1)}, f32[6,28,6]{2,1,0:T(8,128)S(1)}, u32[]{:S(2)}, u32[]{:S(2)}) collective-permute-start(f32[6,28,6]{2,1,0:T(8,128)S(1)} %get-tuple-element.32), channel_id=1, source_target_pairs={{1,0},{2,1},{3,2},{4,3},{5,4},{6,5},{7,6},{0,7},{9,8},{10,9},{11,1... | collective-permute-start | bytes 12104 | tf_op jit(solution)/shard_map/ppermute | solution.py:21
  33.5 0.7 copy-start.2
  34.9 19.2 %all-to-all-start = ((f32[8,4,256]{2,1,0:T(4,128)}), f32[8,4,256]{2,1,0:T(4,128)S(1)}, u32[]{:S(2)}, u32[]{:S(2)}) async-start(f32[8,4,256]{2,1,0:T(4,128)} %broadcast_in_dim.206), calls=%async_computation | async-start | bytes 65536 | tf_op jit(solution)/shard_map/all_to_all | solution.py:88
  54.9 16.9 %all-to-all-start.1 = ((f32[16,32,256]{2,1,0:T(8,128)}), f32[16,32,256]{2,1,0:T(8,128)S(1)}, u32[]{:S(2)}, u32[]{:S(2)}) async-start(f32[16,32,256]{2,1,0:T(8,128)} %broadcast_in_dim.208), calls=%async_computation.1 | async-start | bytes 1048576 | tf_op jit(solution)/shard_map/all_to_all | solution.py:88
  63.6 9.0 %copy-start.1 = (f32[5,16,512]{2,1,0:T(8,128)}, f32[5,16,512]{2,1,0:T(8,128)S(1)}, u32[]{:S(2)}) copy-start(f32[5,16,512]{2,1,0:T(8,128)S(1)} %fusion.36) | copy-start | bytes 491524

commit v8 on v7

--- a/solution.py
+++ b/solution.py
@@ -11,15 +11,20 @@
 HALO = 2 * STEPS
 
 
-def exchange(cells, halo):
+def exchange(cells, zone, halo):
     na = lax.axis_size("axial")
     nh = lax.axis_size("hoop")
-    from_above = lax.ppermute(cells[:, -halo:, :], "axial", [(i, i + 1) for i in range(na - 1)])
-    from_below = lax.ppermute(cells[:, :halo, :], "axial", [(i + 1, i) for i in range(na - 1)])
-    cells = jnp.concatenate([from_above, cells, from_below], axis=1)
-    from_left = lax.ppermute(cells[:, :, -halo:], "hoop", [(j, (j + 1) % nh) for j in range(nh)])
-    from_right = lax.ppermute(cells[:, :, :halo], "hoop", [((j + 1) % nh, j) for j in range(nh)])
-    return jnp.concatenate([from_left, cells, from_right], axis=2)
+
+    def rows_of(lo, hi):
+        return jnp.concatenate([cells[:, lo:hi, :], zone[None, lo:hi, :]], axis=0)
+
+    rows = cells.shape[1]
+    from_above = lax.ppermute(rows_of(rows - halo, rows), "axial", [(i, i + 1) for i in range(na - 1)])
+    from_below = lax.ppermute(rows_of(0, halo), "axial", [(i + 1, i) for i in range(na - 1)])
+    full = jnp.concatenate([from_above, rows_of(0, rows), from_below], axis=1)
+    from_left = lax.ppermute(full[:, :, -halo:], "hoop", [(j, (j + 1) % nh) for j in range(nh)])
+    from_right = lax.ppermute(full[:, :, :halo], "hoop", [((j + 1) % nh, j) for j in range(nh)])
+    return jnp.concatenate([from_left, full, from_right], axis=2)
 
 
 def inner(f):
@@ -51,36 +56,49 @@
     return (va_c, vh_c, normal_axial, normal_hoop, shear_stress), m
 
 
-def image_kernel(rows_ref, delays_ref, out_ref):
+def image_kernel(receivers_ref, waves_ref, delays_ref, out_ref):
     pairs, pix_rows, pix_cols = delays_ref.shape
-    lanes = rows_ref.shape[1]
+    lanes = pix_cols
+    tile = 8
 
     def body(k, acc):
-        d = delays_ref[k]
-        low = jnp.broadcast_to(rows_ref[pl.ds(2 * k, 1), :], (pix_rows, pix_cols))
-        high = jnp.broadcast_to(rows_ref[pl.ds(2 * k + 1, 1), :], (pix_rows, pix_cols))
-        idx = d & (lanes - 1)
-        got_low = jnp.take_along_axis(low, idx, axis=1, mode="promise_in_bounds")
-        got_high = jnp.take_along_axis(high, idx, axis=1, mode="promise_in_bounds")
-        return acc + jnp.where(d >= lanes, got_high, got_low)
+        row = receivers_ref[k]
+        base = pl.multiple_of((row // tile) * tile, tile)
+        block = waves_ref[pl.ds(base, tile), :]
+        pick = jnp.full(block.shape, row % tile, jnp.int32)
+        spread = jnp.take_along_axis(block, pick, axis=0, mode="promise_in_bounds")
+        low = spread[:, :lanes]
+        high = spread[:, lanes:]
+        parts = []
+        for h in range(pix_rows // tile):
+            d = delays_ref[k, pl.ds(h * tile, tile), :]
+            idx = d & (lanes - 1)
+            got_low = jnp.take_along_axis(low, idx, axis=1, mode="promise_in_bounds")
+            got_high = jnp.take_along_axis(high, idx, axis=1, mode="promise_in_bounds")
+            parts.append(jnp.where(d >= lanes, got_high, got_low))
+        return acc + jnp.concatenate(parts, axis=0)
 
     acc = lax.fori_loop(0, pairs, body, jnp.zeros((pix_rows, pix_cols), jnp.float32), unroll=8)
     out_ref[...] = acc
 
 
-def image(rows, delays):
+def image(receivers, waves, delays):
     pairs, pix_rows, pix_cols = delays.shape
     return pl.pallas_call(
         image_kernel,
         out_shape=jax.ShapeDtypeStruct((pix_rows, pix_cols), jnp.float32),
-        in_specs=[pl.BlockSpec(memory_space=pltpu.VMEM)] * 2,
+        in_specs=[
+            pl.BlockSpec(memory_space=pltpu.SMEM),
+            pl.BlockSpec(memory_space=pltpu.VMEM),
+            pl.BlockSpec(memory_space=pltpu.VMEM),
+        ],
         out_specs=pl.BlockSpec(memory_space=pltpu.VMEM),
         cost_estimate=pl.CostEstimate(
             flops=8 * pairs * pix_rows * pix_cols,
-            bytes_accessed=4 * (rows.size + delays.size + pix_rows * pix_cols),
+            bytes_accessed=4 * (waves.size + delays.size + pix_rows * pix_cols),
             transcendentals=0,
         ),
-    )(rows, delays)
+    )(receivers, waves, delays)
 
 
 def a2a_gather(block, axes, count):
@@ -97,10 +115,7 @@
 def per_device(wave_state, layup_zone, moduli, sensors, history, receivers, delays):
     rows, cols = layup_zone.shape
     na = lax.axis_size("axial")
-    stacked = jnp.concatenate(
-        [wave_state[0], layup_zone.astype(jnp.float32)[None]], axis=0
-    )
-    padded = exchange(stacked, HALO)
+    padded = exchange(wave_state[0], layup_zone.astype(jnp.float32), HALO)
     zone = padded[5].astype(jnp.int32)
     global_row = lax.axis_index("axial") * rows - HALO + lax.broadcasted_iota(
         jnp.int32, zone.shape, 0
@@ -113,22 +128,19 @@
         )
     moduli_map = jnp.where(inside[None], moduli_map, jnp.float32(0.0))
     fields = tuple(padded[c] for c in range(5))
-    samples = []
+    totals = []
     for step_index in range(STEPS):
         fields, moduli_map = advance(fields, moduli_map)
         moduli_map = [inner(m) for m in moduli_map]
         off = HALO - 2 * (step_index + 1)
         total = fields[2] + fields[3]
-        tile = total[off:off + rows, off:off + cols]
-        samples.append(tile.reshape(-1)[sensors])
+        totals.append(total[off:off + rows, off:off + cols])
         moduli_map = jnp.stack(moduli_map)
     next_state = jnp.stack(fields)[None]
-    recorded = jnp.stack(samples, axis=1)[None]
+    recorded = jnp.stack(totals).reshape(STEPS, rows * cols)[:, sensors].T[None]
     local_waves = jnp.concatenate([history[0], recorded[0]], axis=1)
     waveforms = gather_waves(local_waves)
-    sample_count = waveforms.shape[1]
-    chosen = waveforms[receivers[0]].reshape(2 * receivers.shape[1], sample_count // 2)
-    partial_value = image(chosen, delays[0])
+    partial_value = image(receivers[0], waveforms, delays[0])
     parts = lax.all_gather(partial_value, "act")
     summed = parts[0]
     for a in range(1, parts.shape[0]):

time: 99.3 us -> 105 us (1.057)
  waiting for transfers between devices: 21.9 us -> 27.5 us
  starting transfers between devices: 37.8 us -> 33.5 us
  local copies, waits for them, and re-layouts: 7.82 us -> 10.6 us
  other arithmetic: 5.45 us -> 6.92 us
    ppermute x4, waiting for transfers between devices: 4.29 us -> 10 us  [the longest x1 10 us: exchange(): lax.ppermute(full[:, :, -halo:], 'hoop', [(j, (j + 1) % nh) for j in rang...]
    all_to_all x2, starting transfers between devices: 17.7 us -> 12.6 us  [a2a_gather(): gathered = lax.all_to_all(spread, axes, 0, 0, tiled=True)]
    another operation x3 -> x1, local copies, waits for them, and re-layouts: 0.28 us -> 2.62 us  [per_device(): recorded = jnp.stack(totals).reshape(STEPS, rows * cols)[:, sensors].T[None]]
    unnamed x20 -> x14, local copies, waits for them, and re-layouts: 2.66 us -> 1.73 us
    gather x4 -> x1, local copies, waits for them, and re-layouts: 2.65 us -> 2.74 us  [per_device(): recorded = jnp.stack(totals).reshape(STEPS, rows * cols)[:, sensors].T[None]]
  transfers between devices with their start and end apart: 6 -> 6, of which waited for: 5 -> 3; matrix products, arithmetic and copies ran while one was open for 1% -> 2% of each run, Pallas kernels for 0% -> 0%
where the time goes in v8:
time: 105 us; the launch traced here: 104 us
  starting transfers between devices  33.5 us (32%)
  waiting for transfers between devices  27.5 us (26%)
  blocking collectives  20 us (19%)
  local copies, waits for them, and re-layouts  10.6 us (10%)
  other arithmetic  6.92 us (7%)
  Pallas kernels  4.41 us (4%)
    all_gather x1, blocking collectives, per_device(): parts = lax.all_gather(partial_value, 'act')  20 us
    all_to_all x2, waiting for transfers between devices, a2a_gather(): gathered = lax.all_to_all(spread, axes, 0, 0, tiled=True)  17.5 us
    ppermute x1, starting transfers between devices, exchange(): lax.ppermute(full[:, :, :halo], 'hoop', [((j + 1) % nh, j) for j in range...  13 us
    all_to_all x2, starting transfers between devices, a2a_gather(): gathered = lax.all_to_all(spread, axes, 0, 0, tiled=True)  12.6 us
    ppermute x1, waiting for transfers between devices, exchange(): lax.ppermute(full[:, :, -halo:], 'hoop', [(j, (j + 1) % nh) for j in rang...  10 us
    ppermute x1, starting transfers between devices, exchange(): lax.ppermute(rows_of(rows - halo, rows), 'axial', [(i, i + 1) for i in ra...  4.66 us
    pallas_call x1, Pallas kernels, image(): pl.pallas_call(image_kernel, out_shape=jax.ShapeDtypeStruct((pix_rows, pi...  4.41 us
    gather x1, local copies, waits for them, and re-layouts, per_device(): recorded = jnp.stack(totals).reshape(STEPS, rows * cols)[:, sensors].T[None]  2.74 us
  transfers between devices with their start and end apart: 6, of which 3 were waited for; matrix products, arithmetic and copies ran while one was open for 2% of the time, Pallas kernels for 0%

profile of v8, /device:TPU:1, one launch (start us, length us, event | category | flops | bytes accessed | tf_op | source)
XLA Modules:
  0.0 103.9 jit_solution(12301984784913198548)
XLA Ops:
  0.6 0.8 convert_bitcast_fusion
  1.4 0.9 fusion.43
  2.4 1.3 %collective-permute-start.1 = (f32[6,6,512]{2,1,0:T(8,128)S(1)}, f32[6,6,512]{2,1,0:T(8,128)S(1)}, u32[]{:S(2)}, u32[]{:S(2)}) collective-permute-start(f32[6,6,512]{2,1,0:T(8,128)S(1)} %pad_maximum_fusion.7), channel_id=1, source_target_pairs={{8,0},{16,8},{24,16},{32,24},{40,32},{48,40},{56,48},{64,56},{72,6... | collective-permute-start | bytes 221192 | tf_op jit(solution)/shard_map/ppermute | solution.py:23
  3.7 4.7 %collective-permute-start = (f32[6,6,512]{2,1,0:T(8,128)S(1)}, f32[6,6,512]{2,1,0:T(8,128)S(1)}, u32[]{:S(2)}, u32[]{:S(2)}) collective-permute-start(f32[6,6,512]{2,1,0:T(8,128)S(1)} %pad_maximum_fusion.6), channel_id=1, source_target_pairs={{0,8},{8,16},{16,24},{24,32},{32,40},{40,48},{48,56},{56,64},{64,7... | collective-permute-start | bytes 221192 | tf_op jit(solution)/shard_map/ppermute | solution.py:22
  8.4 1.0 slice_bitcast_fusion.20
  9.4 0.7 compare_select_fusion
  10.0 0.0 collective-permute-done.1
  10.0 0.0 collective-permute-done
  10.0 0.9 pad_maximum_fusion.5
  11.0 13.0 %collective-permute-start.3 = (f32[6,28,6]{2,1,0:T(8,128)S(1)}, f32[6,28,6]{2,1,0:T(8,128)S(1)}, u32[]{:S(2)}, u32[]{:S(2)}) collective-permute-start(f32[6,28,6]{2,1,0:T(8,128)S(1)} %get-tuple-element.35), channel_id=1, source_target_pairs={{1,0},{2,1},{3,2},{4,3},{5,4},{6,5},{7,6},{0,7},{9,8},{10,9},{11,1... | collective-permute-start | bytes 12104 | tf_op jit(solution)/shard_map/ppermute | solution.py:26
  24.0 1.9 %collective-permute-start.2 = (f32[6,28,6]{2,1,0:T(8,128)S(1)}, f32[6,28,6]{2,1,0:T(8,128)S(1)}, u32[]{:S(2)}, u32[]{:S(2)}) collective-permute-start(f32[6,28,6]{2,1,0:T(8,128)S(1)} %get-tuple-element.34), channel_id=1, source_target_pairs={{0,1},{1,2},{2,3},{3,4},{4,5},{5,6},{6,7},{7,0},{8,9},{9,10},{10,1... | collective-permute-start | bytes 12104 | tf_op jit(solution)/shard_map/ppermute | solution.py:25
  25.9 0.0 collective-permute-done.3
  26.0 10.0 %collective-permute-done.2 = f32[6,28,6]{2,1,0:T(8,128)S(1)} collective-permute-done((f32[6,28,6]{2,1,0:T(8,128)S(1)}, f32[6,28,6]{2,1,0:T(8,128)S(1)}, u32[]{:S(2)}, u32[]{:S(2)}) %collective-permute-start.2) | collective-permute-done | bytes 4064 | tf_op jit(solution)/shard_map/ppermute | solution.py:25
  36.0 1.2 %pad_maximum_fusion = f32[6,28,524]{2,1,0:T(8,128)S(1)} fusion(f32[6,28,6]{2,1,0:T(8,128)S(1)} %collective-permute-done.3, f32[6,6,512]{2,1,0:T(8,128)S(1)} %collective-permute-done.1, f32[1,16,512]{2,1,0:T(8,128)S(1)} %get-tuple-element.49, f32[5,16,512]{2,1,0:T(8,128)} %bitcast.94, f32[6,6,512]{2,1,0:T(8,128)S(1)} %collective-permute-done, ...), kind=kLoop, calls=%fused_computation.1 | loop fusion | flops 440160 | bytes 704256 | tf_op jit(solution)/shard_map/concatenate | solution.py:27
  37.2 0.1 compare_bitcast_fusion.7
  37.3 0.6 select_select_fusion
  37.9 0.1 slice_bitcast_fusion.6
  38.0 0.3 fusion.5
  38.3 0.2 fusion.27
  38.5 0.2 fusion.29
  38.7 0.0 copy-start.2
  38.7 0.2 fusion.24
  38.9 0.2 fusion.15
  39.1 0.2 fusion.9
  39.3 0.1 fusion.30
  39.4 0.2 fusion.8
  39.6 0.1 bitcast_dynamic-update-slice_fusion.3
  39.7 0.1 add_bitcast_fusion
  40.0 0.1 pad_maximum_fusion.1
  40.1 2.6 %copy.15 = f32[3,8192]{0,1:T(8,128)} copy(f32[3,8192]{1,0:T(4,128)S(1)} %pad_maximum_fusion.1) | data formatting | bytes 196608 | tf_op jit(solution)/shard_map/stack | solution.py:140
  42.7 2.7 %gather_fusion = f32[4,3]{1,0:T(4,128)S(1)} fusion(f32[3,8192]{0,1:T(8,128)} %copy.15, s32[1024]{0:T(1024)S(1)} %pad_clamp_fusion), kind=kCustom, calls=%fused_computation | custom fusion | bytes 112 | tf_op jit(solution)/shard_map/gather | solution.py:140
  45.5 0.0 copy-done.2
  45.5 0.1 pad_maximum_fusion.8
  45.5 0.6 broadcast_in_dim.211
  46.2 3.3 %all-to-all-start = ((f32[8,4,256]{2,1,0:T(4,128)}), f32[8,4,256]{2,1,0:T(4,128)S(1)}, u32[]{:S(2)}, u32[]{:S(2)}) async-start(f32[8,4,256]{2,1,0:T(4,128)} %broadcast_in_dim.211), calls=%async_computation | async-start | bytes 65536 | tf_op jit(solution)/shard_map/all_to_all | solution.py:106
  49.5 0.1 bitcast_dynamic-update-slice_fusion.2
  49.6 9.3 %all-to-all-done = f32[8,4,256]{2,1,0:T(4,128)S(1)} async-done(((f32[8,4,256]{2,1,0:T(4,128)}), f32[8,4,256]{2,1,0:T(4,128)S(1)}, u32[]{:S(2)}, u32[]{:S(2)}) %all-to-all-start) | async-done | bytes 32800 | tf_op jit(solution)/shard_map/all_to_all | solution.py:106
  58.9 0.9 broadcast_in_dim.213
  59.8 9.3 %all-to-all-start.1 = ((f32[16,32,256]{2,1,0:T(8,128)}), f32[16,32,256]{2,1,0:T(8,128)S(1)}, u32[]{:S(2)}, u32[]{:S(2)}) async-start(f32[16,32,256]{2,1,0:T(8,128)} %broadcast_in_dim.213), calls=%async_computation.1 | async-start | bytes 1048576 | tf_op jit(solution)/shard_map/all_to_all | solution.py:106
  69.1 0.6 copy.16
  69.7 0.1 fusion.35
  69.9 0.0 copy-start.1
  69.9 8.1 %all-to-all-done.1 = f32[16,32,256]{2,1,0:T(8,128)S(1)} async-done(((f32[16,32,256]{2,1,0:T(8,128)}), f32[16,32,256]{2,1,0:T(8,128)S(1)}, u32[]{:S(2)}, u32[]{:S(2)}) %all-to-all-start.1) | async-done | bytes 524320 | tf_op jit(solution)/shard_map/all_to_all | solution.py:106
  78.0 0.0 copy-start
  78.0 0.8 copy-done
  78.8 4.4 %shard_map.94 = f32[16,128]{1,0:T(8,128)} custom-call(s32[128]{0:T(128)} %bitcast.102, f32[512,256]{1,0:T(8,128)} %bitcast.91, s32[128,16,128]{2,1,0:T(8,128)} %bitcast.95), custom_call_target="tpu_custom_call" | custom-call | flops 2097152 | bytes 1581056 | tf_op jit(solution)/shard_map/pallas_call | solution.py:87
  83.2 20.0 %all-gather = f32[64,128]{1,0:T(8,128)S(1)} all-gather(f32[16,128]{1,0:T(8,128)} %shard_map.94), channel_id=2, replica_groups=mesh['act'=4,'axial'=16,'hoop'=8] {'act'}, dimensions={0}, use_global_device_ids=true | all-gather | bytes 40960 | tf_op jit(solution)/shard_map/all_gather | solution.py:144
  103.3 0.6 fusion.40
  103.9 0.0 copy-done.1
  (11 shorter events, 0.2 us)
Async XLA Ops:
  2.4 7.7 %collective-permute-start.1 = (f32[6,6,512]{2,1,0:T(8,128)S(1)}, f32[6,6,512]{2,1,0:T(8,128)S(1)}, u32[]{:S(2)}, u32[]{:S(2)}) collective-permute-start(f32[6,6,512]{2,1,0:T(8,128)S(1)} %pad_maximum_fusion.7), channel_id=1, source_target_pairs={{8,0},{16,8},{24,16},{32,24},{40,32},{48,40},{56,48},{64,56},{72,6... | collective-permute-start | bytes 221192 | tf_op jit(solution)/shard_map/ppermute | solution.py:23
  3.7 6.3 %collective-permute-start = (f32[6,6,512]{2,1,0:T(8,128)S(1)}, f32[6,6,512]{2,1,0:T(8,128)S(1)}, u32[]{:S(2)}, u32[]{:S(2)}) collective-permute-start(f32[6,6,512]{2,1,0:T(8,128)S(1)} %pad_maximum_fusion.6), channel_id=1, source_target_pairs={{0,8},{8,16},{16,24},{24,32},{32,40},{40,48},{48,56},{56,64},{64,7... | collective-permute-start | bytes 221192 | tf_op jit(solution)/shard_map/ppermute | solution.py:22
  11.0 15.0 %collective-permute-start.3 = (f32[6,28,6]{2,1,0:T(8,128)S(1)}, f32[6,28,6]{2,1,0:T(8,128)S(1)}, u32[]{:S(2)}, u32[]{:S(2)}) collective-permute-start(f32[6,28,6]{2,1,0:T(8,128)S(1)} %get-tuple-element.35), channel_id=1, source_target_pairs={{1,0},{2,1},{3,2},{4,3},{5,4},{6,5},{7,6},{0,7},{9,8},{10,9},{11,1... | collective-permute-start | bytes 12104 | tf_op jit(solution)/shard_map/ppermute | solution.py:26
  24.0 12.0 %collective-permute-start.2 = (f32[6,28,6]{2,1,0:T(8,128)S(1)}, f32[6,28,6]{2,1,0:T(8,128)S(1)}, u32[]{:S(2)}, u32[]{:S(2)}) collective-permute-start(f32[6,28,6]{2,1,0:T(8,128)S(1)} %get-tuple-element.34), channel_id=1, source_target_pairs={{0,1},{1,2},{2,3},{3,4},{4,5},{5,6},{6,7},{7,0},{8,9},{9,10},{10,1... | collective-permute-start | bytes 12104 | tf_op jit(solution)/shard_map/ppermute | solution.py:25
  38.7 6.8 %copy-start.2 = (f32[1,4,253]{2,1,0:T(4,128)S(1)}, f32[1,4,253]{2,1,0:T(4,128)}, u32[]{:S(2)}) copy-start(f32[1,4,253]{2,1,0:T(4,128)} %param.11) | copy-start | bytes 12148
  46.2 12.8 %all-to-all-start = ((f32[8,4,256]{2,1,0:T(4,128)}), f32[8,4,256]{2,1,0:T(4,128)S(1)}, u32[]{:S(2)}, u32[]{:S(2)}) async-start(f32[8,4,256]{2,1,0:T(4,128)} %broadcast_in_dim.211), calls=%async_computation | async-start | bytes 65536 | tf_op jit(solution)/shard_map/all_to_all | solution.py:106
  59.8 18.2 %all-to-all-start.1 = ((f32[16,32,256]{2,1,0:T(8,128)}), f32[16,32,256]{2,1,0:T(8,128)S(1)}, u32[]{:S(2)}, u32[]{:S(2)}) async-start(f32[16,32,256]{2,1,0:T(8,128)} %broadcast_in_dim.213), calls=%async_computation.1 | async-start | bytes 1048576 | tf_op jit(solution)/shard_map/all_to_all | solution.py:106
  69.9 34.0 %copy-start.1 = (f32[5,16,512]{2,1,0:T(8,128)}, f32[5,16,512]{2,1,0:T(8,128)S(1)}, u32[]{:S(2)}) copy-start(f32[5,16,512]{2,1,0:T(8,128)S(1)} %fusion.35) | copy-start | bytes 491524
  78.0 0.8 copy-start

commit v9 on v8

--- a/solution.py
+++ b/solution.py
@@ -11,20 +11,15 @@
 HALO = 2 * STEPS
 
 
-def exchange(cells, zone, halo):
+def exchange(cells, halo):
     na = lax.axis_size("axial")
     nh = lax.axis_size("hoop")
-
-    def rows_of(lo, hi):
-        return jnp.concatenate([cells[:, lo:hi, :], zone[None, lo:hi, :]], axis=0)
-
-    rows = cells.shape[1]
-    from_above = lax.ppermute(rows_of(rows - halo, rows), "axial", [(i, i + 1) for i in range(na - 1)])
-    from_below = lax.ppermute(rows_of(0, halo), "axial", [(i + 1, i) for i in range(na - 1)])
-    full = jnp.concatenate([from_above, rows_of(0, rows), from_below], axis=1)
-    from_left = lax.ppermute(full[:, :, -halo:], "hoop", [(j, (j + 1) % nh) for j in range(nh)])
-    from_right = lax.ppermute(full[:, :, :halo], "hoop", [((j + 1) % nh, j) for j in range(nh)])
-    return jnp.concatenate([from_left, full, from_right], axis=2)
+    from_left = lax.ppermute(cells[:, :, -halo:], "hoop", [(j, (j + 1) % nh) for j in range(nh)])
+    from_right = lax.ppermute(cells[:, :, :halo], "hoop", [((j + 1) % nh, j) for j in range(nh)])
+    cells = jnp.concatenate([from_left, cells, from_right], axis=2)
+    from_above = lax.ppermute(cells[:, -halo:, :], "axial", [(i, i + 1) for i in range(na - 1)])
+    from_below = lax.ppermute(cells[:, :halo, :], "axial", [(i + 1, i) for i in range(na - 1)])
+    return jnp.concatenate([from_above, cells, from_below], axis=1)
 
 
 def inner(f):
@@ -115,7 +110,10 @@
 def per_device(wave_state, layup_zone, moduli, sensors, history, receivers, delays):
     rows, cols = layup_zone.shape
     na = lax.axis_size("axial")
-    padded = exchange(wave_state[0], layup_zone.astype(jnp.float32), HALO)
+    stacked = jnp.concatenate(
+        [wave_state[0], layup_zone.astype(jnp.float32)[None]], axis=0
+    )
+    padded = exchange(stacked, HALO)
     zone = padded[5].astype(jnp.int32)
     global_row = lax.axis_index("axial") * rows - HALO + lax.broadcasted_iota(
         jnp.int32, zone.shape, 0
@@ -128,16 +126,17 @@
         )
     moduli_map = jnp.where(inside[None], moduli_map, jnp.float32(0.0))
     fields = tuple(padded[c] for c in range(5))
-    totals = []
+    samples = []
     for step_index in range(STEPS):
         fields, moduli_map = advance(fields, moduli_map)
         moduli_map = [inner(m) for m in moduli_map]
         off = HALO - 2 * (step_index + 1)
         total = fields[2] + fields[3]
-        totals.append(total[off:off + rows, off:off + cols])
+        tile = total[off:off + rows, off:off + cols]
+        samples.append(tile.reshape(-1)[sensors])
         moduli_map = jnp.stack(moduli_map)
     next_state = jnp.stack(fields)[None]
-    recorded = jnp.stack(totals).reshape(STEPS, rows * cols)[:, sensors].T[None]
+    recorded = jnp.stack(samples, axis=1)[None]
     local_waves = jnp.concatenate([history[0], recorded[0]], axis=1)
     waveforms = gather_waves(local_waves)
     partial_value = image(receivers[0], waveforms, delays[0])

time: 105 us -> 98.4 us (0.937)
  local copies, waits for them, and re-layouts: 10.6 us -> 5.95 us
  waiting for transfers between devices: 27.5 us -> 23 us
  starting transfers between devices: 33.5 us -> 37.7 us
  other arithmetic: 6.92 us -> 5.3 us
    all_to_all x2, starting transfers between devices: 12.6 us -> 17.6 us  [a2a_gather(): gathered = lax.all_to_all(spread, axes, 0, 0, tiled=True)]
    ppermute x4, waiting for transfers between devices: 10 us -> 5.39 us  [the longest x1 3.78 us: exchange(): lax.ppermute(cells[:, :halo, :], 'axial', [(i + 1, i) for i in range(na -...]
    another operation x1 -> x3, local copies, waits for them, and re-layouts: 2.62 us -> 0.28 us  [per_device(): recorded = jnp.stack(samples, axis=1)[None]]
    gather x1 -> x3, local copies, waits for them, and re-layouts: 2.74 us -> 1.9 us  [per_device(): samples.append(tile.reshape(-1)[sensors])]
    unnamed x14 -> x20, local copies, waits for them, and re-layouts: 1.73 us -> 2.17 us
  transfers between devices with their start and end apart: 6 -> 6, of which waited for: 3 -> 5; matrix products, arithmetic and copies ran while one was open for 2% -> 1% of each run, Pallas kernels for 0% -> 0%
where the time goes in v9:
time: 98.4 us; the launch traced here: 97.8 us
  starting transfers between devices  37.7 us (38%)
  waiting for transfers between devices  23 us (23%)
  blocking collectives  20.5 us (21%)
  local copies, waits for them, and re-layouts  5.95 us (6%)
  other arithmetic  5.3 us (5%)
  Pallas kernels  4.41 us (4%)
    all_gather x1, blocking collectives, per_device(): parts = lax.all_gather(partial_value, 'act')  20.5 us
    all_to_all x2, waiting for transfers between devices, a2a_gather(): gathered = lax.all_to_all(spread, axes, 0, 0, tiled=True)  17.6 us
    all_to_all x2, starting transfers between devices, a2a_gather(): gathered = lax.all_to_all(spread, axes, 0, 0, tiled=True)  17.6 us
    ppermute x1, starting transfers between devices, exchange(): lax.ppermute(cells[:, :, :halo], 'hoop', [((j + 1) % nh, j) for j in rang...  11.3 us
    pallas_call x1, Pallas kernels, image(): pl.pallas_call(image_kernel, out_shape=jax.ShapeDtypeStruct((pix_rows, pi...  4.41 us
    ppermute x1, starting transfers between devices, exchange(): lax.ppermute(cells[:, :, -halo:], 'hoop', [(j, (j + 1) % nh) for j in ran...  4.37 us
    ppermute x1, waiting for transfers between devices, exchange(): lax.ppermute(cells[:, :halo, :], 'axial', [(i + 1, i) for i in range(na -...  3.78 us
    ppermute x1, starting transfers between devices, exchange(): lax.ppermute(cells[:, -halo:, :], 'axial', [(i, i + 1) for i in range(na...  3.21 us
  transfers between devices with their start and end apart: 6, of which 5 were waited for; matrix products, arithmetic and copies ran while one was open for 1% of the time, Pallas kernels for 0%

profile of v9, /device:TPU:1, one launch (start us, length us, event | category | flops | bytes accessed | tf_op | source)
XLA Modules:
  0.0 97.8 jit_solution(7755608450011778697)
XLA Ops:
  0.6 0.8 convert_bitcast_fusion
  1.4 0.0 copy-start.1
  1.4 0.0 copy-start.4
  1.4 0.9 pad_maximum_fusion.3
  2.3 4.4 %collective-permute-start = (f32[6,16,6]{2,1,0:T(8,128)S(1)}, f32[6,16,6]{2,1,0:T(8,128)S(1)}, u32[]{:S(2)}, u32[]{:S(2)}) collective-permute-start(f32[6,16,6]{2,1,0:T(8,128)S(1)} %get-tuple-element.37), channel_id=1, source_target_pairs={{0,1},{1,2},{2,3},{3,4},{4,5},{5,6},{6,7},{7,0},{8,9},{9,10},{10,1... | collective-permute-start | bytes 6920 | tf_op jit(solution)/shard_map/ppermute | solution.py:17
  6.7 0.0 copy-start.5
  6.7 11.3 %collective-permute-start.1 = (f32[6,16,6]{2,1,0:T(8,128)S(1)}, f32[6,16,6]{2,1,0:T(8,128)S(1)}, u32[]{:S(2)}, u32[]{:S(2)}) collective-permute-start(f32[6,16,6]{2,1,0:T(8,128)S(1)} %get-tuple-element.38), channel_id=1, source_target_pairs={{1,0},{2,1},{3,2},{4,3},{5,4},{6,5},{7,6},{0,7},{9,8},{10,9},{11,1... | collective-permute-start | bytes 6920 | tf_op jit(solution)/shard_map/ppermute | solution.py:18
  18.0 0.0 copy-done.4
  18.0 0.0 copy-done.5
  18.0 0.0 collective-permute-done
  18.1 1.1 %collective-permute-done.1 = f32[6,16,6]{2,1,0:T(8,128)S(1)} collective-permute-done((f32[6,16,6]{2,1,0:T(8,128)S(1)}, f32[6,16,6]{2,1,0:T(8,128)S(1)}, u32[]{:S(2)}, u32[]{:S(2)}) %collective-permute-start.1) | collective-permute-done | bytes 2336 | tf_op jit(solution)/shard_map/ppermute | solution.py:18
  19.1 0.0 copy-done.1
  19.1 0.1 pad_maximum_fusion.1
  19.3 3.2 %collective-permute-start.2 = (f32[6,6,524]{2,1,0:T(8,128)S(1)}, f32[6,6,524]{2,1,0:T(8,128)S(1)}, u32[]{:S(2)}, u32[]{:S(2)}) collective-permute-start(f32[6,6,524]{2,1,0:T(8,128)S(1)} %get-tuple-element.33), channel_id=1, source_target_pairs={{0,8},{8,16},{16,24},{24,32},{32,40},{40,48},{48,56},{56,64},{64,7... | collective-permute-start | bytes 226376 | tf_op jit(solution)/shard_map/ppermute | solution.py:20
  22.5 1.3 %collective-permute-start.3 = (f32[6,6,524]{2,1,0:T(8,128)S(1)}, f32[6,6,524]{2,1,0:T(8,128)S(1)}, u32[]{:S(2)}, u32[]{:S(2)}) collective-permute-start(f32[6,6,524]{2,1,0:T(8,128)S(1)} %get-tuple-element.34), channel_id=1, source_target_pairs={{8,0},{16,8},{24,16},{32,24},{40,32},{48,40},{56,48},{64,56},{72,6... | collective-permute-start | bytes 226376 | tf_op jit(solution)/shard_map/ppermute | solution.py:21
  23.8 0.5 collective-permute-done.2
  24.4 3.8 %collective-permute-done.3 = f32[6,6,524]{2,1,0:T(8,128)S(1)} collective-permute-done((f32[6,6,524]{2,1,0:T(8,128)S(1)}, f32[6,6,524]{2,1,0:T(8,128)S(1)}, u32[]{:S(2)}, u32[]{:S(2)}) %collective-permute-start.3) | collective-permute-done | bytes 75488 | tf_op jit(solution)/shard_map/ppermute | solution.py:21
  28.1 0.2 pad_maximum_fusion
  28.3 0.1 compare_bitcast_fusion.7
  28.4 0.6 select_select_fusion
  29.1 0.1 slice_bitcast_fusion.6
  29.2 0.3 fusion.5
  29.5 0.2 fusion.27
  29.6 0.2 fusion.29
  29.8 0.1 fusion.30
  29.9 0.2 fusion.24
  30.2 0.2 fusion.9
  30.4 0.2 fusion.15
  30.6 0.6 gather_fusion
  31.2 0.1 copy.16
  31.3 0.2 fusion.8
  31.5 0.1 bitcast_dynamic-update-slice_fusion.3
  31.6 0.1 add_bitcast_fusion
  31.8 0.6 gather_fusion.1
  32.4 0.1 copy.17
  32.5 0.6 gather_fusion.2
  33.2 0.0 copy-start.3
  33.2 0.1 copy.18
  33.3 0.6 copy-done.3
  33.9 0.1 pad_maximum_fusion.4
  33.9 0.6 broadcast_in_dim.205
  34.6 9.6 %all-to-all-start = ((f32[8,4,256]{2,1,0:T(4,128)}), f32[8,4,256]{2,1,0:T(4,128)S(1)}, u32[]{:S(2)}, u32[]{:S(2)}) async-start(f32[8,4,256]{2,1,0:T(4,128)} %broadcast_in_dim.205), calls=%async_computation | async-start | bytes 65536 | tf_op jit(solution)/shard_map/all_to_all | solution.py:101
  44.2 0.1 bitcast_dynamic-update-slice_fusion.2
  44.3 9.4 %all-to-all-done = f32[8,4,256]{2,1,0:T(4,128)S(1)} async-done(((f32[8,4,256]{2,1,0:T(4,128)}), f32[8,4,256]{2,1,0:T(4,128)S(1)}, u32[]{:S(2)}, u32[]{:S(2)}) %all-to-all-start) | async-done | bytes 32800 | tf_op jit(solution)/shard_map/all_to_all | solution.py:101
  53.7 0.9 broadcast_in_dim.207
  54.6 8.0 %all-to-all-start.1 = ((f32[16,32,256]{2,1,0:T(8,128)}), f32[16,32,256]{2,1,0:T(8,128)S(1)}, u32[]{:S(2)}, u32[]{:S(2)}) async-start(f32[16,32,256]{2,1,0:T(8,128)} %broadcast_in_dim.207), calls=%async_computation.1 | async-start | bytes 1048576 | tf_op jit(solution)/shard_map/all_to_all | solution.py:101
  62.5 0.6 copy.19
  63.1 0.1 fusion.35
  63.2 0.0 copy-start.2
  63.3 8.2 %all-to-all-done.1 = f32[16,32,256]{2,1,0:T(8,128)S(1)} async-done(((f32[16,32,256]{2,1,0:T(8,128)}), f32[16,32,256]{2,1,0:T(8,128)S(1)}, u32[]{:S(2)}, u32[]{:S(2)}) %all-to-all-start.1) | async-done | bytes 524320 | tf_op jit(solution)/shard_map/all_to_all | solution.py:101
  71.5 0.0 copy-start
  71.5 0.8 copy-done
  72.3 4.4 %shard_map.94 = f32[16,128]{1,0:T(8,128)} custom-call(s32[128]{0:T(128)} %bitcast.104, f32[512,256]{1,0:T(8,128)} %bitcast.91, s32[128,16,128]{2,1,0:T(8,128)} %bitcast.95), custom_call_target="tpu_custom_call" | custom-call | flops 2097152 | bytes 1581056 | tf_op jit(solution)/shard_map/pallas_call | solution.py:82
  76.7 0.0 copy-done.2
  76.7 20.5 %all-gather = f32[64,128]{1,0:T(8,128)S(1)} all-gather(f32[16,128]{1,0:T(8,128)} %shard_map.94), channel_id=2, replica_groups=mesh['act'=4,'axial'=16,'hoop'=8] {'act'}, dimensions={0}, use_global_device_ids=true | all-gather | bytes 40960 | tf_op jit(solution)/shard_map/all_gather | solution.py:143
  97.2 0.6 fusion.40
  (12 shorter events, 0.1 us)
Async XLA Ops:
  1.4 17.7 %copy-start.1 = (f32[1,5,16,512]{3,2,1,0:T(8,128)S(1)}, f32[1,5,16,512]{3,2,1,0:T(8,128)}, u32[]{:S(2)}) copy-start(f32[1,5,16,512]{3,2,1,0:T(8,128)} %param.7) | copy-start | bytes 491524
  1.4 16.6 %copy-start.4 = (f32[8,6]{1,0:T(8,128)S(1)}, f32[8,6]{1,0:T(8,128)}, u32[]{:S(2)}) copy-start(f32[8,6]{1,0:T(8,128)} %param.9) | copy-start | bytes 580
  2.3 15.7 %collective-permute-start = (f32[6,16,6]{2,1,0:T(8,128)S(1)}, f32[6,16,6]{2,1,0:T(8,128)S(1)}, u32[]{:S(2)}, u32[]{:S(2)}) collective-permute-start(f32[6,16,6]{2,1,0:T(8,128)S(1)} %get-tuple-element.37), channel_id=1, source_target_pairs={{0,1},{1,2},{2,3},{3,4},{4,5},{5,6},{6,7},{7,0},{8,9},{9,10},{10,1... | collective-permute-start | bytes 6920 | tf_op jit(solution)/shard_map/ppermute | solution.py:17
  6.7 11.3 %copy-start.5 = (s32[4]{0:T(128)S(1)}, s32[4]{0:T(128)}, u32[]{:S(2)}) copy-start(s32[4]{0:T(128)} %param.10) | copy-start | bytes 52
  6.7 12.4 %collective-permute-start.1 = (f32[6,16,6]{2,1,0:T(8,128)S(1)}, f32[6,16,6]{2,1,0:T(8,128)S(1)}, u32[]{:S(2)}, u32[]{:S(2)}) collective-permute-start(f32[6,16,6]{2,1,0:T(8,128)S(1)} %get-tuple-element.38), channel_id=1, source_target_pairs={{1,0},{2,1},{3,2},{4,3},{5,4},{6,5},{7,6},{0,7},{9,8},{10,9},{11,1... | collective-permute-start | bytes 6920 | tf_op jit(solution)/shard_map/ppermute | solution.py:18
  19.3 5.1 %collective-permute-start.2 = (f32[6,6,524]{2,1,0:T(8,128)S(1)}, f32[6,6,524]{2,1,0:T(8,128)S(1)}, u32[]{:S(2)}, u32[]{:S(2)}) collective-permute-start(f32[6,6,524]{2,1,0:T(8,128)S(1)} %get-tuple-element.33), channel_id=1, source_target_pairs={{0,8},{8,16},{16,24},{24,32},{32,40},{40,48},{48,56},{56,64},{64,7... | collective-permute-start | bytes 226376 | tf_op jit(solution)/shard_map/ppermute | solution.py:20
  22.5 5.6 %collective-permute-start.3 = (f32[6,6,524]{2,1,0:T(8,128)S(1)}, f32[6,6,524]{2,1,0:T(8,128)S(1)}, u32[]{:S(2)}, u32[]{:S(2)}) collective-permute-start(f32[6,6,524]{2,1,0:T(8,128)S(1)} %get-tuple-element.34), channel_id=1, source_target_pairs={{8,0},{16,8},{24,16},{32,24},{40,32},{48,40},{56,48},{64,56},{72,6... | collective-permute-start | bytes 226376 | tf_op jit(solution)/shard_map/ppermute | solution.py:21
  33.2 0.7 copy-start.3
  34.6 19.1 %all-to-all-start = ((f32[8,4,256]{2,1,0:T(4,128)}), f32[8,4,256]{2,1,0:T(4,128)S(1)}, u32[]{:S(2)}, u32[]{:S(2)}) async-start(f32[8,4,256]{2,1,0:T(4,128)} %broadcast_in_dim.205), calls=%async_computation | async-start | bytes 65536 | tf_op jit(solution)/shard_map/all_to_all | solution.py:101
  54.6 16.9 %all-to-all-start.1 = ((f32[16,32,256]{2,1,0:T(8,128)}), f32[16,32,256]{2,1,0:T(8,128)S(1)}, u32[]{:S(2)}, u32[]{:S(2)}) async-start(f32[16,32,256]{2,1,0:T(8,128)} %broadcast_in_dim.207), calls=%async_computation.1 | async-start | bytes 1048576 | tf_op jit(solution)/shard_map/all_to_all | solution.py:101
  63.2 13.4 %copy-start.2 = (f32[5,16,512]{2,1,0:T(8,128)}, f32[5,16,512]{2,1,0:T(8,128)S(1)}, u32[]{:S(2)}) copy-start(f32[5,16,512]{2,1,0:T(8,128)S(1)} %fusion.35) | copy-start | bytes 491524
  71.5 0.8 copy-start

commit v10 on v9

--- a/solution.py
+++ b/solution.py
@@ -73,7 +73,7 @@
             parts.append(jnp.where(d >= lanes, got_high, got_low))
         return acc + jnp.concatenate(parts, axis=0)
 
-    acc = lax.fori_loop(0, pairs, body, jnp.zeros((pix_rows, pix_cols), jnp.float32), unroll=8)
+    acc = lax.fori_loop(0, pairs, body, jnp.zeros((pix_rows, pix_cols), jnp.float32), unroll=16)
     out_ref[...] = acc
 
 
@@ -140,7 +140,7 @@
     local_waves = jnp.concatenate([history[0], recorded[0]], axis=1)
     waveforms = gather_waves(local_waves)
     partial_value = image(receivers[0], waveforms, delays[0])
-    parts = lax.all_gather(partial_value, "act")
+    parts = lax.all_gather(partial_value.reshape(-1), "act").reshape((-1,) + partial_value.shape)
     summed = parts[0]
     for a in range(1, parts.shape[0]):
         summed = summed + parts[a]

time: 98.4 us -> 97.8 us (level)
  no operation moved by 1% of the time
where the time goes in v10:
time: 97.8 us; the launch traced here: 97.3 us
  starting transfers between devices  37.7 us (39%)
  waiting for transfers between devices  23 us (24%)
  blocking collectives  20.5 us (21%)
  local copies, waits for them, and re-layouts  5.95 us (6%)
  other arithmetic  5.33 us (5%)
  Pallas kernels  3.85 us (4%)
    all_gather x1, blocking collectives, per_device(): lax.all_gather(partial_value.reshape(-1), 'act')  20.5 us
    all_to_all x2, waiting for transfers between devices, a2a_gather(): gathered = lax.all_to_all(spread, axes, 0, 0, tiled=True)  17.6 us
    all_to_all x2, starting transfers between devices, a2a_gather(): gathered = lax.all_to_all(spread, axes, 0, 0, tiled=True)  17.6 us
    ppermute x1, starting transfers between devices, exchange(): lax.ppermute(cells[:, :, :halo], 'hoop', [((j + 1) % nh, j) for j in rang...  11.3 us
    ppermute x1, starting transfers between devices, exchange(): lax.ppermute(cells[:, :, -halo:], 'hoop', [(j, (j + 1) % nh) for j in ran...  4.37 us
    pallas_call x1, Pallas kernels, image(): pl.pallas_call(image_kernel, out_shape=jax.ShapeDtypeStruct((pix_rows, pi...  3.85 us
    ppermute x1, waiting for transfers between devices, exchange(): lax.ppermute(cells[:, :halo, :], 'axial', [(i + 1, i) for i in range(na -...  3.78 us
    ppermute x1, starting transfers between devices, exchange(): lax.ppermute(cells[:, -halo:, :], 'axial', [(i, i + 1) for i in range(na...  3.21 us
  transfers between devices with their start and end apart: 6, of which 5 were waited for; matrix products, arithmetic and copies ran while one was open for 1% of the time, Pallas kernels for 0%

profile of v10, /device:TPU:1, one launch (start us, length us, event | category | flops | bytes accessed | tf_op | source)
XLA Modules:
  0.0 97.3 jit_solution(14670192651586977294)
XLA Ops:
  0.6 0.8 convert_bitcast_fusion
  1.4 0.0 copy-start.1
  1.4 0.0 copy-start.4
  1.4 0.9 pad_maximum_fusion.3
  2.3 4.4 %collective-permute-start = (f32[6,16,6]{2,1,0:T(8,128)S(1)}, f32[6,16,6]{2,1,0:T(8,128)S(1)}, u32[]{:S(2)}, u32[]{:S(2)}) collective-permute-start(f32[6,16,6]{2,1,0:T(8,128)S(1)} %get-tuple-element.40), channel_id=1, source_target_pairs={{0,1},{1,2},{2,3},{3,4},{4,5},{5,6},{6,7},{7,0},{8,9},{9,10},{10,1... | collective-permute-start | bytes 6920 | tf_op jit(solution)/shard_map/ppermute | solution.py:17
  6.7 0.0 copy-start.5
  6.7 11.3 %collective-permute-start.1 = (f32[6,16,6]{2,1,0:T(8,128)S(1)}, f32[6,16,6]{2,1,0:T(8,128)S(1)}, u32[]{:S(2)}, u32[]{:S(2)}) collective-permute-start(f32[6,16,6]{2,1,0:T(8,128)S(1)} %get-tuple-element.41), channel_id=1, source_target_pairs={{1,0},{2,1},{3,2},{4,3},{5,4},{6,5},{7,6},{0,7},{9,8},{10,9},{11,1... | collective-permute-start | bytes 6920 | tf_op jit(solution)/shard_map/ppermute | solution.py:18
  18.0 0.0 copy-done.4
  18.0 0.0 copy-done.5
  18.0 0.0 collective-permute-done
  18.1 1.1 %collective-permute-done.1 = f32[6,16,6]{2,1,0:T(8,128)S(1)} collective-permute-done((f32[6,16,6]{2,1,0:T(8,128)S(1)}, f32[6,16,6]{2,1,0:T(8,128)S(1)}, u32[]{:S(2)}, u32[]{:S(2)}) %collective-permute-start.1) | collective-permute-done | bytes 2336 | tf_op jit(solution)/shard_map/ppermute | solution.py:18
  19.1 0.0 copy-done.1
  19.1 0.1 pad_maximum_fusion.1
  19.3 3.2 %collective-permute-start.2 = (f32[6,6,524]{2,1,0:T(8,128)S(1)}, f32[6,6,524]{2,1,0:T(8,128)S(1)}, u32[]{:S(2)}, u32[]{:S(2)}) collective-permute-start(f32[6,6,524]{2,1,0:T(8,128)S(1)} %get-tuple-element.36), channel_id=1, source_target_pairs={{0,8},{8,16},{16,24},{24,32},{32,40},{40,48},{48,56},{56,64},{64,7... | collective-permute-start | bytes 226376 | tf_op jit(solution)/shard_map/ppermute | solution.py:20
  22.5 1.3 %collective-permute-start.3 = (f32[6,6,524]{2,1,0:T(8,128)S(1)}, f32[6,6,524]{2,1,0:T(8,128)S(1)}, u32[]{:S(2)}, u32[]{:S(2)}) collective-permute-start(f32[6,6,524]{2,1,0:T(8,128)S(1)} %get-tuple-element.37), channel_id=1, source_target_pairs={{8,0},{16,8},{24,16},{32,24},{40,32},{48,40},{56,48},{64,56},{72,6... | collective-permute-start | bytes 226376 | tf_op jit(solution)/shard_map/ppermute | solution.py:21
  23.8 0.5 collective-permute-done.2
  24.4 3.8 %collective-permute-done.3 = f32[6,6,524]{2,1,0:T(8,128)S(1)} collective-permute-done((f32[6,6,524]{2,1,0:T(8,128)S(1)}, f32[6,6,524]{2,1,0:T(8,128)S(1)}, u32[]{:S(2)}, u32[]{:S(2)}) %collective-permute-start.3) | collective-permute-done | bytes 75488 | tf_op jit(solution)/shard_map/ppermute | solution.py:21
  28.1 0.2 pad_maximum_fusion
  28.3 0.1 compare_bitcast_fusion.7
  28.4 0.6 select_select_fusion
  29.1 0.1 slice_bitcast_fusion.6
  29.2 0.3 fusion.5
  29.5 0.2 fusion.27
  29.6 0.2 fusion.29
  29.8 0.1 fusion.30
  29.9 0.2 fusion.24
  30.2 0.2 fusion.9
  30.4 0.2 fusion.15
  30.6 0.6 gather_fusion
  31.2 0.1 copy.21
  31.3 0.2 fusion.8
  31.5 0.1 bitcast_dynamic-update-slice_fusion.3
  31.6 0.1 add_bitcast_fusion
  31.8 0.6 gather_fusion.1
  32.4 0.1 copy.22
  32.5 0.6 gather_fusion.2
  33.2 0.0 copy-start.3
  33.2 0.1 copy.23
  33.3 0.6 copy-done.3
  33.9 0.1 pad_maximum_fusion.4
  33.9 0.6 broadcast_in_dim.205
  34.6 9.6 %all-to-all-start = ((f32[8,4,256]{2,1,0:T(4,128)}), f32[8,4,256]{2,1,0:T(4,128)S(1)}, u32[]{:S(2)}, u32[]{:S(2)}) async-start(f32[8,4,256]{2,1,0:T(4,128)} %broadcast_in_dim.205), calls=%async_computation | async-start | bytes 65536 | tf_op jit(solution)/shard_map/all_to_all | solution.py:101
  44.2 0.1 bitcast_dynamic-update-slice_fusion.2
  44.3 9.4 %all-to-all-done = f32[8,4,256]{2,1,0:T(4,128)S(1)} async-done(((f32[8,4,256]{2,1,0:T(4,128)}), f32[8,4,256]{2,1,0:T(4,128)S(1)}, u32[]{:S(2)}, u32[]{:S(2)}) %all-to-all-start) | async-done | bytes 32800 | tf_op jit(solution)/shard_map/all_to_all | solution.py:101
  53.7 0.9 broadcast_in_dim.207
  54.6 8.0 %all-to-all-start.1 = ((f32[16,32,256]{2,1,0:T(8,128)}), f32[16,32,256]{2,1,0:T(8,128)S(1)}, u32[]{:S(2)}, u32[]{:S(2)}) async-start(f32[16,32,256]{2,1,0:T(8,128)} %broadcast_in_dim.207), calls=%async_computation.1 | async-start | bytes 1048576 | tf_op jit(solution)/shard_map/all_to_all | solution.py:101
  62.6 0.6 copy.24
  63.1 0.1 fusion.35
  63.3 0.0 copy-start.2
  63.3 8.2 %all-to-all-done.1 = f32[16,32,256]{2,1,0:T(8,128)S(1)} async-done(((f32[16,32,256]{2,1,0:T(8,128)}), f32[16,32,256]{2,1,0:T(8,128)S(1)}, u32[]{:S(2)}, u32[]{:S(2)}) %all-to-all-start.1) | async-done | bytes 524320 | tf_op jit(solution)/shard_map/all_to_all | solution.py:101
  71.5 0.0 copy-start
  71.5 0.8 copy-done
  72.3 3.8 %shard_map.94 = f32[16,128]{1,0:T(8,128)} custom-call(s32[128]{0:T(128)} %bitcast.114, f32[512,256]{1,0:T(8,128)} %bitcast.99, s32[128,16,128]{2,1,0:T(8,128)} %bitcast.103), custom_call_target="tpu_custom_call" | custom-call | flops 2097152 | bytes 1581056 | tf_op jit(solution)/shard_map/pallas_call | solution.py:82
  76.1 0.0 copy-done.2
  76.1 20.5 %all-gather = f32[4,1,2048]{2,1,0:T(1,128)S(1)} all-gather(f32[1,1,2048]{2,1,0:T(1,128)} %bitcast.104), channel_id=1, replica_groups=mesh['act'=4,'axial'=16,'hoop'=8] {'act'}, dimensions={0}, use_global_device_ids=true | all-gather | bytes 40960 | tf_op jit(solution)/shard_map/all_gather | solution.py:143
  96.7 0.6 fusion.41
  (12 shorter events, 0.1 us)
Async XLA Ops:
  1.4 17.7 %copy-start.1 = (f32[1,5,16,512]{3,2,1,0:T(8,128)S(1)}, f32[1,5,16,512]{3,2,1,0:T(8,128)}, u32[]{:S(2)}) copy-start(f32[1,5,16,512]{3,2,1,0:T(8,128)} %param.7) | copy-start | bytes 491524
  1.4 16.6 %copy-start.4 = (f32[8,6]{1,0:T(8,128)S(1)}, f32[8,6]{1,0:T(8,128)}, u32[]{:S(2)}) copy-start(f32[8,6]{1,0:T(8,128)} %param.9) | copy-start | bytes 580
  2.3 15.7 %collective-permute-start = (f32[6,16,6]{2,1,0:T(8,128)S(1)}, f32[6,16,6]{2,1,0:T(8,128)S(1)}, u32[]{:S(2)}, u32[]{:S(2)}) collective-permute-start(f32[6,16,6]{2,1,0:T(8,128)S(1)} %get-tuple-element.40), channel_id=1, source_target_pairs={{0,1},{1,2},{2,3},{3,4},{4,5},{5,6},{6,7},{7,0},{8,9},{9,10},{10,1... | collective-permute-start | bytes 6920 | tf_op jit(solution)/shard_map/ppermute | solution.py:17
  6.7 11.3 %copy-start.5 = (s32[4]{0:T(128)S(1)}, s32[4]{0:T(128)}, u32[]{:S(2)}) copy-start(s32[4]{0:T(128)} %param.10) | copy-start | bytes 52
  6.7 12.4 %collective-permute-start.1 = (f32[6,16,6]{2,1,0:T(8,128)S(1)}, f32[6,16,6]{2,1,0:T(8,128)S(1)}, u32[]{:S(2)}, u32[]{:S(2)}) collective-permute-start(f32[6,16,6]{2,1,0:T(8,128)S(1)} %get-tuple-element.41), channel_id=1, source_target_pairs={{1,0},{2,1},{3,2},{4,3},{5,4},{6,5},{7,6},{0,7},{9,8},{10,9},{11,1... | collective-permute-start | bytes 6920 | tf_op jit(solution)/shard_map/ppermute | solution.py:18
  19.3 5.1 %collective-permute-start.2 = (f32[6,6,524]{2,1,0:T(8,128)S(1)}, f32[6,6,524]{2,1,0:T(8,128)S(1)}, u32[]{:S(2)}, u32[]{:S(2)}) collective-permute-start(f32[6,6,524]{2,1,0:T(8,128)S(1)} %get-tuple-element.36), channel_id=1, source_target_pairs={{0,8},{8,16},{16,24},{24,32},{32,40},{40,48},{48,56},{56,64},{64,7... | collective-permute-start | bytes 226376 | tf_op jit(solution)/shard_map/ppermute | solution.py:20
  22.5 5.6 %collective-permute-start.3 = (f32[6,6,524]{2,1,0:T(8,128)S(1)}, f32[6,6,524]{2,1,0:T(8,128)S(1)}, u32[]{:S(2)}, u32[]{:S(2)}) collective-permute-start(f32[6,6,524]{2,1,0:T(8,128)S(1)} %get-tuple-element.37), channel_id=1, source_target_pairs={{8,0},{16,8},{24,16},{32,24},{40,32},{48,40},{56,48},{64,56},{72,6... | collective-permute-start | bytes 226376 | tf_op jit(solution)/shard_map/ppermute | solution.py:21
  33.2 0.7 copy-start.3
  34.6 19.1 %all-to-all-start = ((f32[8,4,256]{2,1,0:T(4,128)}), f32[8,4,256]{2,1,0:T(4,128)S(1)}, u32[]{:S(2)}, u32[]{:S(2)}) async-start(f32[8,4,256]{2,1,0:T(4,128)} %broadcast_in_dim.205), calls=%async_computation | async-start | bytes 65536 | tf_op jit(solution)/shard_map/all_to_all | solution.py:101
  54.6 16.9 %all-to-all-start.1 = ((f32[16,32,256]{2,1,0:T(8,128)}), f32[16,32,256]{2,1,0:T(8,128)S(1)}, u32[]{:S(2)}, u32[]{:S(2)}) async-start(f32[16,32,256]{2,1,0:T(8,128)} %broadcast_in_dim.207), calls=%async_computation.1 | async-start | bytes 1048576 | tf_op jit(solution)/shard_map/all_to_all | solution.py:101
  63.3 12.9 %copy-start.2 = (f32[5,16,512]{2,1,0:T(8,128)}, f32[5,16,512]{2,1,0:T(8,128)S(1)}, u32[]{:S(2)}) copy-start(f32[5,16,512]{2,1,0:T(8,128)S(1)} %fusion.35) | copy-start | bytes 491524
  71.5 0.8 copy-start

commit v11 on v10

--- a/solution.py
+++ b/solution.py
@@ -133,7 +133,10 @@
         off = HALO - 2 * (step_index + 1)
         total = fields[2] + fields[3]
         tile = total[off:off + rows, off:off + cols]
-        samples.append(tile.reshape(-1)[sensors])
+        flat = tile.reshape(1, -1)
+        cell = lax.broadcasted_iota(jnp.int32, (sensors.shape[0], flat.shape[1]), 1)
+        hit = cell == sensors[:, None]
+        samples.append(jnp.sum(jnp.where(hit, flat, jnp.float32(0.0)), axis=1))
         moduli_map = jnp.stack(moduli_map)
     next_state = jnp.stack(fields)[None]
     recorded = jnp.stack(samples, axis=1)[None]

time: 97.8 us -> 96.8 us (0.990)
  local copies, waits for them, and re-layouts: 5.95 us -> 4.66 us
    gather x3 -> x0, local copies, waits for them, and re-layouts: 1.9 us -> none  [per_device(): samples.append(tile.reshape(-1)[sensors])]
where the time goes in v11:
time: 96.8 us; the launch traced here: 96.3 us
  starting transfers between devices  37.7 us (39%)
  waiting for transfers between devices  23 us (24%)
  blocking collectives  20.5 us (21%)
  other arithmetic  5.63 us (6%)
  local copies, waits for them, and re-layouts  4.66 us (5%)
  Pallas kernels  3.85 us (4%)
    all_gather x1, blocking collectives, per_device(): lax.all_gather(partial_value.reshape(-1), 'act')  20.5 us
    all_to_all x2, waiting for transfers between devices, a2a_gather(): gathered = lax.all_to_all(spread, axes, 0, 0, tiled=True)  17.6 us
    all_to_all x2, starting transfers between devices, a2a_gather(): gathered = lax.all_to_all(spread, axes, 0, 0, tiled=True)  17.6 us
    ppermute x1, starting transfers between devices, exchange(): lax.ppermute(cells[:, :, :halo], 'hoop', [((j + 1) % nh, j) for j in rang...  11.3 us
    ppermute x1, starting transfers between devices, exchange(): lax.ppermute(cells[:, :, -halo:], 'hoop', [(j, (j + 1) % nh) for j in ran...  4.37 us
    pallas_call x1, Pallas kernels, image(): pl.pallas_call(image_kernel, out_shape=jax.ShapeDtypeStruct((pix_rows, pi...  3.85 us
    ppermute x1, waiting for transfers between devices, exchange(): lax.ppermute(cells[:, :halo, :], 'axial', [(i + 1, i) for i in range(na -...  3.78 us
    ppermute x1, starting transfers between devices, exchange(): lax.ppermute(cells[:, -halo:, :], 'axial', [(i, i + 1) for i in range(na...  3.21 us
  transfers between devices with their start and end apart: 6, of which 5 were waited for; matrix products, arithmetic and copies ran while one was open for 1% of the time, Pallas kernels for 0%

profile of v11, /device:TPU:1, one launch (start us, length us, event | category | flops | bytes accessed | tf_op | source)
XLA Modules:
  0.0 96.3 jit_solution(8687384499504834028)
XLA Ops:
  0.6 0.8 convert_bitcast_fusion
  1.4 0.0 copy-start.1
  1.4 0.0 copy-start.4
  1.4 0.9 pad_maximum_fusion.3
  2.3 4.4 %collective-permute-start = (f32[6,16,6]{2,1,0:T(8,128)S(1)}, f32[6,16,6]{2,1,0:T(8,128)S(1)}, u32[]{:S(2)}, u32[]{:S(2)}) collective-permute-start(f32[6,16,6]{2,1,0:T(8,128)S(1)} %get-tuple-element.43), channel_id=1, source_target_pairs={{0,1},{1,2},{2,3},{3,4},{4,5},{5,6},{6,7},{7,0},{8,9},{9,10},{10,1... | collective-permute-start | bytes 6920 | tf_op jit(solution)/shard_map/ppermute | solution.py:17
  6.7 11.3 %collective-permute-start.1 = (f32[6,16,6]{2,1,0:T(8,128)S(1)}, f32[6,16,6]{2,1,0:T(8,128)S(1)}, u32[]{:S(2)}, u32[]{:S(2)}) collective-permute-start(f32[6,16,6]{2,1,0:T(8,128)S(1)} %get-tuple-element.44), channel_id=1, source_target_pairs={{1,0},{2,1},{3,2},{4,3},{5,4},{6,5},{7,6},{0,7},{9,8},{10,9},{11,1... | collective-permute-start | bytes 6920 | tf_op jit(solution)/shard_map/ppermute | solution.py:18
  18.0 0.0 copy-done.4
  18.0 0.0 collective-permute-done
  18.0 1.1 %collective-permute-done.1 = f32[6,16,6]{2,1,0:T(8,128)S(1)} collective-permute-done((f32[6,16,6]{2,1,0:T(8,128)S(1)}, f32[6,16,6]{2,1,0:T(8,128)S(1)}, u32[]{:S(2)}, u32[]{:S(2)}) %collective-permute-start.1) | collective-permute-done | bytes 2336 | tf_op jit(solution)/shard_map/ppermute | solution.py:18
  19.1 0.0 copy-done.1
  19.1 0.1 pad_maximum_fusion.1
  19.3 3.2 %collective-permute-start.2 = (f32[6,6,524]{2,1,0:T(8,128)S(1)}, f32[6,6,524]{2,1,0:T(8,128)S(1)}, u32[]{:S(2)}, u32[]{:S(2)}) collective-permute-start(f32[6,6,524]{2,1,0:T(8,128)S(1)} %get-tuple-element.39), channel_id=1, source_target_pairs={{0,8},{8,16},{16,24},{24,32},{32,40},{40,48},{48,56},{56,64},{64,7... | collective-permute-start | bytes 226376 | tf_op jit(solution)/shard_map/ppermute | solution.py:20
  22.5 1.3 %collective-permute-start.3 = (f32[6,6,524]{2,1,0:T(8,128)S(1)}, f32[6,6,524]{2,1,0:T(8,128)S(1)}, u32[]{:S(2)}, u32[]{:S(2)}) collective-permute-start(f32[6,6,524]{2,1,0:T(8,128)S(1)} %get-tuple-element.40), channel_id=1, source_target_pairs={{8,0},{16,8},{24,16},{32,24},{40,32},{48,40},{56,48},{64,56},{72,6... | collective-permute-start | bytes 226376 | tf_op jit(solution)/shard_map/ppermute | solution.py:21
  23.8 0.5 collective-permute-done.2
  24.4 3.8 %collective-permute-done.3 = f32[6,6,524]{2,1,0:T(8,128)S(1)} collective-permute-done((f32[6,6,524]{2,1,0:T(8,128)S(1)}, f32[6,6,524]{2,1,0:T(8,128)S(1)}, u32[]{:S(2)}, u32[]{:S(2)}) %collective-permute-start.3) | collective-permute-done | bytes 75488 | tf_op jit(solution)/shard_map/ppermute | solution.py:21
  28.1 0.2 pad_maximum_fusion
  28.3 0.1 compare_bitcast_fusion.7
  28.4 0.6 select_select_fusion
  29.1 0.1 slice_bitcast_fusion.6
  29.1 0.3 fusion.5
  29.4 0.2 fusion.27
  29.6 0.2 fusion.29
  29.8 0.1 fusion.30
  29.9 0.2 fusion.24
  30.2 0.2 fusion.15
  30.3 0.2 fusion.9
  30.6 0.2 fusion.8
  30.8 0.1 bitcast_dynamic-update-slice_fusion.3
  30.9 0.1 add_bitcast_fusion
  31.1 0.0 copy-start.5
  31.1 0.6 copy-done.5
  31.7 0.3 select_reduce_fusion.2
  32.0 0.1 copy.23
  32.1 0.1 copy.21
  32.2 0.0 copy-start.3
  32.2 0.1 copy.22
  32.3 0.6 copy-done.3
  32.9 0.1 pad_maximum_fusion.4
  33.0 0.6 broadcast_in_dim.239
  33.6 9.6 %all-to-all-start = ((f32[8,4,256]{2,1,0:T(4,128)}), f32[8,4,256]{2,1,0:T(4,128)S(1)}, u32[]{:S(2)}, u32[]{:S(2)}) async-start(f32[8,4,256]{2,1,0:T(4,128)} %broadcast_in_dim.239), calls=%async_computation | async-start | bytes 65536 | tf_op jit(solution)/shard_map/all_to_all | solution.py:101
  43.3 0.1 bitcast_dynamic-update-slice_fusion.2
  43.3 9.4 %all-to-all-done = f32[8,4,256]{2,1,0:T(4,128)S(1)} async-done(((f32[8,4,256]{2,1,0:T(4,128)}), f32[8,4,256]{2,1,0:T(4,128)S(1)}, u32[]{:S(2)}, u32[]{:S(2)}) %all-to-all-start) | async-done | bytes 32800 | tf_op jit(solution)/shard_map/all_to_all | solution.py:101
  52.8 0.8 broadcast_in_dim.241
  53.6 8.0 %all-to-all-start.1 = ((f32[16,32,256]{2,1,0:T(8,128)}), f32[16,32,256]{2,1,0:T(8,128)S(1)}, u32[]{:S(2)}, u32[]{:S(2)}) async-start(f32[16,32,256]{2,1,0:T(8,128)} %broadcast_in_dim.241), calls=%async_computation.1 | async-start | bytes 1048576 | tf_op jit(solution)/shard_map/all_to_all | solution.py:101
  61.6 0.6 copy.24
  62.2 0.1 fusion.35
  62.3 0.0 copy-start.2
  62.3 8.2 %all-to-all-done.1 = f32[16,32,256]{2,1,0:T(8,128)S(1)} async-done(((f32[16,32,256]{2,1,0:T(8,128)}), f32[16,32,256]{2,1,0:T(8,128)S(1)}, u32[]{:S(2)}, u32[]{:S(2)}) %all-to-all-start.1) | async-done | bytes 524320 | tf_op jit(solution)/shard_map/all_to_all | solution.py:101
  70.5 0.0 copy-start
  70.5 0.8 copy-done
  71.3 3.8 %shard_map.94 = f32[16,128]{1,0:T(8,128)} custom-call(s32[128]{0:T(128)} %bitcast.114, f32[512,256]{1,0:T(8,128)} %bitcast.96, s32[128,16,128]{2,1,0:T(8,128)} %bitcast.100), custom_call_target="tpu_custom_call" | custom-call | flops 2097152 | bytes 1581056 | tf_op jit(solution)/shard_map/pallas_call | solution.py:82
  75.2 0.0 copy-done.2
  75.2 20.5 %all-gather = f32[4,1,2048]{2,1,0:T(1,128)S(1)} all-gather(f32[1,1,2048]{2,1,0:T(1,128)} %bitcast.104), channel_id=1, replica_groups=mesh['act'=4,'axial'=16,'hoop'=8] {'act'}, dimensions={0}, use_global_device_ids=true | all-gather | bytes 40960 | tf_op jit(solution)/shard_map/all_gather | solution.py:146
  95.7 0.6 fusion.41
  (10 shorter events, 0.1 us)
Async XLA Ops:
  1.4 17.7 %copy-start.1 = (f32[1,5,16,512]{3,2,1,0:T(8,128)S(1)}, f32[1,5,16,512]{3,2,1,0:T(8,128)}, u32[]{:S(2)}) copy-start(f32[1,5,16,512]{3,2,1,0:T(8,128)} %param.7) | copy-start | bytes 491524
  1.4 16.6 %copy-start.4 = (f32[8,6]{1,0:T(8,128)S(1)}, f32[8,6]{1,0:T(8,128)}, u32[]{:S(2)}) copy-start(f32[8,6]{1,0:T(8,128)} %param.9) | copy-start | bytes 580
  2.3 15.7 %collective-permute-start = (f32[6,16,6]{2,1,0:T(8,128)S(1)}, f32[6,16,6]{2,1,0:T(8,128)S(1)}, u32[]{:S(2)}, u32[]{:S(2)}) collective-permute-start(f32[6,16,6]{2,1,0:T(8,128)S(1)} %get-tuple-element.43), channel_id=1, source_target_pairs={{0,1},{1,2},{2,3},{3,4},{4,5},{5,6},{6,7},{7,0},{8,9},{9,10},{10,1... | collective-permute-start | bytes 6920 | tf_op jit(solution)/shard_map/ppermute | solution.py:17
  6.7 12.4 %collective-permute-start.1 = (f32[6,16,6]{2,1,0:T(8,128)S(1)}, f32[6,16,6]{2,1,0:T(8,128)S(1)}, u32[]{:S(2)}, u32[]{:S(2)}) collective-permute-start(f32[6,16,6]{2,1,0:T(8,128)S(1)} %get-tuple-element.44), channel_id=1, source_target_pairs={{1,0},{2,1},{3,2},{4,3},{5,4},{6,5},{7,6},{0,7},{9,8},{10,9},{11,1... | collective-permute-start | bytes 6920 | tf_op jit(solution)/shard_map/ppermute | solution.py:18
  19.3 5.1 %collective-permute-start.2 = (f32[6,6,524]{2,1,0:T(8,128)S(1)}, f32[6,6,524]{2,1,0:T(8,128)S(1)}, u32[]{:S(2)}, u32[]{:S(2)}) collective-permute-start(f32[6,6,524]{2,1,0:T(8,128)S(1)} %get-tuple-element.39), channel_id=1, source_target_pairs={{0,8},{8,16},{16,24},{24,32},{32,40},{40,48},{48,56},{56,64},{64,7... | collective-permute-start | bytes 226376 | tf_op jit(solution)/shard_map/ppermute | solution.py:20
  22.5 5.6 %collective-permute-start.3 = (f32[6,6,524]{2,1,0:T(8,128)S(1)}, f32[6,6,524]{2,1,0:T(8,128)S(1)}, u32[]{:S(2)}, u32[]{:S(2)}) collective-permute-start(f32[6,6,524]{2,1,0:T(8,128)S(1)} %get-tuple-element.40), channel_id=1, source_target_pairs={{8,0},{16,8},{24,16},{32,24},{40,32},{48,40},{56,48},{64,56},{72,6... | collective-permute-start | bytes 226376 | tf_op jit(solution)/shard_map/ppermute | solution.py:21
  31.1 0.7 copy-start.5
  32.2 0.7 copy-start.3
  33.6 19.1 %all-to-all-start = ((f32[8,4,256]{2,1,0:T(4,128)}), f32[8,4,256]{2,1,0:T(4,128)S(1)}, u32[]{:S(2)}, u32[]{:S(2)}) async-start(f32[8,4,256]{2,1,0:T(4,128)} %broadcast_in_dim.239), calls=%async_computation | async-start | bytes 65536 | tf_op jit(solution)/shard_map/all_to_all | solution.py:101
  53.6 16.9 %all-to-all-start.1 = ((f32[16,32,256]{2,1,0:T(8,128)}), f32[16,32,256]{2,1,0:T(8,128)S(1)}, u32[]{:S(2)}, u32[]{:S(2)}) async-start(f32[16,32,256]{2,1,0:T(8,128)} %broadcast_in_dim.241), calls=%async_computation.1 | async-start | bytes 1048576 | tf_op jit(solution)/shard_map/all_to_all | solution.py:101
  62.3 12.9 %copy-start.2 = (f32[5,16,512]{2,1,0:T(8,128)}, f32[5,16,512]{2,1,0:T(8,128)S(1)}, u32[]{:S(2)}) copy-start(f32[5,16,512]{2,1,0:T(8,128)S(1)} %fusion.35) | copy-start | bytes 491524
  70.5 0.8 copy-start

commit v12 on v11

--- a/solution.py
+++ b/solution.py
@@ -113,6 +113,14 @@
     stacked = jnp.concatenate(
         [wave_state[0], layup_zone.astype(jnp.float32)[None]], axis=0
     )
+    hist = history[0]
+    hist_count = hist.shape[1]
+    hist_wide = jnp.concatenate(
+        [hist, jnp.zeros((hist.shape[0], STEPS), jnp.float32)], axis=1
+    )
+    cell = lax.broadcasted_iota(jnp.int32, (sensors.shape[0], rows * cols), 1)
+    hit = cell == sensors[:, None]
+    stacked, hist_wide, hit = lax.optimization_barrier((stacked, hist_wide, hit))
     padded = exchange(stacked, HALO)
     zone = padded[5].astype(jnp.int32)
     global_row = lax.axis_index("axial") * rows - HALO + lax.broadcasted_iota(
@@ -134,13 +142,13 @@
         total = fields[2] + fields[3]
         tile = total[off:off + rows, off:off + cols]
         flat = tile.reshape(1, -1)
-        cell = lax.broadcasted_iota(jnp.int32, (sensors.shape[0], flat.shape[1]), 1)
-        hit = cell == sensors[:, None]
         samples.append(jnp.sum(jnp.where(hit, flat, jnp.float32(0.0)), axis=1))
         moduli_map = jnp.stack(moduli_map)
     next_state = jnp.stack(fields)[None]
     recorded = jnp.stack(samples, axis=1)[None]
-    local_waves = jnp.concatenate([history[0], recorded[0]], axis=1)
+    column = lax.broadcasted_iota(jnp.int32, hist_wide.shape, 1)
+    trace_wide = jnp.pad(recorded[0], ((0, 0), (hist_count, 0)))
+    local_waves = jnp.where(column >= hist_count, trace_wide, hist_wide)
     waveforms = gather_waves(local_waves)
     partial_value = image(receivers[0], waveforms, delays[0])
     parts = lax.all_gather(partial_value.reshape(-1), "act").reshape((-1,) + partial_value.shape)

time: 96.8 us -> 96.2 us (level)
  other arithmetic: 5.63 us -> 4.04 us
    unnamed x20 -> x21, local copies, waits for them, and re-layouts: 2.8 us -> 3.82 us
where the time goes in v12:
time: 96.2 us; the launch traced here: 95.7 us
  starting transfers between devices  37.7 us (39%)
  waiting for transfers between devices  23 us (24%)
  blocking collectives  20.5 us (21%)
  local copies, waits for them, and re-layouts  5.59 us (6%)
  other arithmetic  4.04 us (4%)
  Pallas kernels  3.85 us (4%)
    all_gather x1, blocking collectives, per_device(): lax.all_gather(partial_value.reshape(-1), 'act')  20.5 us
    all_to_all x2, waiting for transfers between devices, a2a_gather(): gathered = lax.all_to_all(spread, axes, 0, 0, tiled=True)  17.6 us
    all_to_all x2, starting transfers between devices, a2a_gather(): gathered = lax.all_to_all(spread, axes, 0, 0, tiled=True)  17.6 us
    ppermute x1, starting transfers between devices, exchange(): lax.ppermute(cells[:, :, :halo], 'hoop', [((j + 1) % nh, j) for j in rang...  11.3 us
    ppermute x1, starting transfers between devices, exchange(): lax.ppermute(cells[:, :, -halo:], 'hoop', [(j, (j + 1) % nh) for j in ran...  4.37 us
    pallas_call x1, Pallas kernels, image(): pl.pallas_call(image_kernel, out_shape=jax.ShapeDtypeStruct((pix_rows, pi...  3.85 us
    unnamed x21, local copies, waits for them, and re-layouts  3.82 us
    ppermute x1, waiting for transfers between devices, exchange(): lax.ppermute(cells[:, :halo, :], 'axial', [(i + 1, i) for i in range(na -...  3.78 us
  transfers between devices with their start and end apart: 6, of which 5 were waited for; matrix products, arithmetic and copies ran while one was open for 1% of the time, Pallas kernels for 0%

profile of v12, /device:TPU:1, one launch (start us, length us, event | category | flops | bytes accessed | tf_op | source)
XLA Modules:
  0.0 95.7 jit_solution(16544818297945563697)
XLA Ops:
  0.6 0.0 copy-start.2
  0.6 0.8 copy.18
  1.5 0.0 copy-done.2
  1.5 0.0 copy-start.5
  1.5 0.6 copy-done.5
  2.1 0.0 copy-start.1
  2.1 0.1 iota_compare_fusion
  2.3 0.8 copy-done.1
  3.1 0.0 copy-start.4
  3.1 0.1 fusion.46
  3.2 4.4 %collective-permute-start = (f32[6,16,6]{2,1,0:T(8,128)S(1)}, f32[6,16,6]{2,1,0:T(8,128)S(1)}, u32[]{:S(2)}, u32[]{:S(2)}) collective-permute-start(f32[6,16,6]{2,1,0:T(8,128)S(1)} %get-tuple-element.49), channel_id=1, source_target_pairs={{0,1},{1,2},{2,3},{3,4},{4,5},{5,6},{6,7},{7,0},{8,9},{9,10},{10,1... | collective-permute-start | bytes 6920 | tf_op jit(solution)/shard_map/ppermute | solution.py:17
  7.5 11.3 %collective-permute-start.1 = (f32[6,16,6]{2,1,0:T(8,128)S(1)}, f32[6,16,6]{2,1,0:T(8,128)S(1)}, u32[]{:S(2)}, u32[]{:S(2)}) collective-permute-start(f32[6,16,6]{2,1,0:T(8,128)S(1)} %get-tuple-element.50), channel_id=1, source_target_pairs={{1,0},{2,1},{3,2},{4,3},{5,4},{6,5},{7,6},{0,7},{9,8},{10,9},{11,1... | collective-permute-start | bytes 6920 | tf_op jit(solution)/shard_map/ppermute | solution.py:18
  18.8 0.0 copy-done.4
  18.8 0.0 collective-permute-done
  18.9 1.1 %collective-permute-done.1 = f32[6,16,6]{2,1,0:T(8,128)S(1)} collective-permute-done((f32[6,16,6]{2,1,0:T(8,128)S(1)}, f32[6,16,6]{2,1,0:T(8,128)S(1)}, u32[]{:S(2)}, u32[]{:S(2)}) %collective-permute-start.1) | collective-permute-done | bytes 2336 | tf_op jit(solution)/shard_map/ppermute | solution.py:18
  20.0 0.1 pad_maximum_fusion.1
  20.1 3.2 %collective-permute-start.2 = (f32[6,6,524]{2,1,0:T(8,128)S(1)}, f32[6,6,524]{2,1,0:T(8,128)S(1)}, u32[]{:S(2)}, u32[]{:S(2)}) collective-permute-start(f32[6,6,524]{2,1,0:T(8,128)S(1)} %get-tuple-element.45), channel_id=1, source_target_pairs={{0,8},{8,16},{16,24},{24,32},{32,40},{40,48},{48,56},{56,64},{64,7... | collective-permute-start | bytes 226376 | tf_op jit(solution)/shard_map/ppermute | solution.py:20
  23.3 1.3 %collective-permute-start.3 = (f32[6,6,524]{2,1,0:T(8,128)S(1)}, f32[6,6,524]{2,1,0:T(8,128)S(1)}, u32[]{:S(2)}, u32[]{:S(2)}) collective-permute-start(f32[6,6,524]{2,1,0:T(8,128)S(1)} %get-tuple-element.46), channel_id=1, source_target_pairs={{8,0},{16,8},{24,16},{32,24},{40,32},{48,40},{56,48},{64,56},{72,6... | collective-permute-start | bytes 226376 | tf_op jit(solution)/shard_map/ppermute | solution.py:21
  24.7 0.5 collective-permute-done.2
  25.2 3.8 %collective-permute-done.3 = f32[6,6,524]{2,1,0:T(8,128)S(1)} collective-permute-done((f32[6,6,524]{2,1,0:T(8,128)S(1)}, f32[6,6,524]{2,1,0:T(8,128)S(1)}, u32[]{:S(2)}, u32[]{:S(2)}) %collective-permute-start.3) | collective-permute-done | bytes 75488 | tf_op jit(solution)/shard_map/ppermute | solution.py:21
  29.0 0.2 pad_maximum_fusion
  29.2 0.1 compare_bitcast_fusion.7
  29.3 0.6 select_select_fusion
  29.9 0.1 slice_bitcast_fusion.6
  30.0 0.3 fusion.5
  30.3 0.2 fusion.27
  30.4 0.2 fusion.29
  30.7 0.1 fusion.30
  30.7 0.2 fusion.24
  31.0 0.2 fusion.9
  31.2 0.2 fusion.15
  31.4 0.2 fusion.8
  31.6 0.1 bitcast_dynamic-update-slice_fusion.3
  31.7 0.1 add_bitcast_fusion
  31.9 0.3 select_reduce_fusion.2
  32.2 0.1 pad_select_fusion
  32.3 0.1 copy.20
  32.4 0.6 broadcast_in_dim.237
  33.0 9.6 %all-to-all-start = ((f32[8,4,256]{2,1,0:T(4,128)}), f32[8,4,256]{2,1,0:T(4,128)S(1)}, u32[]{:S(2)}, u32[]{:S(2)}) async-start(f32[8,4,256]{2,1,0:T(4,128)} %broadcast_in_dim.237), calls=%async_computation | async-start | bytes 65536 | tf_op jit(solution)/shard_map/all_to_all | solution.py:101
  42.6 0.1 bitcast_dynamic-update-slice_fusion.2
  42.7 9.4 %all-to-all-done = f32[8,4,256]{2,1,0:T(4,128)S(1)} async-done(((f32[8,4,256]{2,1,0:T(4,128)}), f32[8,4,256]{2,1,0:T(4,128)S(1)}, u32[]{:S(2)}, u32[]{:S(2)}) %all-to-all-start) | async-done | bytes 32800 | tf_op jit(solution)/shard_map/all_to_all | solution.py:101
  52.1 0.9 broadcast_in_dim.239
  53.0 8.0 %all-to-all-start.1 = ((f32[16,32,256]{2,1,0:T(8,128)}), f32[16,32,256]{2,1,0:T(8,128)S(1)}, u32[]{:S(2)}, u32[]{:S(2)}) async-start(f32[16,32,256]{2,1,0:T(8,128)} %broadcast_in_dim.239), calls=%async_computation.1 | async-start | bytes 1048576 | tf_op jit(solution)/shard_map/all_to_all | solution.py:101
  61.0 0.6 copy.21
  61.6 0.1 fusion.35
  61.7 0.0 copy-start.3
  61.7 8.2 %all-to-all-done.1 = f32[16,32,256]{2,1,0:T(8,128)S(1)} async-done(((f32[16,32,256]{2,1,0:T(8,128)}), f32[16,32,256]{2,1,0:T(8,128)S(1)}, u32[]{:S(2)}, u32[]{:S(2)}) %all-to-all-start.1) | async-done | bytes 524320 | tf_op jit(solution)/shard_map/all_to_all | solution.py:101
  69.9 0.0 copy-start
  69.9 0.8 copy-done
  70.7 3.8 %shard_map.94 = f32[16,128]{1,0:T(8,128)} custom-call(s32[128]{0:T(128)} %bitcast.109, f32[512,256]{1,0:T(8,128)} %bitcast.96, s32[128,16,128]{2,1,0:T(8,128)} %bitcast.97), custom_call_target="tpu_custom_call" | custom-call | flops 2097152 | bytes 1581056 | tf_op jit(solution)/shard_map/pallas_call | solution.py:82
  74.6 0.0 copy-done.3
  74.6 20.5 %all-gather = f32[4,1,2048]{2,1,0:T(1,128)S(1)} all-gather(f32[1,1,2048]{2,1,0:T(1,128)} %bitcast.103), channel_id=1, replica_groups=mesh['act'=4,'axial'=16,'hoop'=8] {'act'}, dimensions={0}, use_global_device_ids=true | all-gather | bytes 40960 | tf_op jit(solution)/shard_map/all_gather | solution.py:154
  95.1 0.6 fusion.41
  (14 shorter events, 0.1 us)
Async XLA Ops:
  0.6 0.8 copy-start.2
  1.5 0.7 copy-start.5
  2.1 0.9 copy-start.1
  3.1 15.7 %copy-start.4 = (f32[8,6]{1,0:T(8,128)S(1)}, f32[8,6]{1,0:T(8,128)}, u32[]{:S(2)}) copy-start(f32[8,6]{1,0:T(8,128)} %param.9) | copy-start | bytes 580
  3.2 15.7 %collective-permute-start = (f32[6,16,6]{2,1,0:T(8,128)S(1)}, f32[6,16,6]{2,1,0:T(8,128)S(1)}, u32[]{:S(2)}, u32[]{:S(2)}) collective-permute-start(f32[6,16,6]{2,1,0:T(8,128)S(1)} %get-tuple-element.49), channel_id=1, source_target_pairs={{0,1},{1,2},{2,3},{3,4},{4,5},{5,6},{6,7},{7,0},{8,9},{9,10},{10,1... | collective-permute-start | bytes 6920 | tf_op jit(solution)/shard_map/ppermute | solution.py:17
  7.5 12.4 %collective-permute-start.1 = (f32[6,16,6]{2,1,0:T(8,128)S(1)}, f32[6,16,6]{2,1,0:T(8,128)S(1)}, u32[]{:S(2)}, u32[]{:S(2)}) collective-permute-start(f32[6,16,6]{2,1,0:T(8,128)S(1)} %get-tuple-element.50), channel_id=1, source_target_pairs={{1,0},{2,1},{3,2},{4,3},{5,4},{6,5},{7,6},{0,7},{9,8},{10,9},{11,1... | collective-permute-start | bytes 6920 | tf_op jit(solution)/shard_map/ppermute | solution.py:18
  20.1 5.1 %collective-permute-start.2 = (f32[6,6,524]{2,1,0:T(8,128)S(1)}, f32[6,6,524]{2,1,0:T(8,128)S(1)}, u32[]{:S(2)}, u32[]{:S(2)}) collective-permute-start(f32[6,6,524]{2,1,0:T(8,128)S(1)} %get-tuple-element.45), channel_id=1, source_target_pairs={{0,8},{8,16},{16,24},{24,32},{32,40},{40,48},{48,56},{56,64},{64,7... | collective-permute-start | bytes 226376 | tf_op jit(solution)/shard_map/ppermute | solution.py:20
  23.3 5.6 %collective-permute-start.3 = (f32[6,6,524]{2,1,0:T(8,128)S(1)}, f32[6,6,524]{2,1,0:T(8,128)S(1)}, u32[]{:S(2)}, u32[]{:S(2)}) collective-permute-start(f32[6,6,524]{2,1,0:T(8,128)S(1)} %get-tuple-element.46), channel_id=1, source_target_pairs={{8,0},{16,8},{24,16},{32,24},{40,32},{48,40},{56,48},{64,56},{72,6... | collective-permute-start | bytes 226376 | tf_op jit(solution)/shard_map/ppermute | solution.py:21
  33.0 19.1 %all-to-all-start = ((f32[8,4,256]{2,1,0:T(4,128)}), f32[8,4,256]{2,1,0:T(4,128)S(1)}, u32[]{:S(2)}, u32[]{:S(2)}) async-start(f32[8,4,256]{2,1,0:T(4,128)} %broadcast_in_dim.237), calls=%async_computation | async-start | bytes 65536 | tf_op jit(solution)/shard_map/all_to_all | solution.py:101
  53.0 16.9 %all-to-all-start.1 = ((f32[16,32,256]{2,1,0:T(8,128)}), f32[16,32,256]{2,1,0:T(8,128)S(1)}, u32[]{:S(2)}, u32[]{:S(2)}) async-start(f32[16,32,256]{2,1,0:T(8,128)} %broadcast_in_dim.239), calls=%async_computation.1 | async-start | bytes 1048576 | tf_op jit(solution)/shard_map/all_to_all | solution.py:101
  61.7 12.9 %copy-start.3 = (f32[5,16,512]{2,1,0:T(8,128)}, f32[5,16,512]{2,1,0:T(8,128)S(1)}, u32[]{:S(2)}) copy-start(f32[5,16,512]{2,1,0:T(8,128)S(1)} %fusion.35) | copy-start | bytes 491524
  69.9 0.8 copy-start

commit v13 on v12

--- a/solution.py
+++ b/solution.py
@@ -118,6 +118,8 @@
     hist_wide = jnp.concatenate(
         [hist, jnp.zeros((hist.shape[0], STEPS), jnp.float32)], axis=1
     )
+    hoop_count = lax.axis_size("hoop")
+    hist_wide = jnp.broadcast_to(hist_wide[None], (hoop_count,) + hist_wide.shape)
     cell = lax.broadcasted_iota(jnp.int32, (sensors.shape[0], rows * cols), 1)
     hit = cell == sensors[:, None]
     stacked, hist_wide, hit = lax.optimization_barrier((stacked, hist_wide, hit))
@@ -146,10 +148,13 @@
         moduli_map = jnp.stack(moduli_map)
     next_state = jnp.stack(fields)[None]
     recorded = jnp.stack(samples, axis=1)[None]
-    column = lax.broadcasted_iota(jnp.int32, hist_wide.shape, 1)
+    column = lax.broadcasted_iota(jnp.int32, hist_wide.shape, hist_wide.ndim - 1)
     trace_wide = jnp.pad(recorded[0], ((0, 0), (hist_count, 0)))
-    local_waves = jnp.where(column >= hist_count, trace_wide, hist_wide)
-    waveforms = gather_waves(local_waves)
+    spread = jnp.where(column >= hist_count, trace_wide[None], hist_wide)
+    inner_waves = lax.all_to_all(spread, "hoop", 0, 0, tiled=True).reshape(
+        (-1,) + spread.shape[2:]
+    )
+    waveforms = a2a_gather(inner_waves, "axial", lax.axis_size("axial"))
     partial_value = image(receivers[0], waveforms, delays[0])
     parts = lax.all_gather(partial_value.reshape(-1), "act").reshape((-1,) + partial_value.shape)
     summed = parts[0]

time: 96.2 us -> 95.6 us (level)
  local copies, waits for them, and re-layouts: 5.59 us -> 2.78 us
  other arithmetic: 4.04 us -> 6.25 us
    all_to_all x2 -> x1, starting transfers between devices: 17.6 us -> 7.96 us  [a2a_gather(): gathered = lax.all_to_all(spread, axes, 0, 0, tiled=True)]
    all_to_all x0 -> x1, starting transfers between devices: none -> 9.64 us  [per_device(): lax.all_to_all(spread, 'hoop', 0, 0, tiled=True)]
    all_to_all x0 -> x1, waiting for transfers between devices: none -> 9.41 us  [per_device(): lax.all_to_all(spread, 'hoop', 0, 0, tiled=True)]
    all_to_all x2 -> x1, waiting for transfers between devices: 17.6 us -> 8.22 us  [a2a_gather(): gathered = lax.all_to_all(spread, axes, 0, 0, tiled=True)]
    unnamed x21 -> x19, local copies, waits for them, and re-layouts: 3.82 us -> 1.66 us
where the time goes in v13:
time: 95.6 us; the launch traced here: 95.1 us
  starting transfers between devices  37.7 us (39%)
  waiting for transfers between devices  23 us (24%)
  blocking collectives  20.5 us (21%)
  other arithmetic  6.25 us (7%)
  Pallas kernels  3.85 us (4%)
  local copies, waits for them, and re-layouts  2.78 us (3%)
    all_gather x1, blocking collectives, per_device(): lax.all_gather(partial_value.reshape(-1), 'act')  20.5 us
    ppermute x1, starting transfers between devices, exchange(): lax.ppermute(cells[:, :, :halo], 'hoop', [((j + 1) % nh, j) for j in rang...  11.3 us
    all_to_all x1, starting transfers between devices, per_device(): lax.all_to_all(spread, 'hoop', 0, 0, tiled=True)  9.64 us
    all_to_all x1, waiting for transfers between devices, per_device(): lax.all_to_all(spread, 'hoop', 0, 0, tiled=True)  9.41 us
    all_to_all x1, waiting for transfers between devices, a2a_gather(): gathered = lax.all_to_all(spread, axes, 0, 0, tiled=True)  8.22 us
    all_to_all x1, starting transfers between devices, a2a_gather(): gathered = lax.all_to_all(spread, axes, 0, 0, tiled=True)  7.96 us
    ppermute x1, starting transfers between devices, exchange(): lax.ppermute(cells[:, :, -halo:], 'hoop', [(j, (j + 1) % nh) for j in ran...  4.37 us
    pallas_call x1, Pallas kernels, image(): pl.pallas_call(image_kernel, out_shape=jax.ShapeDtypeStruct((pix_rows, pi...  3.85 us
  transfers between devices with their start and end apart: 6, of which 5 were waited for; matrix products, arithmetic and copies ran while one was open for 1% of the time, Pallas kernels for 0%

profile of v13, /device:TPU:1, one launch (start us, length us, event | category | flops | bytes accessed | tf_op | source)
XLA Modules:
  0.0 95.1 jit_solution(5493420939332623262)
XLA Ops:
  0.6 0.0 copy-start.4
  0.6 0.8 convert_bitcast_fusion
  1.4 0.0 copy-done.4
  1.4 0.1 iota_compare_fusion
  1.5 0.0 copy-start.2
  1.5 0.9 pad_maximum_fusion.2
  2.5 0.0 copy-done.2
  2.5 0.0 copy-start.3
  2.5 0.1 fusion.46
  2.6 4.4 %collective-permute-start = (f32[6,16,6]{2,1,0:T(8,128)S(1)}, f32[6,16,6]{2,1,0:T(8,128)S(1)}, u32[]{:S(2)}, u32[]{:S(2)}) collective-permute-start(f32[6,16,6]{2,1,0:T(8,128)S(1)} %get-tuple-element.49), channel_id=1, source_target_pairs={{0,1},{1,2},{2,3},{3,4},{4,5},{5,6},{6,7},{7,0},{8,9},{9,10},{10,1... | collective-permute-start | bytes 6920 | tf_op jit(solution)/shard_map/ppermute | solution.py:17
  7.0 11.3 %collective-permute-start.1 = (f32[6,16,6]{2,1,0:T(8,128)S(1)}, f32[6,16,6]{2,1,0:T(8,128)S(1)}, u32[]{:S(2)}, u32[]{:S(2)}) collective-permute-start(f32[6,16,6]{2,1,0:T(8,128)S(1)} %get-tuple-element.50), channel_id=1, source_target_pairs={{1,0},{2,1},{3,2},{4,3},{5,4},{6,5},{7,6},{0,7},{9,8},{10,9},{11,1... | collective-permute-start | bytes 6920 | tf_op jit(solution)/shard_map/ppermute | solution.py:18
  18.2 0.0 copy-done.3
  18.3 0.0 collective-permute-done
  18.3 1.1 %collective-permute-done.1 = f32[6,16,6]{2,1,0:T(8,128)S(1)} collective-permute-done((f32[6,16,6]{2,1,0:T(8,128)S(1)}, f32[6,16,6]{2,1,0:T(8,128)S(1)}, u32[]{:S(2)}, u32[]{:S(2)}) %collective-permute-start.1) | collective-permute-done | bytes 2336 | tf_op jit(solution)/shard_map/ppermute | solution.py:18
  19.4 0.1 pad_maximum_fusion.1
  19.6 3.2 %collective-permute-start.2 = (f32[6,6,524]{2,1,0:T(8,128)S(1)}, f32[6,6,524]{2,1,0:T(8,128)S(1)}, u32[]{:S(2)}, u32[]{:S(2)}) collective-permute-start(f32[6,6,524]{2,1,0:T(8,128)S(1)} %get-tuple-element.45), channel_id=1, source_target_pairs={{0,8},{8,16},{16,24},{24,32},{32,40},{40,48},{48,56},{56,64},{64,7... | collective-permute-start | bytes 226376 | tf_op jit(solution)/shard_map/ppermute | solution.py:20
  22.8 1.3 %collective-permute-start.3 = (f32[6,6,524]{2,1,0:T(8,128)S(1)}, f32[6,6,524]{2,1,0:T(8,128)S(1)}, u32[]{:S(2)}, u32[]{:S(2)}) collective-permute-start(f32[6,6,524]{2,1,0:T(8,128)S(1)} %get-tuple-element.46), channel_id=1, source_target_pairs={{8,0},{16,8},{24,16},{32,24},{40,32},{48,40},{56,48},{64,56},{72,6... | collective-permute-start | bytes 226376 | tf_op jit(solution)/shard_map/ppermute | solution.py:21
  24.1 0.5 collective-permute-done.2
  24.6 3.8 %collective-permute-done.3 = f32[6,6,524]{2,1,0:T(8,128)S(1)} collective-permute-done((f32[6,6,524]{2,1,0:T(8,128)S(1)}, f32[6,6,524]{2,1,0:T(8,128)S(1)}, u32[]{:S(2)}, u32[]{:S(2)}) %collective-permute-start.3) | collective-permute-done | bytes 75488 | tf_op jit(solution)/shard_map/ppermute | solution.py:21
  28.4 0.2 pad_maximum_fusion
  28.6 0.1 compare_bitcast_fusion.7
  28.7 0.6 select_select_fusion
  29.3 0.1 slice_bitcast_fusion.6
  29.4 0.3 fusion.5
  29.7 0.2 fusion.27
  29.9 0.2 fusion.29
  30.1 0.1 fusion.30
  30.2 0.2 fusion.24
  30.4 0.2 fusion.9
  30.6 0.2 fusion.15
  30.8 0.2 fusion.8
  31.1 0.1 bitcast_dynamic-update-slice_fusion.3
  31.1 0.1 add_bitcast_fusion
  31.3 0.3 select_reduce_fusion.2
  31.6 0.1 copy.21
  31.7 0.1 pad.5.clone
  31.8 0.6 broadcast_select_fusion
  32.4 9.6 %all-to-all-start = ((f32[8,4,256]{2,1,0:T(4,128)}), f32[8,4,256]{2,1,0:T(4,128)S(1)}, u32[]{:S(2)}, u32[]{:S(2)}) async-start(f32[8,4,256]{2,1,0:T(4,128)} %broadcast_select_fusion), calls=%async_computation | async-start | bytes 65536 | tf_op jit(solution)/shard_map/all_to_all | solution.py:154
  42.1 0.1 bitcast_dynamic-update-slice_fusion.2
  42.1 9.4 %all-to-all-done = f32[8,4,256]{2,1,0:T(4,128)S(1)} async-done(((f32[8,4,256]{2,1,0:T(4,128)}), f32[8,4,256]{2,1,0:T(4,128)S(1)}, u32[]{:S(2)}, u32[]{:S(2)}) %all-to-all-start) | async-done | bytes 32800 | tf_op jit(solution)/shard_map/all_to_all | solution.py:154
  51.6 0.8 broadcast_in_dim.249
  52.4 8.0 %all-to-all-start.1 = ((f32[16,32,256]{2,1,0:T(8,128)}), f32[16,32,256]{2,1,0:T(8,128)S(1)}, u32[]{:S(2)}, u32[]{:S(2)}) async-start(f32[16,32,256]{2,1,0:T(8,128)} %broadcast_in_dim.249), calls=%async_computation.1 | async-start | bytes 1048576 | tf_op jit(solution)/shard_map/all_to_all | solution.py:101
  60.4 0.6 copy.18
  61.0 0.1 fusion.35
  61.1 0.0 copy-start.1
  61.1 8.2 %all-to-all-done.1 = f32[16,32,256]{2,1,0:T(8,128)S(1)} async-done(((f32[16,32,256]{2,1,0:T(8,128)}), f32[16,32,256]{2,1,0:T(8,128)S(1)}, u32[]{:S(2)}, u32[]{:S(2)}) %all-to-all-start.1) | async-done | bytes 524320 | tf_op jit(solution)/shard_map/all_to_all | solution.py:101
  69.3 0.0 copy-start
  69.3 0.8 copy-done
  70.1 3.8 %shard_map.94 = f32[16,128]{1,0:T(8,128)} custom-call(s32[128]{0:T(128)} %bitcast.109, f32[512,256]{1,0:T(8,128)} %bitcast.96, s32[128,16,128]{2,1,0:T(8,128)} %bitcast.97), custom_call_target="tpu_custom_call" | custom-call | flops 2097152 | bytes 1581056 | tf_op jit(solution)/shard_map/pallas_call | solution.py:82
  74.0 0.0 copy-done.1
  74.0 20.5 %all-gather = f32[4,1,2048]{2,1,0:T(1,128)S(1)} all-gather(f32[1,1,2048]{2,1,0:T(1,128)} %bitcast.102), channel_id=1, replica_groups=mesh['act'=4,'axial'=16,'hoop'=8] {'act'}, dimensions={0}, use_global_device_ids=true | all-gather | bytes 40960 | tf_op jit(solution)/shard_map/all_gather | solution.py:159
  94.5 0.6 fusion.41
  (13 shorter events, 0.1 us)
Async XLA Ops:
  0.6 0.8 copy-start.4
  1.5 1.0 %copy-start.2 = (f32[1,4,253]{2,1,0:T(4,128)S(1)}, f32[1,4,253]{2,1,0:T(4,128)}, u32[]{:S(2)}) copy-start(f32[1,4,253]{2,1,0:T(4,128)} %param.11) | copy-start | bytes 12148
  2.5 15.7 %copy-start.3 = (f32[8,6]{1,0:T(8,128)S(1)}, f32[8,6]{1,0:T(8,128)}, u32[]{:S(2)}) copy-start(f32[8,6]{1,0:T(8,128)} %param.9) | copy-start | bytes 580
  2.6 15.7 %collective-permute-start = (f32[6,16,6]{2,1,0:T(8,128)S(1)}, f32[6,16,6]{2,1,0:T(8,128)S(1)}, u32[]{:S(2)}, u32[]{:S(2)}) collective-permute-start(f32[6,16,6]{2,1,0:T(8,128)S(1)} %get-tuple-element.49), channel_id=1, source_target_pairs={{0,1},{1,2},{2,3},{3,4},{4,5},{5,6},{6,7},{7,0},{8,9},{9,10},{10,1... | collective-permute-start | bytes 6920 | tf_op jit(solution)/shard_map/ppermute | solution.py:17
  7.0 12.4 %collective-permute-start.1 = (f32[6,16,6]{2,1,0:T(8,128)S(1)}, f32[6,16,6]{2,1,0:T(8,128)S(1)}, u32[]{:S(2)}, u32[]{:S(2)}) collective-permute-start(f32[6,16,6]{2,1,0:T(8,128)S(1)} %get-tuple-element.50), channel_id=1, source_target_pairs={{1,0},{2,1},{3,2},{4,3},{5,4},{6,5},{7,6},{0,7},{9,8},{10,9},{11,1... | collective-permute-start | bytes 6920 | tf_op jit(solution)/shard_map/ppermute | solution.py:18
  19.6 5.1 %collective-permute-start.2 = (f32[6,6,524]{2,1,0:T(8,128)S(1)}, f32[6,6,524]{2,1,0:T(8,128)S(1)}, u32[]{:S(2)}, u32[]{:S(2)}) collective-permute-start(f32[6,6,524]{2,1,0:T(8,128)S(1)} %get-tuple-element.45), channel_id=1, source_target_pairs={{0,8},{8,16},{16,24},{24,32},{32,40},{40,48},{48,56},{56,64},{64,7... | collective-permute-start | bytes 226376 | tf_op jit(solution)/shard_map/ppermute | solution.py:20
  22.8 5.6 %collective-permute-start.3 = (f32[6,6,524]{2,1,0:T(8,128)S(1)}, f32[6,6,524]{2,1,0:T(8,128)S(1)}, u32[]{:S(2)}, u32[]{:S(2)}) collective-permute-start(f32[6,6,524]{2,1,0:T(8,128)S(1)} %get-tuple-element.46), channel_id=1, source_target_pairs={{8,0},{16,8},{24,16},{32,24},{40,32},{48,40},{56,48},{64,56},{72,6... | collective-permute-start | bytes 226376 | tf_op jit(solution)/shard_map/ppermute | solution.py:21
  32.4 19.1 %all-to-all-start = ((f32[8,4,256]{2,1,0:T(4,128)}), f32[8,4,256]{2,1,0:T(4,128)S(1)}, u32[]{:S(2)}, u32[]{:S(2)}) async-start(f32[8,4,256]{2,1,0:T(4,128)} %broadcast_select_fusion), calls=%async_computation | async-start | bytes 65536 | tf_op jit(solution)/shard_map/all_to_all | solution.py:154
  52.4 16.9 %all-to-all-start.1 = ((f32[16,32,256]{2,1,0:T(8,128)}), f32[16,32,256]{2,1,0:T(8,128)S(1)}, u32[]{:S(2)}, u32[]{:S(2)}) async-start(f32[16,32,256]{2,1,0:T(8,128)} %broadcast_in_dim.249), calls=%async_computation.1 | async-start | bytes 1048576 | tf_op jit(solution)/shard_map/all_to_all | solution.py:101
  61.1 12.9 %copy-start.1 = (f32[5,16,512]{2,1,0:T(8,128)}, f32[5,16,512]{2,1,0:T(8,128)S(1)}, u32[]{:S(2)}) copy-start(f32[5,16,512]{2,1,0:T(8,128)S(1)} %fusion.35) | copy-start | bytes 491524
  69.3 0.8 copy-start

commit v14 on v13

--- a/solution.py
+++ b/solution.py
@@ -110,9 +110,12 @@
 def per_device(wave_state, layup_zone, moduli, sensors, history, receivers, delays):
     rows, cols = layup_zone.shape
     na = lax.axis_size("axial")
-    stacked = jnp.concatenate(
-        [wave_state[0], layup_zone.astype(jnp.float32)[None]], axis=0
-    )
+    local_moduli = jnp.zeros((moduli.shape[1],) + layup_zone.shape, jnp.float32)
+    for zone_level in range(moduli.shape[0]):
+        local_moduli = jnp.where(
+            (layup_zone == zone_level)[None], moduli[zone_level][:, None, None], local_moduli
+        )
+    stacked = jnp.concatenate([wave_state[0], local_moduli], axis=0)
     hist = history[0]
     hist_count = hist.shape[1]
     hist_wide = jnp.concatenate(
@@ -124,17 +127,7 @@
     hit = cell == sensors[:, None]
     stacked, hist_wide, hit = lax.optimization_barrier((stacked, hist_wide, hit))
     padded = exchange(stacked, HALO)
-    zone = padded[5].astype(jnp.int32)
-    global_row = lax.axis_index("axial") * rows - HALO + lax.broadcasted_iota(
-        jnp.int32, zone.shape, 0
-    )
-    inside = (global_row >= 0) & (global_row < na * rows)
-    moduli_map = jnp.zeros((moduli.shape[1],) + zone.shape, jnp.float32)
-    for zone_level in range(moduli.shape[0]):
-        moduli_map = jnp.where(
-            (zone == zone_level)[None], moduli[zone_level][:, None, None], moduli_map
-        )
-    moduli_map = jnp.where(inside[None], moduli_map, jnp.float32(0.0))
+    moduli_map = padded[5:]
     fields = tuple(padded[c] for c in range(5))
     samples = []
     for step_index in range(STEPS):

time: 95.6 us -> 97.9 us (1.024)
  local copies, waits for them, and re-layouts: 2.78 us -> 4.76 us
  waiting for transfers between devices: 23 us -> 24.6 us
  other arithmetic: 6.25 us -> 4.97 us
    unnamed x19 -> x21, local copies, waits for them, and re-layouts: 1.66 us -> 3.6 us
    ppermute x1, waiting for transfers between devices: 0.53 us -> 1.58 us  [exchange(): lax.ppermute(cells[:, -halo:, :], 'axial', [(i, i + 1) for i in range(na...]
  transfers between devices with their start and end apart: 6 -> 6, of which waited for: 5 -> 6; matrix products, arithmetic and copies ran while one was open for 1% -> 1% of each run, Pallas kernels for 0% -> 0%
where the time goes in v14:
time: 97.9 us; the launch traced here: 97.4 us
  starting transfers between devices  37.8 us (39%)
  waiting for transfers between devices  24.6 us (25%)
  blocking collectives  20.5 us (21%)
  other arithmetic  4.97 us (5%)
  local copies, waits for them, and re-layouts  4.76 us (5%)
  Pallas kernels  3.85 us (4%)
    all_gather x1, blocking collectives, per_device(): lax.all_gather(partial_value.reshape(-1), 'act')  20.5 us
    ppermute x1, starting transfers between devices, exchange(): lax.ppermute(cells[:, :, :halo], 'hoop', [((j + 1) % nh, j) for j in rang...  11.3 us
    all_to_all x1, starting transfers between devices, per_device(): lax.all_to_all(spread, 'hoop', 0, 0, tiled=True)  9.7 us
    all_to_all x1, waiting for transfers between devices, per_device(): lax.all_to_all(spread, 'hoop', 0, 0, tiled=True)  9.41 us
    all_to_all x1, waiting for transfers between devices, a2a_gather(): gathered = lax.all_to_all(spread, axes, 0, 0, tiled=True)  8.22 us
    all_to_all x1, starting transfers between devices, a2a_gather(): gathered = lax.all_to_all(spread, axes, 0, 0, tiled=True)  7.95 us
    ppermute x1, starting transfers between devices, exchange(): lax.ppermute(cells[:, :, -halo:], 'hoop', [(j, (j + 1) % nh) for j in ran...  4.38 us
    pallas_call x1, Pallas kernels, image(): pl.pallas_call(image_kernel, out_shape=jax.ShapeDtypeStruct((pix_rows, pi...  3.85 us
  transfers between devices with their start and end apart: 6, of which 6 were waited for; matrix products, arithmetic and copies ran while one was open for 1% of the time, Pallas kernels for 0%

profile of v14, /device:TPU:1, one launch (start us, length us, event | category | flops | bytes accessed | tf_op | source)
XLA Modules:
  0.0 97.4 jit_solution(14611575843207759314)
XLA Ops:
  0.6 0.0 copy-start.3
  0.6 0.8 broadcast_compare_fusion.7
  1.4 0.0 copy-done.3
  1.5 0.0 copy-start.5
  1.5 0.6 copy-done.5
  2.1 0.0 copy-start.1
  2.1 0.1 iota_compare_fusion
  2.2 0.2 select_select_fusion
  2.4 0.6 copy-done.1
  3.0 0.0 copy-start.4
  3.1 0.7 copy-done.4
  3.7 0.1 fusion.46
  3.8 4.4 %collective-permute-start = (f32[11,16,6]{2,1,0:T(8,128)S(1)}, f32[11,16,6]{2,1,0:T(8,128)S(1)}, u32[]{:S(2)}, u32[]{:S(2)}) collective-permute-start(f32[11,16,6]{2,1,0:T(8,128)S(1)} %get-tuple-element.37), channel_id=1, source_target_pairs={{0,1},{1,2},{2,3},{3,4},{4,5},{5,6},{6,7},{7,0},{8,9},{9,10},{10,1... | collective-permute-start | bytes 12680 | tf_op jit(solution)/shard_map/ppermute | solution.py:17
  8.2 11.3 %collective-permute-start.1 = (f32[11,16,6]{2,1,0:T(8,128)S(1)}, f32[11,16,6]{2,1,0:T(8,128)S(1)}, u32[]{:S(2)}, u32[]{:S(2)}) collective-permute-start(f32[11,16,6]{2,1,0:T(8,128)S(1)} %get-tuple-element.38), channel_id=1, source_target_pairs={{1,0},{2,1},{3,2},{4,3},{5,4},{6,5},{7,6},{0,7},{9,8},{10,9},{11,1... | collective-permute-start | bytes 12680 | tf_op jit(solution)/shard_map/ppermute | solution.py:18
  19.5 0.1 collective-permute-done
  19.5 1.5 %collective-permute-done.1 = f32[11,16,6]{2,1,0:T(8,128)S(1)} collective-permute-done((f32[11,16,6]{2,1,0:T(8,128)S(1)}, f32[11,16,6]{2,1,0:T(8,128)S(1)}, u32[]{:S(2)}, u32[]{:S(2)}) %collective-permute-start.1) | collective-permute-done | bytes 4256 | tf_op jit(solution)/shard_map/ppermute | solution.py:18
  21.0 0.2 pad_maximum_fusion.1
  21.3 3.2 %collective-permute-start.2 = (f32[11,6,524]{2,1,0:T(8,128)S(1)}, f32[11,6,524]{2,1,0:T(8,128)S(1)}, u32[]{:S(2)}, u32[]{:S(2)}) collective-permute-start(f32[11,6,524]{2,1,0:T(8,128)S(1)} %get-tuple-element.35), channel_id=1, source_target_pairs={{0,8},{8,16},{16,24},{24,32},{32,40},{40,48},{48,56},{56,64},{64,7... | collective-permute-start | bytes 415016 | tf_op jit(solution)/shard_map/ppermute | solution.py:20
  24.5 1.3 %collective-permute-start.3 = (f32[11,6,524]{2,1,0:T(8,128)S(1)}, f32[11,6,524]{2,1,0:T(8,128)S(1)}, u32[]{:S(2)}, u32[]{:S(2)}) collective-permute-start(f32[11,6,524]{2,1,0:T(8,128)S(1)} %get-tuple-element.36), channel_id=1, source_target_pairs={{8,0},{16,8},{24,16},{32,24},{40,32},{48,40},{56,48},{64,56},{72,6... | collective-permute-start | bytes 415016 | tf_op jit(solution)/shard_map/ppermute | solution.py:21
  25.8 1.6 %collective-permute-done.2 = f32[11,6,524]{2,1,0:T(8,128)S(1)} collective-permute-done((f32[11,6,524]{2,1,0:T(8,128)S(1)}, f32[11,6,524]{2,1,0:T(8,128)S(1)}, u32[]{:S(2)}, u32[]{:S(2)}) %collective-permute-start.2) | collective-permute-done | bytes 138368 | tf_op jit(solution)/shard_map/ppermute | solution.py:20
  27.4 3.8 %collective-permute-done.3 = f32[11,6,524]{2,1,0:T(8,128)S(1)} collective-permute-done((f32[11,6,524]{2,1,0:T(8,128)S(1)}, f32[11,6,524]{2,1,0:T(8,128)S(1)}, u32[]{:S(2)}, u32[]{:S(2)}) %collective-permute-start.3) | collective-permute-done | bytes 138368 | tf_op jit(solution)/shard_map/ppermute | solution.py:21
  31.2 0.3 pad_maximum_fusion
  31.5 0.1 slice_bitcast_fusion.6
  31.6 0.3 fusion.5
  31.9 0.2 fusion.27
  32.0 0.2 fusion.29
  32.3 0.1 fusion.30
  32.3 0.2 fusion.24
  32.6 0.2 fusion.9
  32.8 0.2 fusion.15
  33.0 0.2 fusion.8
  33.2 0.1 bitcast_dynamic-update-slice_fusion.3
  33.3 0.1 add_bitcast_fusion
  33.5 0.3 select_reduce_fusion.2
  33.8 0.1 copy.21
  33.9 0.1 pad.5.clone
  33.9 0.6 broadcast_select_fusion
  34.6 9.7 %all-to-all-start = ((f32[8,4,256]{2,1,0:T(4,128)}), f32[8,4,256]{2,1,0:T(4,128)S(1)}, u32[]{:S(2)}, u32[]{:S(2)}) async-start(f32[8,4,256]{2,1,0:T(4,128)} %broadcast_select_fusion), calls=%async_computation | async-start | bytes 65536 | tf_op jit(solution)/shard_map/all_to_all | solution.py:147
  44.3 0.1 bitcast_dynamic-update-slice_fusion.2
  44.3 9.4 %all-to-all-done = f32[8,4,256]{2,1,0:T(4,128)S(1)} async-done(((f32[8,4,256]{2,1,0:T(4,128)}), f32[8,4,256]{2,1,0:T(4,128)S(1)}, u32[]{:S(2)}, u32[]{:S(2)}) %all-to-all-start) | async-done | bytes 32800 | tf_op jit(solution)/shard_map/all_to_all | solution.py:147
  53.8 0.9 broadcast_in_dim.209
  54.6 8.0 %all-to-all-start.1 = ((f32[16,32,256]{2,1,0:T(8,128)}), f32[16,32,256]{2,1,0:T(8,128)S(1)}, u32[]{:S(2)}, u32[]{:S(2)}) async-start(f32[16,32,256]{2,1,0:T(8,128)} %broadcast_in_dim.209), calls=%async_computation.1 | async-start | bytes 1048576 | tf_op jit(solution)/shard_map/all_to_all | solution.py:101
  62.6 0.6 copy.18
  63.2 0.1 fusion.35
  63.3 0.0 copy-start.2
  63.3 8.2 %all-to-all-done.1 = f32[16,32,256]{2,1,0:T(8,128)S(1)} async-done(((f32[16,32,256]{2,1,0:T(8,128)}), f32[16,32,256]{2,1,0:T(8,128)S(1)}, u32[]{:S(2)}, u32[]{:S(2)}) %all-to-all-start.1) | async-done | bytes 524320 | tf_op jit(solution)/shard_map/all_to_all | solution.py:101
  71.5 0.0 copy-start
  71.5 0.8 copy-done
  72.3 3.8 %shard_map.94 = f32[16,128]{1,0:T(8,128)} custom-call(s32[128]{0:T(128)} %bitcast.91, f32[512,256]{1,0:T(8,128)} %bitcast.78, s32[128,16,128]{2,1,0:T(8,128)} %bitcast.79), custom_call_target="tpu_custom_call" | custom-call | flops 2097152 | bytes 1581056 | tf_op jit(solution)/shard_map/pallas_call | solution.py:82
  76.2 0.0 copy-done.2
  76.2 20.5 %all-gather = f32[4,1,2048]{2,1,0:T(1,128)S(1)} all-gather(f32[1,1,2048]{2,1,0:T(1,128)} %bitcast.84), channel_id=1, replica_groups=mesh['act'=4,'axial'=16,'hoop'=8] {'act'}, dimensions={0}, use_global_device_ids=true | all-gather | bytes 40960 | tf_op jit(solution)/shard_map/all_gather | solution.py:152
  96.7 0.6 fusion.41
  (13 shorter events, 0.2 us)
Async XLA Ops:
  0.6 0.8 copy-start.3
  1.5 0.7 copy-start.5
  2.1 0.9 copy-start.1
  3.0 0.7 copy-start.4
  3.8 15.7 %collective-permute-start = (f32[11,16,6]{2,1,0:T(8,128)S(1)}, f32[11,16,6]{2,1,0:T(8,128)S(1)}, u32[]{:S(2)}, u32[]{:S(2)}) collective-permute-start(f32[11,16,6]{2,1,0:T(8,128)S(1)} %get-tuple-element.37), channel_id=1, source_target_pairs={{0,1},{1,2},{2,3},{3,4},{4,5},{5,6},{6,7},{7,0},{8,9},{9,10},{10,1... | collective-permute-start | bytes 12680 | tf_op jit(solution)/shard_map/ppermute | solution.py:17
  8.2 12.8 %collective-permute-start.1 = (f32[11,16,6]{2,1,0:T(8,128)S(1)}, f32[11,16,6]{2,1,0:T(8,128)S(1)}, u32[]{:S(2)}, u32[]{:S(2)}) collective-permute-start(f32[11,16,6]{2,1,0:T(8,128)S(1)} %get-tuple-element.38), channel_id=1, source_target_pairs={{1,0},{2,1},{3,2},{4,3},{5,4},{6,5},{7,6},{0,7},{9,8},{10,9},{11,1... | collective-permute-start | bytes 12680 | tf_op jit(solution)/shard_map/ppermute | solution.py:18
  21.3 6.1 %collective-permute-start.2 = (f32[11,6,524]{2,1,0:T(8,128)S(1)}, f32[11,6,524]{2,1,0:T(8,128)S(1)}, u32[]{:S(2)}, u32[]{:S(2)}) collective-permute-start(f32[11,6,524]{2,1,0:T(8,128)S(1)} %get-tuple-element.35), channel_id=1, source_target_pairs={{0,8},{8,16},{16,24},{24,32},{32,40},{40,48},{48,56},{56,64},{64,7... | collective-permute-start | bytes 415016 | tf_op jit(solution)/shard_map/ppermute | solution.py:20
  24.5 6.7 %collective-permute-start.3 = (f32[11,6,524]{2,1,0:T(8,128)S(1)}, f32[11,6,524]{2,1,0:T(8,128)S(1)}, u32[]{:S(2)}, u32[]{:S(2)}) collective-permute-start(f32[11,6,524]{2,1,0:T(8,128)S(1)} %get-tuple-element.36), channel_id=1, source_target_pairs={{8,0},{16,8},{24,16},{32,24},{40,32},{48,40},{56,48},{64,56},{72,6... | collective-permute-start | bytes 415016 | tf_op jit(solution)/shard_map/ppermute | solution.py:21
  34.6 19.2 %all-to-all-start = ((f32[8,4,256]{2,1,0:T(4,128)}), f32[8,4,256]{2,1,0:T(4,128)S(1)}, u32[]{:S(2)}, u32[]{:S(2)}) async-start(f32[8,4,256]{2,1,0:T(4,128)} %broadcast_select_fusion), calls=%async_computation | async-start | bytes 65536 | tf_op jit(solution)/shard_map/all_to_all | solution.py:147
  54.6 16.9 %all-to-all-start.1 = ((f32[16,32,256]{2,1,0:T(8,128)}), f32[16,32,256]{2,1,0:T(8,128)S(1)}, u32[]{:S(2)}, u32[]{:S(2)}) async-start(f32[16,32,256]{2,1,0:T(8,128)} %broadcast_in_dim.209), calls=%async_computation.1 | async-start | bytes 1048576 | tf_op jit(solution)/shard_map/all_to_all | solution.py:101
  63.3 12.9 %copy-start.2 = (f32[5,16,512]{2,1,0:T(8,128)}, f32[5,16,512]{2,1,0:T(8,128)S(1)}, u32[]{:S(2)}) copy-start(f32[5,16,512]{2,1,0:T(8,128)S(1)} %fusion.35) | copy-start | bytes 491524
  71.5 0.8 copy-start

commit v15 on v13

--- a/solution.py
+++ b/solution.py
@@ -73,7 +73,7 @@
             parts.append(jnp.where(d >= lanes, got_high, got_low))
         return acc + jnp.concatenate(parts, axis=0)
 
-    acc = lax.fori_loop(0, pairs, body, jnp.zeros((pix_rows, pix_cols), jnp.float32), unroll=16)
+    acc = lax.fori_loop(0, pairs, body, jnp.zeros((pix_rows, pix_cols), jnp.float32), unroll=32)
     out_ref[...] = acc
 
 

time: 95.6 us -> 95.3 us (level)
  no operation moved by 1% of the time
where the time goes in v15:
time: 95.3 us; the launch traced here: 94.8 us
  starting transfers between devices  37.7 us (40%)
  waiting for transfers between devices  23 us (24%)
  blocking collectives  20.5 us (22%)
  other arithmetic  6.25 us (7%)
  Pallas kernels  3.54 us (4%)
  local copies, waits for them, and re-layouts  2.78 us (3%)
    all_gather x1, blocking collectives, per_device(): lax.all_gather(partial_value.reshape(-1), 'act')  20.5 us
    ppermute x1, starting transfers between devices, exchange(): lax.ppermute(cells[:, :, :halo], 'hoop', [((j + 1) % nh, j) for j in rang...  11.3 us
    all_to_all x1, starting transfers between devices, per_device(): lax.all_to_all(spread, 'hoop', 0, 0, tiled=True)  9.64 us
    all_to_all x1, waiting for transfers between devices, per_device(): lax.all_to_all(spread, 'hoop', 0, 0, tiled=True)  9.41 us
    all_to_all x1, waiting for transfers between devices, a2a_gather(): gathered = lax.all_to_all(spread, axes, 0, 0, tiled=True)  8.22 us
    all_to_all x1, starting transfers between devices, a2a_gather(): gathered = lax.all_to_all(spread, axes, 0, 0, tiled=True)  7.96 us
    ppermute x1, starting transfers between devices, exchange(): lax.ppermute(cells[:, :, -halo:], 'hoop', [(j, (j + 1) % nh) for j in ran...  4.37 us
    ppermute x1, waiting for transfers between devices, exchange(): lax.ppermute(cells[:, :halo, :], 'axial', [(i + 1, i) for i in range(na -...  3.78 us
  transfers between devices with their start and end apart: 6, of which 5 were waited for; matrix products, arithmetic and copies ran while one was open for 1% of the time, Pallas kernels for 0%

profile of v15, /device:TPU:1, one launch (start us, length us, event | category | flops | bytes accessed | tf_op | source)
XLA Modules:
  0.0 94.8 jit_solution(9152265548896084587)
XLA Ops:
  0.6 0.0 copy-start.4
  0.6 0.8 convert_bitcast_fusion
  1.4 0.0 copy-done.4
  1.4 0.1 iota_compare_fusion
  1.5 0.0 copy-start.2
  1.5 0.9 pad_maximum_fusion.2
  2.5 0.0 copy-done.2
  2.5 0.0 copy-start.3
  2.5 0.1 fusion.46
  2.6 4.4 %collective-permute-start = (f32[6,16,6]{2,1,0:T(8,128)S(1)}, f32[6,16,6]{2,1,0:T(8,128)S(1)}, u32[]{:S(2)}, u32[]{:S(2)}) collective-permute-start(f32[6,16,6]{2,1,0:T(8,128)S(1)} %get-tuple-element.49), channel_id=1, source_target_pairs={{0,1},{1,2},{2,3},{3,4},{4,5},{5,6},{6,7},{7,0},{8,9},{9,10},{10,1... | collective-permute-start | bytes 6920 | tf_op jit(solution)/shard_map/ppermute | solution.py:17
  7.0 11.3 %collective-permute-start.1 = (f32[6,16,6]{2,1,0:T(8,128)S(1)}, f32[6,16,6]{2,1,0:T(8,128)S(1)}, u32[]{:S(2)}, u32[]{:S(2)}) collective-permute-start(f32[6,16,6]{2,1,0:T(8,128)S(1)} %get-tuple-element.50), channel_id=1, source_target_pairs={{1,0},{2,1},{3,2},{4,3},{5,4},{6,5},{7,6},{0,7},{9,8},{10,9},{11,1... | collective-permute-start | bytes 6920 | tf_op jit(solution)/shard_map/ppermute | solution.py:18
  18.2 0.0 copy-done.3
  18.3 0.0 collective-permute-done
  18.3 1.1 %collective-permute-done.1 = f32[6,16,6]{2,1,0:T(8,128)S(1)} collective-permute-done((f32[6,16,6]{2,1,0:T(8,128)S(1)}, f32[6,16,6]{2,1,0:T(8,128)S(1)}, u32[]{:S(2)}, u32[]{:S(2)}) %collective-permute-start.1) | collective-permute-done | bytes 2336 | tf_op jit(solution)/shard_map/ppermute | solution.py:18
  19.4 0.1 pad_maximum_fusion.1
  19.6 3.2 %collective-permute-start.2 = (f32[6,6,524]{2,1,0:T(8,128)S(1)}, f32[6,6,524]{2,1,0:T(8,128)S(1)}, u32[]{:S(2)}, u32[]{:S(2)}) collective-permute-start(f32[6,6,524]{2,1,0:T(8,128)S(1)} %get-tuple-element.45), channel_id=1, source_target_pairs={{0,8},{8,16},{16,24},{24,32},{32,40},{40,48},{48,56},{56,64},{64,7... | collective-permute-start | bytes 226376 | tf_op jit(solution)/shard_map/ppermute | solution.py:20
  22.8 1.3 %collective-permute-start.3 = (f32[6,6,524]{2,1,0:T(8,128)S(1)}, f32[6,6,524]{2,1,0:T(8,128)S(1)}, u32[]{:S(2)}, u32[]{:S(2)}) collective-permute-start(f32[6,6,524]{2,1,0:T(8,128)S(1)} %get-tuple-element.46), channel_id=1, source_target_pairs={{8,0},{16,8},{24,16},{32,24},{40,32},{48,40},{56,48},{64,56},{72,6... | collective-permute-start | bytes 226376 | tf_op jit(solution)/shard_map/ppermute | solution.py:21
  24.1 0.5 collective-permute-done.2
  24.6 3.8 %collective-permute-done.3 = f32[6,6,524]{2,1,0:T(8,128)S(1)} collective-permute-done((f32[6,6,524]{2,1,0:T(8,128)S(1)}, f32[6,6,524]{2,1,0:T(8,128)S(1)}, u32[]{:S(2)}, u32[]{:S(2)}) %collective-permute-start.3) | collective-permute-done | bytes 75488 | tf_op jit(solution)/shard_map/ppermute | solution.py:21
  28.4 0.2 pad_maximum_fusion
  28.6 0.1 compare_bitcast_fusion.7
  28.7 0.6 select_select_fusion
  29.3 0.1 slice_bitcast_fusion.6
  29.4 0.3 fusion.5
  29.7 0.2 fusion.27
  29.9 0.2 fusion.29
  30.1 0.1 fusion.30
  30.2 0.2 fusion.24
  30.4 0.2 fusion.9
  30.6 0.2 fusion.15
  30.8 0.2 fusion.8
  31.1 0.1 bitcast_dynamic-update-slice_fusion.3
  31.1 0.1 add_bitcast_fusion
  31.3 0.3 select_reduce_fusion.2
  31.6 0.1 copy.21
  31.7 0.1 pad.5.clone
  31.8 0.6 broadcast_select_fusion
  32.4 9.6 %all-to-all-start = ((f32[8,4,256]{2,1,0:T(4,128)}), f32[8,4,256]{2,1,0:T(4,128)S(1)}, u32[]{:S(2)}, u32[]{:S(2)}) async-start(f32[8,4,256]{2,1,0:T(4,128)} %broadcast_select_fusion), calls=%async_computation | async-start | bytes 65536 | tf_op jit(solution)/shard_map/all_to_all | solution.py:154
  42.1 0.1 bitcast_dynamic-update-slice_fusion.2
  42.1 9.4 %all-to-all-done = f32[8,4,256]{2,1,0:T(4,128)S(1)} async-done(((f32[8,4,256]{2,1,0:T(4,128)}), f32[8,4,256]{2,1,0:T(4,128)S(1)}, u32[]{:S(2)}, u32[]{:S(2)}) %all-to-all-start) | async-done | bytes 32800 | tf_op jit(solution)/shard_map/all_to_all | solution.py:154
  51.6 0.8 broadcast_in_dim.249
  52.4 8.0 %all-to-all-start.1 = ((f32[16,32,256]{2,1,0:T(8,128)}), f32[16,32,256]{2,1,0:T(8,128)S(1)}, u32[]{:S(2)}, u32[]{:S(2)}) async-start(f32[16,32,256]{2,1,0:T(8,128)} %broadcast_in_dim.249), calls=%async_computation.1 | async-start | bytes 1048576 | tf_op jit(solution)/shard_map/all_to_all | solution.py:101
  60.4 0.6 copy.18
  61.0 0.1 fusion.35
  61.1 0.0 copy-start.1
  61.1 8.2 %all-to-all-done.1 = f32[16,32,256]{2,1,0:T(8,128)S(1)} async-done(((f32[16,32,256]{2,1,0:T(8,128)}), f32[16,32,256]{2,1,0:T(8,128)S(1)}, u32[]{:S(2)}, u32[]{:S(2)}) %all-to-all-start.1) | async-done | bytes 524320 | tf_op jit(solution)/shard_map/all_to_all | solution.py:101
  69.3 0.0 copy-start
  69.3 0.8 copy-done
  70.1 3.5 %shard_map.94 = f32[16,128]{1,0:T(8,128)} custom-call(s32[128]{0:T(128)} %bitcast.109, f32[512,256]{1,0:T(8,128)} %bitcast.96, s32[128,16,128]{2,1,0:T(8,128)} %bitcast.97), custom_call_target="tpu_custom_call" | custom-call | flops 2097152 | bytes 1581056 | tf_op jit(solution)/shard_map/pallas_call | solution.py:82
  73.7 0.0 copy-done.1
  73.7 20.5 %all-gather = f32[4,1,2048]{2,1,0:T(1,128)S(1)} all-gather(f32[1,1,2048]{2,1,0:T(1,128)} %bitcast.102), channel_id=1, replica_groups=mesh['act'=4,'axial'=16,'hoop'=8] {'act'}, dimensions={0}, use_global_device_ids=true | all-gather | bytes 40960 | tf_op jit(solution)/shard_map/all_gather | solution.py:159
  94.2 0.6 fusion.41
  (13 shorter events, 0.1 us)
Async XLA Ops:
  0.6 0.8 copy-start.4
  1.5 1.0 %copy-start.2 = (f32[1,4,253]{2,1,0:T(4,128)S(1)}, f32[1,4,253]{2,1,0:T(4,128)}, u32[]{:S(2)}) copy-start(f32[1,4,253]{2,1,0:T(4,128)} %param.11) | copy-start | bytes 12148
  2.5 15.7 %copy-start.3 = (f32[8,6]{1,0:T(8,128)S(1)}, f32[8,6]{1,0:T(8,128)}, u32[]{:S(2)}) copy-start(f32[8,6]{1,0:T(8,128)} %param.9) | copy-start | bytes 580
  2.6 15.7 %collective-permute-start = (f32[6,16,6]{2,1,0:T(8,128)S(1)}, f32[6,16,6]{2,1,0:T(8,128)S(1)}, u32[]{:S(2)}, u32[]{:S(2)}) collective-permute-start(f32[6,16,6]{2,1,0:T(8,128)S(1)} %get-tuple-element.49), channel_id=1, source_target_pairs={{0,1},{1,2},{2,3},{3,4},{4,5},{5,6},{6,7},{7,0},{8,9},{9,10},{10,1... | collective-permute-start | bytes 6920 | tf_op jit(solution)/shard_map/ppermute | solution.py:17
  7.0 12.4 %collective-permute-start.1 = (f32[6,16,6]{2,1,0:T(8,128)S(1)}, f32[6,16,6]{2,1,0:T(8,128)S(1)}, u32[]{:S(2)}, u32[]{:S(2)}) collective-permute-start(f32[6,16,6]{2,1,0:T(8,128)S(1)} %get-tuple-element.50), channel_id=1, source_target_pairs={{1,0},{2,1},{3,2},{4,3},{5,4},{6,5},{7,6},{0,7},{9,8},{10,9},{11,1... | collective-permute-start | bytes 6920 | tf_op jit(solution)/shard_map/ppermute | solution.py:18
  19.6 5.1 %collective-permute-start.2 = (f32[6,6,524]{2,1,0:T(8,128)S(1)}, f32[6,6,524]{2,1,0:T(8,128)S(1)}, u32[]{:S(2)}, u32[]{:S(2)}) collective-permute-start(f32[6,6,524]{2,1,0:T(8,128)S(1)} %get-tuple-element.45), channel_id=1, source_target_pairs={{0,8},{8,16},{16,24},{24,32},{32,40},{40,48},{48,56},{56,64},{64,7... | collective-permute-start | bytes 226376 | tf_op jit(solution)/shard_map/ppermute | solution.py:20
  22.8 5.6 %collective-permute-start.3 = (f32[6,6,524]{2,1,0:T(8,128)S(1)}, f32[6,6,524]{2,1,0:T(8,128)S(1)}, u32[]{:S(2)}, u32[]{:S(2)}) collective-permute-start(f32[6,6,524]{2,1,0:T(8,128)S(1)} %get-tuple-element.46), channel_id=1, source_target_pairs={{8,0},{16,8},{24,16},{32,24},{40,32},{48,40},{56,48},{64,56},{72,6... | collective-permute-start | bytes 226376 | tf_op jit(solution)/shard_map/ppermute | solution.py:21
  32.4 19.1 %all-to-all-start = ((f32[8,4,256]{2,1,0:T(4,128)}), f32[8,4,256]{2,1,0:T(4,128)S(1)}, u32[]{:S(2)}, u32[]{:S(2)}) async-start(f32[8,4,256]{2,1,0:T(4,128)} %broadcast_select_fusion), calls=%async_computation | async-start | bytes 65536 | tf_op jit(solution)/shard_map/all_to_all | solution.py:154
  52.4 16.9 %all-to-all-start.1 = ((f32[16,32,256]{2,1,0:T(8,128)}), f32[16,32,256]{2,1,0:T(8,128)S(1)}, u32[]{:S(2)}, u32[]{:S(2)}) async-start(f32[16,32,256]{2,1,0:T(8,128)} %broadcast_in_dim.249), calls=%async_computation.1 | async-start | bytes 1048576 | tf_op jit(solution)/shard_map/all_to_all | solution.py:101
  61.1 12.6 %copy-start.1 = (f32[5,16,512]{2,1,0:T(8,128)}, f32[5,16,512]{2,1,0:T(8,128)S(1)}, u32[]{:S(2)}) copy-start(f32[5,16,512]{2,1,0:T(8,128)S(1)} %fusion.35) | copy-start | bytes 491524
  69.3 0.8 copy-start

commit v16 on v15

--- a/solution.py
+++ b/solution.py
@@ -73,7 +73,7 @@
             parts.append(jnp.where(d >= lanes, got_high, got_low))
         return acc + jnp.concatenate(parts, axis=0)
 
-    acc = lax.fori_loop(0, pairs, body, jnp.zeros((pix_rows, pix_cols), jnp.float32), unroll=32)
+    acc = lax.fori_loop(0, pairs, body, jnp.zeros((pix_rows, pix_cols), jnp.float32), unroll=64)
     out_ref[...] = acc
 
 

time: 95.3 us -> 95.2 us (level)
  no operation moved by 1% of the time
where the time goes in v16:
time: 95.2 us; the launch traced here: 94.7 us
  starting transfers between devices  37.7 us (40%)
  waiting for transfers between devices  23 us (24%)
  blocking collectives  20.5 us (22%)
  other arithmetic  6.25 us (7%)
  Pallas kernels  3.41 us (4%)
  local copies, waits for them, and re-layouts  2.78 us (3%)
    all_gather x1, blocking collectives, per_device(): lax.all_gather(partial_value.reshape(-1), 'act')  20.5 us
    ppermute x1, starting transfers between devices, exchange(): lax.ppermute(cells[:, :, :halo], 'hoop', [((j + 1) % nh, j) for j in rang...  11.3 us
    all_to_all x1, starting transfers between devices, per_device(): lax.all_to_all(spread, 'hoop', 0, 0, tiled=True)  9.64 us
    all_to_all x1, waiting for transfers between devices, per_device(): lax.all_to_all(spread, 'hoop', 0, 0, tiled=True)  9.41 us
    all_to_all x1, waiting for transfers between devices, a2a_gather(): gathered = lax.all_to_all(spread, axes, 0, 0, tiled=True)  8.22 us
    all_to_all x1, starting transfers between devices, a2a_gather(): gathered = lax.all_to_all(spread, axes, 0, 0, tiled=True)  7.96 us
    ppermute x1, starting transfers between devices, exchange(): lax.ppermute(cells[:, :, -halo:], 'hoop', [(j, (j + 1) % nh) for j in ran...  4.37 us
    ppermute x1, waiting for transfers between devices, exchange(): lax.ppermute(cells[:, :halo, :], 'axial', [(i + 1, i) for i in range(na -...  3.78 us
  transfers between devices with their start and end apart: 6, of which 5 were waited for; matrix products, arithmetic and copies ran while one was open for 1% of the time, Pallas kernels for 0%

profile of v16, /device:TPU:1, one launch (start us, length us, event | category | flops | bytes accessed | tf_op | source)
XLA Modules:
  0.0 94.7 jit_solution(7090367533396456148)
XLA Ops:
  0.6 0.0 copy-start.4
  0.6 0.8 convert_bitcast_fusion
  1.4 0.0 copy-done.4
  1.4 0.1 iota_compare_fusion
  1.5 0.0 copy-start.2
  1.5 0.9 pad_maximum_fusion.2
  2.5 0.0 copy-done.2
  2.5 0.0 copy-start.3
  2.5 0.1 fusion.46
  2.6 4.4 %collective-permute-start = (f32[6,16,6]{2,1,0:T(8,128)S(1)}, f32[6,16,6]{2,1,0:T(8,128)S(1)}, u32[]{:S(2)}, u32[]{:S(2)}) collective-permute-start(f32[6,16,6]{2,1,0:T(8,128)S(1)} %get-tuple-element.49), channel_id=1, source_target_pairs={{0,1},{1,2},{2,3},{3,4},{4,5},{5,6},{6,7},{7,0},{8,9},{9,10},{10,1... | collective-permute-start | bytes 6920 | tf_op jit(solution)/shard_map/ppermute | solution.py:17
  7.0 11.3 %collective-permute-start.1 = (f32[6,16,6]{2,1,0:T(8,128)S(1)}, f32[6,16,6]{2,1,0:T(8,128)S(1)}, u32[]{:S(2)}, u32[]{:S(2)}) collective-permute-start(f32[6,16,6]{2,1,0:T(8,128)S(1)} %get-tuple-element.50), channel_id=1, source_target_pairs={{1,0},{2,1},{3,2},{4,3},{5,4},{6,5},{7,6},{0,7},{9,8},{10,9},{11,1... | collective-permute-start | bytes 6920 | tf_op jit(solution)/shard_map/ppermute | solution.py:18
  18.2 0.0 copy-done.3
  18.3 0.0 collective-permute-done
  18.3 1.1 %collective-permute-done.1 = f32[6,16,6]{2,1,0:T(8,128)S(1)} collective-permute-done((f32[6,16,6]{2,1,0:T(8,128)S(1)}, f32[6,16,6]{2,1,0:T(8,128)S(1)}, u32[]{:S(2)}, u32[]{:S(2)}) %collective-permute-start.1) | collective-permute-done | bytes 2336 | tf_op jit(solution)/shard_map/ppermute | solution.py:18
  19.4 0.1 pad_maximum_fusion.1
  19.6 3.2 %collective-permute-start.2 = (f32[6,6,524]{2,1,0:T(8,128)S(1)}, f32[6,6,524]{2,1,0:T(8,128)S(1)}, u32[]{:S(2)}, u32[]{:S(2)}) collective-permute-start(f32[6,6,524]{2,1,0:T(8,128)S(1)} %get-tuple-element.45), channel_id=1, source_target_pairs={{0,8},{8,16},{16,24},{24,32},{32,40},{40,48},{48,56},{56,64},{64,7... | collective-permute-start | bytes 226376 | tf_op jit(solution)/shard_map/ppermute | solution.py:20
  22.8 1.3 %collective-permute-start.3 = (f32[6,6,524]{2,1,0:T(8,128)S(1)}, f32[6,6,524]{2,1,0:T(8,128)S(1)}, u32[]{:S(2)}, u32[]{:S(2)}) collective-permute-start(f32[6,6,524]{2,1,0:T(8,128)S(1)} %get-tuple-element.46), channel_id=1, source_target_pairs={{8,0},{16,8},{24,16},{32,24},{40,32},{48,40},{56,48},{64,56},{72,6... | collective-permute-start | bytes 226376 | tf_op jit(solution)/shard_map/ppermute | solution.py:21
  24.1 0.5 collective-permute-done.2
  24.6 3.8 %collective-permute-done.3 = f32[6,6,524]{2,1,0:T(8,128)S(1)} collective-permute-done((f32[6,6,524]{2,1,0:T(8,128)S(1)}, f32[6,6,524]{2,1,0:T(8,128)S(1)}, u32[]{:S(2)}, u32[]{:S(2)}) %collective-permute-start.3) | collective-permute-done | bytes 75488 | tf_op jit(solution)/shard_map/ppermute | solution.py:21
  28.4 0.2 pad_maximum_fusion
  28.6 0.1 compare_bitcast_fusion.7
  28.7 0.6 select_select_fusion
  29.3 0.1 slice_bitcast_fusion.6
  29.4 0.3 fusion.5
  29.7 0.2 fusion.27
  29.9 0.2 fusion.29
  30.1 0.1 fusion.30
  30.2 0.2 fusion.24
  30.4 0.2 fusion.9
  30.6 0.2 fusion.15
  30.8 0.2 fusion.8
  31.1 0.1 bitcast_dynamic-update-slice_fusion.3
  31.1 0.1 add_bitcast_fusion
  31.3 0.3 select_reduce_fusion.2
  31.6 0.1 copy.21
  31.7 0.1 pad.5.clone
  31.8 0.6 broadcast_select_fusion
  32.4 9.6 %all-to-all-start = ((f32[8,4,256]{2,1,0:T(4,128)}), f32[8,4,256]{2,1,0:T(4,128)S(1)}, u32[]{:S(2)}, u32[]{:S(2)}) async-start(f32[8,4,256]{2,1,0:T(4,128)} %broadcast_select_fusion), calls=%async_computation | async-start | bytes 65536 | tf_op jit(solution)/shard_map/all_to_all | solution.py:154
  42.1 0.1 bitcast_dynamic-update-slice_fusion.2
  42.1 9.4 %all-to-all-done = f32[8,4,256]{2,1,0:T(4,128)S(1)} async-done(((f32[8,4,256]{2,1,0:T(4,128)}), f32[8,4,256]{2,1,0:T(4,128)S(1)}, u32[]{:S(2)}, u32[]{:S(2)}) %all-to-all-start) | async-done | bytes 32800 | tf_op jit(solution)/shard_map/all_to_all | solution.py:154
  51.6 0.8 broadcast_in_dim.249
  52.4 8.0 %all-to-all-start.1 = ((f32[16,32,256]{2,1,0:T(8,128)}), f32[16,32,256]{2,1,0:T(8,128)S(1)}, u32[]{:S(2)}, u32[]{:S(2)}) async-start(f32[16,32,256]{2,1,0:T(8,128)} %broadcast_in_dim.249), calls=%async_computation.1 | async-start | bytes 1048576 | tf_op jit(solution)/shard_map/all_to_all | solution.py:101
  60.4 0.6 copy.18
  61.0 0.1 fusion.35
  61.1 0.0 copy-start.1
  61.1 8.2 %all-to-all-done.1 = f32[16,32,256]{2,1,0:T(8,128)S(1)} async-done(((f32[16,32,256]{2,1,0:T(8,128)}), f32[16,32,256]{2,1,0:T(8,128)S(1)}, u32[]{:S(2)}, u32[]{:S(2)}) %all-to-all-start.1) | async-done | bytes 524320 | tf_op jit(solution)/shard_map/all_to_all | solution.py:101
  69.3 0.0 copy-start
  69.3 0.8 copy-done
  70.1 3.4 %shard_map.94 = f32[16,128]{1,0:T(8,128)} custom-call(s32[128]{0:T(128)} %bitcast.109, f32[512,256]{1,0:T(8,128)} %bitcast.96, s32[128,16,128]{2,1,0:T(8,128)} %bitcast.97), custom_call_target="tpu_custom_call" | custom-call | flops 2097152 | bytes 1581056 | tf_op jit(solution)/shard_map/pallas_call | solution.py:82
  73.5 0.0 copy-done.1
  73.5 20.5 %all-gather = f32[4,1,2048]{2,1,0:T(1,128)S(1)} all-gather(f32[1,1,2048]{2,1,0:T(1,128)} %bitcast.102), channel_id=1, replica_groups=mesh['act'=4,'axial'=16,'hoop'=8] {'act'}, dimensions={0}, use_global_device_ids=true | all-gather | bytes 40960 | tf_op jit(solution)/shard_map/all_gather | solution.py:159
  94.1 0.6 fusion.41
  (13 shorter events, 0.1 us)
Async XLA Ops:
  0.6 0.8 copy-start.4
  1.5 1.0 %copy-start.2 = (f32[1,4,253]{2,1,0:T(4,128)S(1)}, f32[1,4,253]{2,1,0:T(4,128)}, u32[]{:S(2)}) copy-start(f32[1,4,253]{2,1,0:T(4,128)} %param.11) | copy-start | bytes 12148
  2.5 15.7 %copy-start.3 = (f32[8,6]{1,0:T(8,128)S(1)}, f32[8,6]{1,0:T(8,128)}, u32[]{:S(2)}) copy-start(f32[8,6]{1,0:T(8,128)} %param.9) | copy-start | bytes 580
  2.6 15.7 %collective-permute-start = (f32[6,16,6]{2,1,0:T(8,128)S(1)}, f32[6,16,6]{2,1,0:T(8,128)S(1)}, u32[]{:S(2)}, u32[]{:S(2)}) collective-permute-start(f32[6,16,6]{2,1,0:T(8,128)S(1)} %get-tuple-element.49), channel_id=1, source_target_pairs={{0,1},{1,2},{2,3},{3,4},{4,5},{5,6},{6,7},{7,0},{8,9},{9,10},{10,1... | collective-permute-start | bytes 6920 | tf_op jit(solution)/shard_map/ppermute | solution.py:17
  7.0 12.4 %collective-permute-start.1 = (f32[6,16,6]{2,1,0:T(8,128)S(1)}, f32[6,16,6]{2,1,0:T(8,128)S(1)}, u32[]{:S(2)}, u32[]{:S(2)}) collective-permute-start(f32[6,16,6]{2,1,0:T(8,128)S(1)} %get-tuple-element.50), channel_id=1, source_target_pairs={{1,0},{2,1},{3,2},{4,3},{5,4},{6,5},{7,6},{0,7},{9,8},{10,9},{11,1... | collective-permute-start | bytes 6920 | tf_op jit(solution)/shard_map/ppermute | solution.py:18
  19.6 5.1 %collective-permute-start.2 = (f32[6,6,524]{2,1,0:T(8,128)S(1)}, f32[6,6,524]{2,1,0:T(8,128)S(1)}, u32[]{:S(2)}, u32[]{:S(2)}) collective-permute-start(f32[6,6,524]{2,1,0:T(8,128)S(1)} %get-tuple-element.45), channel_id=1, source_target_pairs={{0,8},{8,16},{16,24},{24,32},{32,40},{40,48},{48,56},{56,64},{64,7... | collective-permute-start | bytes 226376 | tf_op jit(solution)/shard_map/ppermute | solution.py:20
  22.8 5.6 %collective-permute-start.3 = (f32[6,6,524]{2,1,0:T(8,128)S(1)}, f32[6,6,524]{2,1,0:T(8,128)S(1)}, u32[]{:S(2)}, u32[]{:S(2)}) collective-permute-start(f32[6,6,524]{2,1,0:T(8,128)S(1)} %get-tuple-element.46), channel_id=1, source_target_pairs={{8,0},{16,8},{24,16},{32,24},{40,32},{48,40},{56,48},{64,56},{72,6... | collective-permute-start | bytes 226376 | tf_op jit(solution)/shard_map/ppermute | solution.py:21
  32.4 19.1 %all-to-all-start = ((f32[8,4,256]{2,1,0:T(4,128)}), f32[8,4,256]{2,1,0:T(4,128)S(1)}, u32[]{:S(2)}, u32[]{:S(2)}) async-start(f32[8,4,256]{2,1,0:T(4,128)} %broadcast_select_fusion), calls=%async_computation | async-start | bytes 65536 | tf_op jit(solution)/shard_map/all_to_all | solution.py:154
  52.4 16.9 %all-to-all-start.1 = ((f32[16,32,256]{2,1,0:T(8,128)}), f32[16,32,256]{2,1,0:T(8,128)S(1)}, u32[]{:S(2)}, u32[]{:S(2)}) async-start(f32[16,32,256]{2,1,0:T(8,128)} %broadcast_in_dim.249), calls=%async_computation.1 | async-start | bytes 1048576 | tf_op jit(solution)/shard_map/all_to_all | solution.py:101
  61.1 12.4 %copy-start.1 = (f32[5,16,512]{2,1,0:T(8,128)}, f32[5,16,512]{2,1,0:T(8,128)S(1)}, u32[]{:S(2)}) copy-start(f32[5,16,512]{2,1,0:T(8,128)S(1)} %fusion.35) | copy-start | bytes 491524
  69.3 0.8 copy-start

commit v17 on v16

--- a/solution.py
+++ b/solution.py
@@ -73,7 +73,7 @@
             parts.append(jnp.where(d >= lanes, got_high, got_low))
         return acc + jnp.concatenate(parts, axis=0)
 
-    acc = lax.fori_loop(0, pairs, body, jnp.zeros((pix_rows, pix_cols), jnp.float32), unroll=64)
+    acc = lax.fori_loop(0, pairs, body, jnp.zeros((pix_rows, pix_cols), jnp.float32), unroll=True)
     out_ref[...] = acc
 
 

time: 95.2 us -> 95.1 us (level)
  no operation moved by 1% of the time
where the time goes in v17:
time: 95.1 us; the launch traced here: 94.6 us
  starting transfers between devices  37.7 us (40%)
  waiting for transfers between devices  23 us (24%)
  blocking collectives  20.5 us (22%)
  other arithmetic  6.25 us (7%)
  Pallas kernels  3.34 us (4%)
  local copies, waits for them, and re-layouts  2.78 us (3%)
    all_gather x1, blocking collectives, per_device(): lax.all_gather(partial_value.reshape(-1), 'act')  20.5 us
    ppermute x1, starting transfers between devices, exchange(): lax.ppermute(cells[:, :, :halo], 'hoop', [((j + 1) % nh, j) for j in rang...  11.3 us
    all_to_all x1, starting transfers between devices, per_device(): lax.all_to_all(spread, 'hoop', 0, 0, tiled=True)  9.64 us
    all_to_all x1, waiting for transfers between devices, per_device(): lax.all_to_all(spread, 'hoop', 0, 0, tiled=True)  9.41 us
    all_to_all x1, waiting for transfers between devices, a2a_gather(): gathered = lax.all_to_all(spread, axes, 0, 0, tiled=True)  8.22 us
    all_to_all x1, starting transfers between devices, a2a_gather(): gathered = lax.all_to_all(spread, axes, 0, 0, tiled=True)  7.96 us
    ppermute x1, starting transfers between devices, exchange(): lax.ppermute(cells[:, :, -halo:], 'hoop', [(j, (j + 1) % nh) for j in ran...  4.37 us
    ppermute x1, waiting for transfers between devices, exchange(): lax.ppermute(cells[:, :halo, :], 'axial', [(i + 1, i) for i in range(na -...  3.78 us
  transfers between devices with their start and end apart: 6, of which 5 were waited for; matrix products, arithmetic and copies ran while one was open for 1% of the time, Pallas kernels for 0%

profile of v17, /device:TPU:1, one launch (start us, length us, event | category | flops | bytes accessed | tf_op | source)
XLA Modules:
  0.0 94.6 jit_solution(15985291507603636405)
XLA Ops:
  0.6 0.0 copy-start.4
  0.6 0.8 convert_bitcast_fusion
  1.4 0.0 copy-done.4
  1.4 0.1 iota_compare_fusion
  1.5 0.0 copy-start.2
  1.5 0.9 pad_maximum_fusion.2
  2.5 0.0 copy-done.2
  2.5 0.0 copy-start.3
  2.5 0.1 fusion.46
  2.6 4.4 %collective-permute-start = (f32[6,16,6]{2,1,0:T(8,128)S(1)}, f32[6,16,6]{2,1,0:T(8,128)S(1)}, u32[]{:S(2)}, u32[]{:S(2)}) collective-permute-start(f32[6,16,6]{2,1,0:T(8,128)S(1)} %get-tuple-element.49), channel_id=1, source_target_pairs={{0,1},{1,2},{2,3},{3,4},{4,5},{5,6},{6,7},{7,0},{8,9},{9,10},{10,1... | collective-permute-start | bytes 6920 | tf_op jit(solution)/shard_map/ppermute | solution.py:17
  7.0 11.3 %collective-permute-start.1 = (f32[6,16,6]{2,1,0:T(8,128)S(1)}, f32[6,16,6]{2,1,0:T(8,128)S(1)}, u32[]{:S(2)}, u32[]{:S(2)}) collective-permute-start(f32[6,16,6]{2,1,0:T(8,128)S(1)} %get-tuple-element.50), channel_id=1, source_target_pairs={{1,0},{2,1},{3,2},{4,3},{5,4},{6,5},{7,6},{0,7},{9,8},{10,9},{11,1... | collective-permute-start | bytes 6920 | tf_op jit(solution)/shard_map/ppermute | solution.py:18
  18.2 0.0 copy-done.3
  18.3 0.0 collective-permute-done
  18.3 1.1 %collective-permute-done.1 = f32[6,16,6]{2,1,0:T(8,128)S(1)} collective-permute-done((f32[6,16,6]{2,1,0:T(8,128)S(1)}, f32[6,16,6]{2,1,0:T(8,128)S(1)}, u32[]{:S(2)}, u32[]{:S(2)}) %collective-permute-start.1) | collective-permute-done | bytes 2336 | tf_op jit(solution)/shard_map/ppermute | solution.py:18
  19.4 0.1 pad_maximum_fusion.1
  19.6 3.2 %collective-permute-start.2 = (f32[6,6,524]{2,1,0:T(8,128)S(1)}, f32[6,6,524]{2,1,0:T(8,128)S(1)}, u32[]{:S(2)}, u32[]{:S(2)}) collective-permute-start(f32[6,6,524]{2,1,0:T(8,128)S(1)} %get-tuple-element.45), channel_id=1, source_target_pairs={{0,8},{8,16},{16,24},{24,32},{32,40},{40,48},{48,56},{56,64},{64,7... | collective-permute-start | bytes 226376 | tf_op jit(solution)/shard_map/ppermute | solution.py:20
  22.8 1.3 %collective-permute-start.3 = (f32[6,6,524]{2,1,0:T(8,128)S(1)}, f32[6,6,524]{2,1,0:T(8,128)S(1)}, u32[]{:S(2)}, u32[]{:S(2)}) collective-permute-start(f32[6,6,524]{2,1,0:T(8,128)S(1)} %get-tuple-element.46), channel_id=1, source_target_pairs={{8,0},{16,8},{24,16},{32,24},{40,32},{48,40},{56,48},{64,56},{72,6... | collective-permute-start | bytes 226376 | tf_op jit(solution)/shard_map/ppermute | solution.py:21
  24.1 0.5 collective-permute-done.2
  24.6 3.8 %collective-permute-done.3 = f32[6,6,524]{2,1,0:T(8,128)S(1)} collective-permute-done((f32[6,6,524]{2,1,0:T(8,128)S(1)}, f32[6,6,524]{2,1,0:T(8,128)S(1)}, u32[]{:S(2)}, u32[]{:S(2)}) %collective-permute-start.3) | collective-permute-done | bytes 75488 | tf_op jit(solution)/shard_map/ppermute | solution.py:21
  28.4 0.2 pad_maximum_fusion
  28.6 0.1 compare_bitcast_fusion.7
  28.7 0.6 select_select_fusion
  29.3 0.1 slice_bitcast_fusion.6
  29.4 0.3 fusion.5
  29.7 0.2 fusion.27
  29.9 0.2 fusion.29
  30.1 0.1 fusion.30
  30.2 0.2 fusion.24
  30.4 0.2 fusion.9
  30.6 0.2 fusion.15
  30.8 0.2 fusion.8
  31.1 0.1 bitcast_dynamic-update-slice_fusion.3
  31.1 0.1 add_bitcast_fusion
  31.3 0.3 select_reduce_fusion.2
  31.6 0.1 copy.21
  31.7 0.1 pad.5.clone
  31.8 0.6 broadcast_select_fusion
  32.4 9.6 %all-to-all-start = ((f32[8,4,256]{2,1,0:T(4,128)}), f32[8,4,256]{2,1,0:T(4,128)S(1)}, u32[]{:S(2)}, u32[]{:S(2)}) async-start(f32[8,4,256]{2,1,0:T(4,128)} %broadcast_select_fusion), calls=%async_computation | async-start | bytes 65536 | tf_op jit(solution)/shard_map/all_to_all | solution.py:154
  42.1 0.1 bitcast_dynamic-update-slice_fusion.2
  42.1 9.4 %all-to-all-done = f32[8,4,256]{2,1,0:T(4,128)S(1)} async-done(((f32[8,4,256]{2,1,0:T(4,128)}), f32[8,4,256]{2,1,0:T(4,128)S(1)}, u32[]{:S(2)}, u32[]{:S(2)}) %all-to-all-start) | async-done | bytes 32800 | tf_op jit(solution)/shard_map/all_to_all | solution.py:154
  51.6 0.8 broadcast_in_dim.249
  52.4 8.0 %all-to-all-start.1 = ((f32[16,32,256]{2,1,0:T(8,128)}), f32[16,32,256]{2,1,0:T(8,128)S(1)}, u32[]{:S(2)}, u32[]{:S(2)}) async-start(f32[16,32,256]{2,1,0:T(8,128)} %broadcast_in_dim.249), calls=%async_computation.1 | async-start | bytes 1048576 | tf_op jit(solution)/shard_map/all_to_all | solution.py:101
  60.4 0.6 copy.18
  61.0 0.1 fusion.35
  61.1 0.0 copy-start.1
  61.1 8.2 %all-to-all-done.1 = f32[16,32,256]{2,1,0:T(8,128)S(1)} async-done(((f32[16,32,256]{2,1,0:T(8,128)}), f32[16,32,256]{2,1,0:T(8,128)S(1)}, u32[]{:S(2)}, u32[]{:S(2)}) %all-to-all-start.1) | async-done | bytes 524320 | tf_op jit(solution)/shard_map/all_to_all | solution.py:101
  69.3 0.0 copy-start
  69.3 0.8 copy-done
  70.1 3.3 %shard_map.94 = f32[16,128]{1,0:T(8,128)} custom-call(s32[128]{0:T(128)} %bitcast.109, f32[512,256]{1,0:T(8,128)} %bitcast.96, s32[128,16,128]{2,1,0:T(8,128)} %bitcast.97), custom_call_target="tpu_custom_call" | custom-call | flops 2097152 | bytes 1581056 | tf_op jit(solution)/shard_map/pallas_call | solution.py:82
  73.4 0.0 copy-done.1
  73.5 20.5 %all-gather = f32[4,1,2048]{2,1,0:T(1,128)S(1)} all-gather(f32[1,1,2048]{2,1,0:T(1,128)} %bitcast.102), channel_id=1, replica_groups=mesh['act'=4,'axial'=16,'hoop'=8] {'act'}, dimensions={0}, use_global_device_ids=true | all-gather | bytes 40960 | tf_op jit(solution)/shard_map/all_gather | solution.py:159
  94.0 0.6 fusion.41
  (13 shorter events, 0.1 us)
Async XLA Ops:
  0.6 0.8 copy-start.4
  1.5 1.0 %copy-start.2 = (f32[1,4,253]{2,1,0:T(4,128)S(1)}, f32[1,4,253]{2,1,0:T(4,128)}, u32[]{:S(2)}) copy-start(f32[1,4,253]{2,1,0:T(4,128)} %param.11) | copy-start | bytes 12148
  2.5 15.7 %copy-start.3 = (f32[8,6]{1,0:T(8,128)S(1)}, f32[8,6]{1,0:T(8,128)}, u32[]{:S(2)}) copy-start(f32[8,6]{1,0:T(8,128)} %param.9) | copy-start | bytes 580
  2.6 15.7 %collective-permute-start = (f32[6,16,6]{2,1,0:T(8,128)S(1)}, f32[6,16,6]{2,1,0:T(8,128)S(1)}, u32[]{:S(2)}, u32[]{:S(2)}) collective-permute-start(f32[6,16,6]{2,1,0:T(8,128)S(1)} %get-tuple-element.49), channel_id=1, source_target_pairs={{0,1},{1,2},{2,3},{3,4},{4,5},{5,6},{6,7},{7,0},{8,9},{9,10},{10,1... | collective-permute-start | bytes 6920 | tf_op jit(solution)/shard_map/ppermute | solution.py:17
  7.0 12.4 %collective-permute-start.1 = (f32[6,16,6]{2,1,0:T(8,128)S(1)}, f32[6,16,6]{2,1,0:T(8,128)S(1)}, u32[]{:S(2)}, u32[]{:S(2)}) collective-permute-start(f32[6,16,6]{2,1,0:T(8,128)S(1)} %get-tuple-element.50), channel_id=1, source_target_pairs={{1,0},{2,1},{3,2},{4,3},{5,4},{6,5},{7,6},{0,7},{9,8},{10,9},{11,1... | collective-permute-start | bytes 6920 | tf_op jit(solution)/shard_map/ppermute | solution.py:18
  19.6 5.1 %collective-permute-start.2 = (f32[6,6,524]{2,1,0:T(8,128)S(1)}, f32[6,6,524]{2,1,0:T(8,128)S(1)}, u32[]{:S(2)}, u32[]{:S(2)}) collective-permute-start(f32[6,6,524]{2,1,0:T(8,128)S(1)} %get-tuple-element.45), channel_id=1, source_target_pairs={{0,8},{8,16},{16,24},{24,32},{32,40},{40,48},{48,56},{56,64},{64,7... | collective-permute-start | bytes 226376 | tf_op jit(solution)/shard_map/ppermute | solution.py:20
  22.8 5.6 %collective-permute-start.3 = (f32[6,6,524]{2,1,0:T(8,128)S(1)}, f32[6,6,524]{2,1,0:T(8,128)S(1)}, u32[]{:S(2)}, u32[]{:S(2)}) collective-permute-start(f32[6,6,524]{2,1,0:T(8,128)S(1)} %get-tuple-element.46), channel_id=1, source_target_pairs={{8,0},{16,8},{24,16},{32,24},{40,32},{48,40},{56,48},{64,56},{72,6... | collective-permute-start | bytes 226376 | tf_op jit(solution)/shard_map/ppermute | solution.py:21
  32.4 19.1 %all-to-all-start = ((f32[8,4,256]{2,1,0:T(4,128)}), f32[8,4,256]{2,1,0:T(4,128)S(1)}, u32[]{:S(2)}, u32[]{:S(2)}) async-start(f32[8,4,256]{2,1,0:T(4,128)} %broadcast_select_fusion), calls=%async_computation | async-start | bytes 65536 | tf_op jit(solution)/shard_map/all_to_all | solution.py:154
  52.4 16.9 %all-to-all-start.1 = ((f32[16,32,256]{2,1,0:T(8,128)}), f32[16,32,256]{2,1,0:T(8,128)S(1)}, u32[]{:S(2)}, u32[]{:S(2)}) async-start(f32[16,32,256]{2,1,0:T(8,128)} %broadcast_in_dim.249), calls=%async_computation.1 | async-start | bytes 1048576 | tf_op jit(solution)/shard_map/all_to_all | solution.py:101
  61.1 12.4 %copy-start.1 = (f32[5,16,512]{2,1,0:T(8,128)}, f32[5,16,512]{2,1,0:T(8,128)S(1)}, u32[]{:S(2)}) copy-start(f32[5,16,512]{2,1,0:T(8,128)S(1)} %fusion.35) | copy-start | bytes 491524
  69.3 0.8 copy-start

commit v18 on v17

--- a/solution.py
+++ b/solution.py
@@ -73,8 +73,12 @@
             parts.append(jnp.where(d >= lanes, got_high, got_low))
         return acc + jnp.concatenate(parts, axis=0)
 
-    acc = lax.fori_loop(0, pairs, body, jnp.zeros((pix_rows, pix_cols), jnp.float32), unroll=True)
-    out_ref[...] = acc
+    def two(j, accs):
+        return body(2 * j, accs[0]), body(2 * j + 1, accs[1])
+
+    zero = jnp.zeros((pix_rows, pix_cols), jnp.float32)
+    even, odd = lax.fori_loop(0, pairs // 2, two, (zero, zero), unroll=True)
+    out_ref[...] = even + odd
 
 
 def image(receivers, waves, delays):

time: 95.1 us -> 95.1 us (level)
  no operation moved by 1% of the time
where the time goes in v18:
time: 95.1 us; the launch traced here: 94.6 us
  starting transfers between devices  37.7 us (40%)
  waiting for transfers between devices  23 us (24%)
  blocking collectives  20.5 us (22%)
  other arithmetic  6.25 us (7%)
  Pallas kernels  3.34 us (4%)
  local copies, waits for them, and re-layouts  2.78 us (3%)
    all_gather x1, blocking collectives, per_device(): lax.all_gather(partial_value.reshape(-1), 'act')  20.5 us
    ppermute x1, starting transfers between devices, exchange(): lax.ppermute(cells[:, :, :halo], 'hoop', [((j + 1) % nh, j) for j in rang...  11.3 us
    all_to_all x1, starting transfers between devices, per_device(): lax.all_to_all(spread, 'hoop', 0, 0, tiled=True)  9.64 us
    all_to_all x1, waiting for transfers between devices, per_device(): lax.all_to_all(spread, 'hoop', 0, 0, tiled=True)  9.41 us
    all_to_all x1, waiting for transfers between devices, a2a_gather(): gathered = lax.all_to_all(spread, axes, 0, 0, tiled=True)  8.22 us
    all_to_all x1, starting transfers between devices, a2a_gather(): gathered = lax.all_to_all(spread, axes, 0, 0, tiled=True)  7.96 us
    ppermute x1, starting transfers between devices, exchange(): lax.ppermute(cells[:, :, -halo:], 'hoop', [(j, (j + 1) % nh) for j in ran...  4.37 us
    ppermute x1, waiting for transfers between devices, exchange(): lax.ppermute(cells[:, :halo, :], 'axial', [(i + 1, i) for i in range(na -...  3.78 us
  transfers between devices with their start and end apart: 6, of which 5 were waited for; matrix products, arithmetic and copies ran while one was open for 1% of the time, Pallas kernels for 0%

profile of v18, /device:TPU:1, one launch (start us, length us, event | category | flops | bytes accessed | tf_op | source)
XLA Modules:
  0.0 94.6 jit_solution(11934758453434005826)
XLA Ops:
  0.6 0.0 copy-start.4
  0.6 0.8 convert_bitcast_fusion
  1.4 0.0 copy-done.4
  1.4 0.1 iota_compare_fusion
  1.5 0.0 copy-start.2
  1.5 0.9 pad_maximum_fusion.2
  2.5 0.0 copy-done.2
  2.5 0.0 copy-start.3
  2.5 0.1 fusion.46
  2.6 4.4 %collective-permute-start = (f32[6,16,6]{2,1,0:T(8,128)S(1)}, f32[6,16,6]{2,1,0:T(8,128)S(1)}, u32[]{:S(2)}, u32[]{:S(2)}) collective-permute-start(f32[6,16,6]{2,1,0:T(8,128)S(1)} %get-tuple-element.49), channel_id=1, source_target_pairs={{0,1},{1,2},{2,3},{3,4},{4,5},{5,6},{6,7},{7,0},{8,9},{9,10},{10,1... | collective-permute-start | bytes 6920 | tf_op jit(solution)/shard_map/ppermute | solution.py:17
  7.0 11.3 %collective-permute-start.1 = (f32[6,16,6]{2,1,0:T(8,128)S(1)}, f32[6,16,6]{2,1,0:T(8,128)S(1)}, u32[]{:S(2)}, u32[]{:S(2)}) collective-permute-start(f32[6,16,6]{2,1,0:T(8,128)S(1)} %get-tuple-element.50), channel_id=1, source_target_pairs={{1,0},{2,1},{3,2},{4,3},{5,4},{6,5},{7,6},{0,7},{9,8},{10,9},{11,1... | collective-permute-start | bytes 6920 | tf_op jit(solution)/shard_map/ppermute | solution.py:18
  18.2 0.0 copy-done.3
  18.3 0.0 collective-permute-done
  18.3 1.1 %collective-permute-done.1 = f32[6,16,6]{2,1,0:T(8,128)S(1)} collective-permute-done((f32[6,16,6]{2,1,0:T(8,128)S(1)}, f32[6,16,6]{2,1,0:T(8,128)S(1)}, u32[]{:S(2)}, u32[]{:S(2)}) %collective-permute-start.1) | collective-permute-done | bytes 2336 | tf_op jit(solution)/shard_map/ppermute | solution.py:18
  19.4 0.1 pad_maximum_fusion.1
  19.6 3.2 %collective-permute-start.2 = (f32[6,6,524]{2,1,0:T(8,128)S(1)}, f32[6,6,524]{2,1,0:T(8,128)S(1)}, u32[]{:S(2)}, u32[]{:S(2)}) collective-permute-start(f32[6,6,524]{2,1,0:T(8,128)S(1)} %get-tuple-element.45), channel_id=1, source_target_pairs={{0,8},{8,16},{16,24},{24,32},{32,40},{40,48},{48,56},{56,64},{64,7... | collective-permute-start | bytes 226376 | tf_op jit(solution)/shard_map/ppermute | solution.py:20
  22.8 1.3 %collective-permute-start.3 = (f32[6,6,524]{2,1,0:T(8,128)S(1)}, f32[6,6,524]{2,1,0:T(8,128)S(1)}, u32[]{:S(2)}, u32[]{:S(2)}) collective-permute-start(f32[6,6,524]{2,1,0:T(8,128)S(1)} %get-tuple-element.46), channel_id=1, source_target_pairs={{8,0},{16,8},{24,16},{32,24},{40,32},{48,40},{56,48},{64,56},{72,6... | collective-permute-start | bytes 226376 | tf_op jit(solution)/shard_map/ppermute | solution.py:21
  24.1 0.5 collective-permute-done.2
  24.6 3.8 %collective-permute-done.3 = f32[6,6,524]{2,1,0:T(8,128)S(1)} collective-permute-done((f32[6,6,524]{2,1,0:T(8,128)S(1)}, f32[6,6,524]{2,1,0:T(8,128)S(1)}, u32[]{:S(2)}, u32[]{:S(2)}) %collective-permute-start.3) | collective-permute-done | bytes 75488 | tf_op jit(solution)/shard_map/ppermute | solution.py:21
  28.4 0.2 pad_maximum_fusion
  28.6 0.1 compare_bitcast_fusion.7
  28.7 0.6 select_select_fusion
  29.3 0.1 slice_bitcast_fusion.6
  29.4 0.3 fusion.5
  29.7 0.2 fusion.27
  29.9 0.2 fusion.29
  30.1 0.1 fusion.30
  30.2 0.2 fusion.24
  30.4 0.2 fusion.9
  30.6 0.2 fusion.15
  30.8 0.2 fusion.8
  31.1 0.1 bitcast_dynamic-update-slice_fusion.3
  31.1 0.1 add_bitcast_fusion
  31.3 0.3 select_reduce_fusion.2
  31.6 0.1 copy.21
  31.7 0.1 pad.5.clone
  31.8 0.6 broadcast_select_fusion
  32.4 9.6 %all-to-all-start = ((f32[8,4,256]{2,1,0:T(4,128)}), f32[8,4,256]{2,1,0:T(4,128)S(1)}, u32[]{:S(2)}, u32[]{:S(2)}) async-start(f32[8,4,256]{2,1,0:T(4,128)} %broadcast_select_fusion), calls=%async_computation | async-start | bytes 65536 | tf_op jit(solution)/shard_map/all_to_all | solution.py:158
  42.1 0.1 bitcast_dynamic-update-slice_fusion.2
  42.1 9.4 %all-to-all-done = f32[8,4,256]{2,1,0:T(4,128)S(1)} async-done(((f32[8,4,256]{2,1,0:T(4,128)}), f32[8,4,256]{2,1,0:T(4,128)S(1)}, u32[]{:S(2)}, u32[]{:S(2)}) %all-to-all-start) | async-done | bytes 32800 | tf_op jit(solution)/shard_map/all_to_all | solution.py:158
  51.6 0.8 broadcast_in_dim.249
  52.4 8.0 %all-to-all-start.1 = ((f32[16,32,256]{2,1,0:T(8,128)}), f32[16,32,256]{2,1,0:T(8,128)S(1)}, u32[]{:S(2)}, u32[]{:S(2)}) async-start(f32[16,32,256]{2,1,0:T(8,128)} %broadcast_in_dim.249), calls=%async_computation.1 | async-start | bytes 1048576 | tf_op jit(solution)/shard_map/all_to_all | solution.py:105
  60.4 0.6 copy.18
  61.0 0.1 fusion.35
  61.1 0.0 copy-start.1
  61.1 8.2 %all-to-all-done.1 = f32[16,32,256]{2,1,0:T(8,128)S(1)} async-done(((f32[16,32,256]{2,1,0:T(8,128)}), f32[16,32,256]{2,1,0:T(8,128)S(1)}, u32[]{:S(2)}, u32[]{:S(2)}) %all-to-all-start.1) | async-done | bytes 524320 | tf_op jit(solution)/shard_map/all_to_all | solution.py:105
  69.3 0.0 copy-start
  69.3 0.8 copy-done
  70.1 3.3 %shard_map.94 = f32[16,128]{1,0:T(8,128)} custom-call(s32[128]{0:T(128)} %bitcast.109, f32[512,256]{1,0:T(8,128)} %bitcast.96, s32[128,16,128]{2,1,0:T(8,128)} %bitcast.97), custom_call_target="tpu_custom_call" | custom-call | flops 2097152 | bytes 1581056 | tf_op jit(solution)/shard_map/pallas_call | solution.py:86
  73.5 0.0 copy-done.1
  73.5 20.5 %all-gather = f32[4,1,2048]{2,1,0:T(1,128)S(1)} all-gather(f32[1,1,2048]{2,1,0:T(1,128)} %bitcast.102), channel_id=1, replica_groups=mesh['act'=4,'axial'=16,'hoop'=8] {'act'}, dimensions={0}, use_global_device_ids=true | all-gather | bytes 40960 | tf_op jit(solution)/shard_map/all_gather | solution.py:163
  94.0 0.6 fusion.41
  (13 shorter events, 0.1 us)
Async XLA Ops:
  0.6 0.8 copy-start.4
  1.5 1.0 %copy-start.2 = (f32[1,4,253]{2,1,0:T(4,128)S(1)}, f32[1,4,253]{2,1,0:T(4,128)}, u32[]{:S(2)}) copy-start(f32[1,4,253]{2,1,0:T(4,128)} %param.11) | copy-start | bytes 12148
  2.5 15.7 %copy-start.3 = (f32[8,6]{1,0:T(8,128)S(1)}, f32[8,6]{1,0:T(8,128)}, u32[]{:S(2)}) copy-start(f32[8,6]{1,0:T(8,128)} %param.9) | copy-start | bytes 580
  2.6 15.7 %collective-permute-start = (f32[6,16,6]{2,1,0:T(8,128)S(1)}, f32[6,16,6]{2,1,0:T(8,128)S(1)}, u32[]{:S(2)}, u32[]{:S(2)}) collective-permute-start(f32[6,16,6]{2,1,0:T(8,128)S(1)} %get-tuple-element.49), channel_id=1, source_target_pairs={{0,1},{1,2},{2,3},{3,4},{4,5},{5,6},{6,7},{7,0},{8,9},{9,10},{10,1... | collective-permute-start | bytes 6920 | tf_op jit(solution)/shard_map/ppermute | solution.py:17
  7.0 12.4 %collective-permute-start.1 = (f32[6,16,6]{2,1,0:T(8,128)S(1)}, f32[6,16,6]{2,1,0:T(8,128)S(1)}, u32[]{:S(2)}, u32[]{:S(2)}) collective-permute-start(f32[6,16,6]{2,1,0:T(8,128)S(1)} %get-tuple-element.50), channel_id=1, source_target_pairs={{1,0},{2,1},{3,2},{4,3},{5,4},{6,5},{7,6},{0,7},{9,8},{10,9},{11,1... | collective-permute-start | bytes 6920 | tf_op jit(solution)/shard_map/ppermute | solution.py:18
  19.6 5.1 %collective-permute-start.2 = (f32[6,6,524]{2,1,0:T(8,128)S(1)}, f32[6,6,524]{2,1,0:T(8,128)S(1)}, u32[]{:S(2)}, u32[]{:S(2)}) collective-permute-start(f32[6,6,524]{2,1,0:T(8,128)S(1)} %get-tuple-element.45), channel_id=1, source_target_pairs={{0,8},{8,16},{16,24},{24,32},{32,40},{40,48},{48,56},{56,64},{64,7... | collective-permute-start | bytes 226376 | tf_op jit(solution)/shard_map/ppermute | solution.py:20
  22.8 5.6 %collective-permute-start.3 = (f32[6,6,524]{2,1,0:T(8,128)S(1)}, f32[6,6,524]{2,1,0:T(8,128)S(1)}, u32[]{:S(2)}, u32[]{:S(2)}) collective-permute-start(f32[6,6,524]{2,1,0:T(8,128)S(1)} %get-tuple-element.46), channel_id=1, source_target_pairs={{8,0},{16,8},{24,16},{32,24},{40,32},{48,40},{56,48},{64,56},{72,6... | collective-permute-start | bytes 226376 | tf_op jit(solution)/shard_map/ppermute | solution.py:21
  32.4 19.1 %all-to-all-start = ((f32[8,4,256]{2,1,0:T(4,128)}), f32[8,4,256]{2,1,0:T(4,128)S(1)}, u32[]{:S(2)}, u32[]{:S(2)}) async-start(f32[8,4,256]{2,1,0:T(4,128)} %broadcast_select_fusion), calls=%async_computation | async-start | bytes 65536 | tf_op jit(solution)/shard_map/all_to_all | solution.py:158
  52.4 16.9 %all-to-all-start.1 = ((f32[16,32,256]{2,1,0:T(8,128)}), f32[16,32,256]{2,1,0:T(8,128)S(1)}, u32[]{:S(2)}, u32[]{:S(2)}) async-start(f32[16,32,256]{2,1,0:T(8,128)} %broadcast_in_dim.249), calls=%async_computation.1 | async-start | bytes 1048576 | tf_op jit(solution)/shard_map/all_to_all | solution.py:105
  61.1 12.4 %copy-start.1 = (f32[5,16,512]{2,1,0:T(8,128)}, f32[5,16,512]{2,1,0:T(8,128)S(1)}, u32[]{:S(2)}) copy-start(f32[5,16,512]{2,1,0:T(8,128)S(1)} %fusion.35) | copy-start | bytes 491524
  69.3 0.8 copy-start
